TPU v7x, 512 devices: a whole 4x8x8 slice. The times are simulated.
512 devices in a mesh: section: 32 (over x, z), expert: 16 (over y, core).
Axes of the slice: x: 4, y: 8, z: 8, core: 2. Of those that a mesh axis runs over, the one named last changes fastest.
Arguments:
- tokens: bfloat16 [32, 3072, 1024], P('section', 'expert'), may hold values from -6 to 6
- out_grad: bfloat16 [32, 3072, 1024], P('section', 'expert'), may hold values from -6 to 6
- expert_ids: int32 [32, 3072, 2], P('section', 'expert'), may hold values from 0 to 15, all different within a row; in each aligned block of 192 rows (0 to 191, 192 to 383, ..., all dimensions but the last counted through in order) at most 48 rows name the same one
- gate_weights: float32 [32, 3072, 2], P('section', 'expert'), may hold values from 0.2 to 1
- w_gate: bfloat16 [32, 16, 1024, 256], P('section', 'expert'), may hold values from -0.1875 to 0.1875
- w_up: bfloat16 [32, 16, 1024, 256], P('section', 'expert'), may hold values from -0.1875 to 0.1875
- w_down: bfloat16 [32, 16, 256, 1024], P('section', 'expert'), may hold values from -0.25 to 0.25
Outputs:
- token_grad: bfloat16 [32, 3072, 1024], P('section', 'expert')
- grad_gate: bfloat16 [32, 16, 1024, 256], P('section', 'expert')
- grad_up: bfloat16 [32, 16, 1024, 256], P('section', 'expert')
- grad_down: bfloat16 [32, 16, 256, 1024], P('section', 'expert')
Inputs may be any that keep to these rules, and one draw needn't show every extreme that they name: `expert_ids`: each token names 2 different experts. Among the 192 tokens of one device (aligned blocks of rows of one section) no expert is named by more than 48 (token, choice) pairs, a bound that some block reaches.
All inputs are finite; a program needn't handle non-finite values.
Results may differ from a plain program's by a relative error of at most 0.009.
Values may be sent and summed in bfloat16 or wider, within the bound.
No kernel may reach another device: no remote copies, remote signals or barrier semaphores. Data moves between devices by JAX's collectives and lax.ppermute only.
A program may use at most 64 MiB of HBM per device.

v0:
```python
import math

import jax
import jax.numpy as jnp
from jax import lax
from jax.sharding import PartitionSpec as P


def partner(value, axis, bit):
    mask = 2**bit
    pairs = [(source, source ^ mask) for source in range(lax.axis_size(axis))]
    return lax.ppermute(value, axis, pairs)


def make_slots(ids, gates, inputs, grads, cap, experts):
    tok, topk = ids.shape
    width = inputs.shape[1]
    count = tok * topk
    flat = ids.reshape(count)
    onehot = (flat[:, None] == jnp.arange(experts, dtype=jnp.int32)[None, :]).astype(jnp.int32)
    before = jnp.cumsum(onehot, axis=0) - onehot
    rank = jnp.sum(before * onehot, axis=1)
    slot = flat * cap + rank
    source = (
        jnp.full((experts * cap,), count, jnp.int32)
        .at[slot]
        .set(jnp.arange(count, dtype=jnp.int32))
    )
    token = source // topk
    padded_in = jnp.concatenate([inputs, jnp.zeros((1, width), inputs.dtype)], axis=0)
    scaled = (gates[:, :, None] * grads.astype(jnp.float32)[:, None, :]).astype(jnp.bfloat16)
    padded_grad = jnp.concatenate(
        [scaled.reshape(count, width), jnp.zeros((1, width), jnp.bfloat16)], axis=0
    )
    slot_in = padded_in[token].reshape(experts, cap, width)
    slot_grad = padded_grad[source].reshape(experts, cap, width)
    live = (source < count).reshape(experts, cap)
    return (slot_in, slot_grad, live, slot)


def unslot(slot_rows, slot, tok, topk):
    width = slot_rows.shape[-1]
    picked = slot_rows[slot].astype(jnp.float32).reshape(tok, topk, width)
    return jnp.sum(picked, axis=1).astype(jnp.bfloat16)


def expert_grads(rows_in, rows_grad, gate_w, up_w, down_w):
    contract_last = (((1,), (1,)), ((), ()))
    contract_rows = (((0,), (0,)), ((), ()))
    gate_pre = jnp.dot(rows_in, gate_w, preferred_element_type=jnp.float32)
    up_pre = jnp.dot(rows_in, up_w, preferred_element_type=jnp.float32)
    sigmoid_g = jax.nn.sigmoid(gate_pre)
    swish_val = gate_pre * sigmoid_g
    act = (swish_val * up_pre).astype(jnp.bfloat16)
    act_grad = lax.dot_general(rows_grad, down_w, contract_last, preferred_element_type=jnp.float32)
    gate_grad = (act_grad * up_pre * sigmoid_g * (1.0 + gate_pre * (1.0 - sigmoid_g))).astype(
        jnp.bfloat16
    )
    up_grad = (act_grad * swish_val).astype(jnp.bfloat16)
    pair_grad = lax.dot_general(
        gate_grad, gate_w, contract_last, preferred_element_type=jnp.float32
    )
    pair_grad = pair_grad + lax.dot_general(
        up_grad, up_w, contract_last, preferred_element_type=jnp.float32
    )
    grad_g = lax.dot_general(rows_in, gate_grad, contract_rows, preferred_element_type=jnp.float32)
    grad_u = lax.dot_general(rows_in, up_grad, contract_rows, preferred_element_type=jnp.float32)
    grad_d = lax.dot_general(act, rows_grad, contract_rows, preferred_element_type=jnp.float32)
    return (pair_grad, grad_g, grad_u, grad_d)


def run_expert(rows_in, rows_grad, gate_w, up_w, down_w):
    return expert_grads(rows_in, rows_grad, gate_w, up_w, down_w)


def per_device(tokens, out_grad, expert_ids, gate_weights, w_gate, w_up, w_down):
    inputs = tokens[0]
    grads = out_grad[0]
    ids = expert_ids[0]
    gates = gate_weights[0]
    tok, topk = ids.shape
    width = inputs.shape[1]
    experts = lax.axis_size("expert")
    cap = 2 * topk * tok // experts
    scale = 1.0 / math.sqrt(2 * topk * tok)
    pair_bit = lax.axis_size("section").bit_length() - 2
    slot_in, slot_grad, live, slot = make_slots(ids, gates, inputs, grads, cap, experts)
    recv_in, recv_grad, recv_live = (
        lax.all_to_all(slot_in, "expert", split_axis=0, concat_axis=0, tiled=True),
        lax.all_to_all(slot_grad, "expert", split_axis=0, concat_axis=0, tiled=True),
        lax.all_to_all(
            live.astype(jnp.bfloat16), "expert", split_axis=0, concat_axis=0, tiled=True
        ),
    )
    rows = experts * cap
    recv_in = recv_in.reshape(rows, width)
    recv_grad = recv_grad.reshape(rows, width)
    recv_live = recv_live.reshape(rows)
    own_gate = w_gate[0, 0]
    own_up = w_up[0, 0]
    own_down = w_down[0, 0]
    half = own_gate.shape[1]
    other_gate, other_up, other_down = partner((own_gate, own_up, own_down), "section", pair_bit)
    full_gate = jnp.concatenate([own_gate, other_gate], axis=1)
    full_up = jnp.concatenate([own_up, other_up], axis=1)
    full_down = jnp.concatenate([own_down, other_down], axis=0)
    pair_grad, grad_g, grad_u, grad_d = run_expert(
        recv_in, recv_grad, full_gate, full_up, full_down
    )
    peer_g, peer_u, peer_d = (
        partner(grad_g[:, half:].astype(jnp.bfloat16), "section", pair_bit).astype(jnp.float32),
        partner(grad_u[:, half:].astype(jnp.bfloat16), "section", pair_bit).astype(jnp.float32),
        partner(grad_d[half:, :].astype(jnp.bfloat16), "section", pair_bit).astype(jnp.float32),
    )
    mine_g = grad_g[:, :half] + peer_g
    mine_u = grad_u[:, :half] + peer_u
    mine_d = grad_d[:half, :] + peer_d
    back_slots = pair_grad.astype(jnp.bfloat16).reshape(experts, cap, width)
    home_slots = lax.all_to_all(back_slots, "expert", split_axis=0, concat_axis=0, tiled=True)
    token_grad = unslot(home_slots.reshape(rows, width), slot, tok, topk)
    out_g = (mine_g * scale).astype(jnp.bfloat16)
    out_u = (mine_u * scale).astype(jnp.bfloat16)
    out_d = (mine_d * scale).astype(jnp.bfloat16)
    return (token_grad[None], out_g[None, None], out_u[None, None], out_d[None, None])


def solution(mesh):
    in_specs = (
        P("section", "expert", None),
        P("section", "expert", None),
        P("section", "expert", None),
        P("section", "expert", None),
        P("section", "expert", None, None),
        P("section", "expert", None, None),
        P("section", "expert", None, None),
    )
    out_specs = (
        P("section", "expert", None),
        P("section", "expert", None, None),
        P("section", "expert", None, None),
        P("section", "expert", None, None),
    )
    return jax.shard_map(
        per_device, mesh=mesh, in_specs=in_specs, out_specs=out_specs, check_vma=False
    )
```

profile of v0, /device:TPU:1, one launch (start us, length us, event | category | flops | bytes accessed | tf_op | source)
XLA Modules:
  0.0 168.6 jit_solution(17971966431553553128)
XLA Ops:
  0.6 0.8 copy.13
  1.4 0.1 eq.29
  1.6 0.1 eq.25
  1.7 0.7 broadcast_multiply_fusion
  2.4 0.9 reduce-window.6
  3.3 0.2 slice_reduce_fusion
  3.5 0.1 copy.12
  3.7 0.1 mul.77
  3.8 0.1 fusion.21
  3.9 2.9 %scatter_custom_fusion = s32[768]{0:T(1024)S(1)} fusion(s32[384]{0:T(512)S(1)} %fusion.27, s32[384]{0:T(512)S(1)} %iota.11, s32[]{:T(128)} %constant.13.clone.1), kind=kCustom, calls=%fused_computation.59 | custom fusion | bytes 3076 | tf_op jit(solution)/shard_map/scatter | solution.py:27
  6.9 1.0 concatenate.17
  7.9 3.6 %gather_fusion.1 = bf16[768,1024]{1,0:T(8,128)(2,1)} fusion(bf16[193,1024]{1,0:T(8,128)(2,1)S(1)} %concatenate.17, s32[1024]{0:T(1024)S(1)} %get-tuple-element.8), kind=kCustom, calls=%fused_computation.1 | custom fusion | bytes 3148800 | tf_op jit(solution)/shard_map/gather | solution.py:35
  11.5 11.1 %all-to-all-start.1 = ((bf16[16,48,1024]{2,1,0:T(8,128)(2,1)}), bf16[16,48,1024]{2,1,0:T(8,128)(2,1)}, u32[]{:S(2)}, u32[]{:S(2)}) async-start(bf16[16,48,1024]{2,1,0:T(8,128)(2,1)} %bitcast.6), calls=%async_computation.1 | async-start | bytes 3145728 | tf_op jit(solution)/shard_map/all_to_all | solution.py:89
  22.6 0.0 copy-done.8
  22.6 0.1 bitcast_convert_fusion
  22.7 0.5 mul.72
  23.2 0.0 copy-start.9
  23.2 1.1 mul.73
  24.3 0.0 copy-done.9
  24.3 0.1 copy.11
  24.5 0.1 mul.70
  24.6 0.2 multiply_convert_fusion.3
  24.8 0.1 concatenate.15
  24.8 3.6 %gather_fusion = bf16[768,1024]{1,0:T(8,128)(2,1)} fusion(bf16[385,1024]{1,0:T(8,128)(2,1)S(1)} %concatenate.15, s32[1024]{0:T(1024)S(1)} %get-tuple-element.9), kind=kCustom, calls=%fused_computation | custom fusion | bytes 3148800 | tf_op jit(solution)/shard_map/gather | solution.py:36
  28.4 32.9 %all-to-all-done.1 = bf16[16,48,1024]{2,1,0:T(8,128)(2,1)} async-done(((bf16[16,48,1024]{2,1,0:T(8,128)(2,1)}), bf16[16,48,1024]{2,1,0:T(8,128)(2,1)}, u32[]{:S(2)}, u32[]{:S(2)}) %all-to-all-start.1) | async-done | bytes 1572896 | tf_op jit(solution)/shard_map/all_to_all | solution.py:89
  61.3 4.3 %all-to-all-start = ((bf16[16,48,1024]{2,1,0:T(8,128)(2,1)}), bf16[16,48,1024]{2,1,0:T(8,128)(2,1)S(1)}, u32[]{:S(2)}, u32[]{:S(2)}) async-start(bf16[16,48,1024]{2,1,0:T(8,128)(2,1)} %bitcast.2), calls=%async_computation | async-start | bytes 3145728 | tf_op jit(solution)/shard_map/all_to_all | solution.py:90
  65.5 0.0 copy-done.5
  65.6 2.2 %collective-permute-start.2 = (bf16[1024,256]{1,0:T(8,128)(2,1)S(1)}, bf16[1024,256]{1,0:T(8,128)(2,1)S(1)}, u32[]{:S(2)}, u32[]{:S(2)}) collective-permute-start(bf16[1024,256]{1,0:T(8,128)(2,1)S(1)} %bitcast.56), channel_id=1, source_target_pairs={{0,256},{16,272},{32,288},{48,304},{64,320},{80,336},{96,352},{112... | collective-permute-start | bytes 1572872 | tf_op jit(solution)/shard_map/ppermute | solution.py:12
  67.8 0.0 copy-done.4
  67.8 4.6 %collective-permute-start.1 = (bf16[1024,256]{1,0:T(8,128)(2,1)S(1)}, bf16[1024,256]{1,0:T(8,128)(2,1)S(1)}, u32[]{:S(2)}, u32[]{:S(2)}) collective-permute-start(bf16[1024,256]{1,0:T(8,128)(2,1)S(1)} %bitcast.53), channel_id=1, source_target_pairs={{0,256},{16,272},{32,288},{48,304},{64,320},{80,336},{96,352},{112... | collective-permute-start | bytes 1572872 | tf_op jit(solution)/shard_map/ppermute | solution.py:12
  72.4 2.2 %collective-permute-start = (bf16[256,1024]{1,0:T(8,128)(2,1)}, bf16[256,1024]{1,0:T(8,128)(2,1)}, u32[]{:S(2)}, u32[]{:S(2)}) collective-permute-start(bf16[256,1024]{1,0:T(8,128)(2,1)} %bitcast.62), channel_id=1, source_target_pairs={{0,256},{16,272},{32,288},{48,304},{64,320},{80,336},{96,352},{112... | collective-permute-start | bytes 1572872 | tf_op jit(solution)/shard_map/ppermute | solution.py:12
  74.6 7.7 %collective-permute-done.2 = bf16[1024,256]{1,0:T(8,128)(2,1)S(1)} collective-permute-done((bf16[1024,256]{1,0:T(8,128)(2,1)S(1)}, bf16[1024,256]{1,0:T(8,128)(2,1)S(1)}, u32[]{:S(2)}, u32[]{:S(2)}) %collective-permute-start.2) | collective-permute-done | bytes 524320 | tf_op jit(solution)/shard_map/ppermute | solution.py:12
  82.3 3.5 %fusion.12 = f32[768,512]{1,0:T(8,128)} fusion(bf16[768,1024]{1,0:T(8,128)(2,1)} %bitcast.7, bf16[1024,256]{1,0:T(8,128)(2,1)S(1)} %collective-permute-done.2, bf16[1024,256]{1,0:T(8,128)(2,1)S(1)} %bitcast.57), kind=kOutput, calls=%fused_computation.30 | convolution fusion | flops 807403520 | bytes 4194304 | tf_op jit(solution)/shard_map/dot_general | solution.py:50
  85.9 7.7 %collective-permute-done.1 = bf16[1024,256]{1,0:T(8,128)(2,1)S(1)} collective-permute-done((bf16[1024,256]{1,0:T(8,128)(2,1)S(1)}, bf16[1024,256]{1,0:T(8,128)(2,1)S(1)}, u32[]{:S(2)}, u32[]{:S(2)}) %collective-permute-start.1) | collective-permute-done | bytes 524320 | tf_op jit(solution)/shard_map/ppermute | solution.py:12
  93.6 3.7 %fusion.14 = f32[768,512]{1,0:T(8,128)} fusion(bf16[768,1024]{1,0:T(8,128)(2,1)} %bitcast.7, bf16[1024,256]{1,0:T(8,128)(2,1)S(1)} %collective-permute-done.1, bf16[1024,256]{1,0:T(8,128)(2,1)S(1)} %bitcast.54), kind=kOutput, calls=%fused_computation.32 | convolution fusion | flops 807403520 | bytes 4194304 | tf_op jit(solution)/shard_map/dot_general | solution.py:51
  97.3 0.0 copy-done.6
  97.3 7.6 %collective-permute-done = bf16[256,1024]{1,0:T(8,128)(2,1)} collective-permute-done((bf16[256,1024]{1,0:T(8,128)(2,1)}, bf16[256,1024]{1,0:T(8,128)(2,1)}, u32[]{:S(2)}, u32[]{:S(2)}) %collective-permute-start) | collective-permute-done | bytes 524320 | tf_op jit(solution)/shard_map/ppermute | solution.py:12
  104.9 0.0 all-to-all-done
  104.9 3.7 %multiply_convert_fusion.2 = (bf16[768,512]{1,0:T(8,128)(2,1)S(1)}, bf16[768,512]{1,0:T(8,128)(2,1)S(1)}) fusion(f32[768,512]{1,0:T(8,128)} %fusion.12, f32[768,512]{1,0:T(8,128)} %fusion.14, bf16[768,1024]{1,0:T(8,128)(2,1)S(1)} %bitcast.51, bf16[256,1024]{1,0:T(8,128)(2,1)} %collective-permute-done, bf16[256,1024]{1,0:T(8,128)(2,1)} %bitcast.63), kind=kOutput, calls=%fused_computation.7 | convolution fusion | flops 812515328 | bytes 7340032 | tf_op jit(solution)/shard_map/dot_general | solution.py:55
  108.7 0.0 copy-start
  108.7 1.0 fusion.13
  109.7 0.0 copy-done
  109.7 0.1 copy-done.2
  109.8 2.2 %add_convert_fusion = bf16[768,1024]{1,0:T(8,128)(2,1)} fusion(f32[768,1024]{1,0:T(8,128)S(1)} %fusion.13, bf16[768,512]{1,0:T(8,128)(2,1)S(1)} %get-tuple-element.4, bf16[1024,256]{1,0:T(8,128)(2,1)S(1)} %collective-permute-done.2, bf16[1024,256]{1,0:T(8,128)(2,1)S(1)} %bitcast.58), kind=kOutput, calls=%fused_computation.4 | convolution fusion | flops 808976384 | bytes 6553600 | tf_op jit(solution)/shard_map/dot_general | solution.py:60
  112.0 7.8 %all-to-all-start.2 = ((bf16[16,48,1024]{2,1,0:T(8,128)(2,1)}), bf16[16,48,1024]{2,1,0:T(8,128)(2,1)S(1)}, u32[]{:S(2)}, u32[]{:S(2)}) async-start(bf16[16,48,1024]{2,1,0:T(8,128)(2,1)} %bitcast.10), calls=%async_computation.2 | async-start | bytes 3145728 | tf_op jit(solution)/shard_map/all_to_all | solution.py:119
  119.8 3.1 %fusion.11 = f32[512,1024]{1,0:T(8,128)S(1)} fusion(bf16[768,1024]{1,0:T(8,128)(2,1)S(1)} %bitcast.52, f32[768,512]{1,0:T(8,128)} %fusion.14, f32[768,512]{1,0:T(8,128)} %fusion.12), kind=kOutput, calls=%fused_computation.29 | convolution fusion | flops 807665664 | bytes 6815744 | tf_op jit(solution)/shard_map/dot_general | solution.py:68
  122.9 0.1 slice.73
  123.0 2.4 %collective-permute-start.5 = (bf16[256,1024]{1,0:T(8,128)(2,1)S(1)}, bf16[256,1024]{1,0:T(8,128)(2,1)S(1)}, u32[]{:S(2)}, u32[]{:S(2)}) collective-permute-start(bf16[256,1024]{1,0:T(8,128)(2,1)S(1)} %slice.73), channel_id=1, source_target_pairs={{0,256},{16,272},{32,288},{48,304},{64,320},{80,336},{96,352},{112... | collective-permute-start | bytes 1572872 | tf_op jit(solution)/shard_map/ppermute | solution.py:12
  125.3 2.4 %fusion.35 = f32[1024,512]{1,0:T(8,128)S(1)} fusion(bf16[768,1024]{1,0:T(8,128)(2,1)} %bitcast.7, bf16[768,512]{1,0:T(8,128)(2,1)S(1)} %copy-done.1), kind=kOutput, calls=%fused_computation.70 | convolution fusion | flops 805306368 | bytes 4456448 | tf_op jit(solution)/shard_map/dot_general | solution.py:67
  127.8 0.1 slice.74
  127.9 4.6 %collective-permute-start.4 = (bf16[1024,256]{1,0:T(8,128)(2,1)S(1)}, bf16[1024,256]{1,0:T(8,128)(2,1)S(1)}, u32[]{:S(2)}, u32[]{:S(2)}) collective-permute-start(bf16[1024,256]{1,0:T(8,128)(2,1)S(1)} %slice.74), channel_id=1, source_target_pairs={{0,256},{16,272},{32,288},{48,304},{64,320},{80,336},{96,352},{112... | collective-permute-start | bytes 1572872 | tf_op jit(solution)/shard_map/ppermute | solution.py:12
  132.4 2.4 %fusion.34 = f32[1024,512]{1,0:T(8,128)S(1)} fusion(bf16[768,1024]{1,0:T(8,128)(2,1)} %bitcast.7, bf16[768,512]{1,0:T(8,128)(2,1)S(1)} %copy-done.3), kind=kOutput, calls=%fused_computation.69 | convolution fusion | flops 805306368 | bytes 4456448 | tf_op jit(solution)/shard_map/dot_general | solution.py:66
  134.8 0.1 slice.75
  134.9 2.2 %collective-permute-start.3 = (bf16[1024,256]{1,0:T(8,128)(2,1)S(1)}, bf16[1024,256]{1,0:T(8,128)(2,1)S(1)}, u32[]{:S(2)}, u32[]{:S(2)}) collective-permute-start(bf16[1024,256]{1,0:T(8,128)(2,1)S(1)} %slice.75), channel_id=1, source_target_pairs={{0,256},{16,272},{32,288},{48,304},{64,320},{80,336},{96,352},{112... | collective-permute-start | bytes 1572872 | tf_op jit(solution)/shard_map/ppermute | solution.py:12
  137.2 2.7 %collective-permute-done.5 = bf16[256,1024]{1,0:T(8,128)(2,1)S(1)} collective-permute-done((bf16[256,1024]{1,0:T(8,128)(2,1)S(1)}, bf16[256,1024]{1,0:T(8,128)(2,1)S(1)}, u32[]{:S(2)}, u32[]{:S(2)}) %collective-permute-start.5) | collective-permute-done | bytes 524320 | tf_op jit(solution)/shard_map/ppermute | solution.py:12
  139.9 1.0 fusion.17
  140.8 10.3 %collective-permute-done.4 = bf16[1024,256]{1,0:T(8,128)(2,1)S(1)} collective-permute-done((bf16[1024,256]{1,0:T(8,128)(2,1)S(1)}, bf16[1024,256]{1,0:T(8,128)(2,1)S(1)}, u32[]{:S(2)}, u32[]{:S(2)}) %collective-permute-start.4) | collective-permute-done | bytes 524320 | tf_op jit(solution)/shard_map/ppermute | solution.py:12
  151.1 1.0 fusion.16
  152.1 10.2 %collective-permute-done.3 = bf16[1024,256]{1,0:T(8,128)(2,1)S(1)} collective-permute-done((bf16[1024,256]{1,0:T(8,128)(2,1)S(1)}, bf16[1024,256]{1,0:T(8,128)(2,1)S(1)}, u32[]{:S(2)}, u32[]{:S(2)}) %collective-permute-start.3) | collective-permute-done | bytes 524320 | tf_op jit(solution)/shard_map/ppermute | solution.py:12
  162.3 1.0 fusion.15
  163.3 0.0 all-to-all-done.2
  163.3 2.1 %gather_fusion.2 = bf16[384,1024]{1,0:T(8,128)(2,1)S(1)} fusion(bf16[768,1024]{1,0:T(8,128)(2,1)S(1)} %bitcast.50, s32[1024]{0:T(1024)S(1)} %pad_clamp_fusion), kind=kCustom, calls=%fused_computation.2 | custom fusion | bytes 1574400 | tf_op jit(solution)/shard_map/gather | solution.py:43
  165.4 0.3 convert_element_type.82
  165.7 2.9 %reduce = bf16[192,1024]{1,0:T(8,128)(2,1)} reduce(bf16[192,2,1024]{2,1,0:T(2,128)(2,1)S(1)} %convert_element_type.82, bf16[]{:T(256)} %constant.12.clone.1), dimensions={1}, to_apply=%region_4.5.clone | reduce | flops 196608 | bytes 1179650 | tf_op jit(solution)/shard_map/reduce_sum | solution.py:44
  (18 shorter events, 0.1 us)
Async XLA Ops:
  11.5 11.1 %copy-start.8 = (bf16[1,192,1024]{2,1,0:T(8,128)(2,1)S(1)}, bf16[1,192,1024]{2,1,0:T(8,128)(2,1)}, u32[]{:S(2)}) copy-start(bf16[1,192,1024]{2,1,0:T(8,128)(2,1)} %param.8) | copy-start | bytes 1179652
  11.5 49.8 %all-to-all-start.1 = ((bf16[16,48,1024]{2,1,0:T(8,128)(2,1)}), bf16[16,48,1024]{2,1,0:T(8,128)(2,1)}, u32[]{:S(2)}, u32[]{:S(2)}) async-start(bf16[16,48,1024]{2,1,0:T(8,128)(2,1)} %bitcast.6), calls=%async_computation.1 | async-start | bytes 3145728 | tf_op jit(solution)/shard_map/all_to_all | solution.py:89
  23.2 1.1 copy-start.9
  61.3 4.3 %copy-start.5 = (bf16[1,1,1024,256]{3,2,1,0:T(8,128)(2,1)S(1)}, bf16[1,1,1024,256]{3,2,1,0:T(8,128)(2,1)}, u32[]{:S(2)}) copy-start(bf16[1,1,1024,256]{3,2,1,0:T(8,128)(2,1)} %param.11) | copy-start | bytes 1572868
  61.3 6.5 %copy-start.4 = (bf16[1,1,1024,256]{3,2,1,0:T(8,128)(2,1)S(1)}, bf16[1,1,1024,256]{3,2,1,0:T(8,128)(2,1)}, u32[]{:S(2)}) copy-start(bf16[1,1,1024,256]{3,2,1,0:T(8,128)(2,1)} %param.12) | copy-start | bytes 1572868
  61.3 43.6 %all-to-all-start = ((bf16[16,48,1024]{2,1,0:T(8,128)(2,1)}), bf16[16,48,1024]{2,1,0:T(8,128)(2,1)S(1)}, u32[]{:S(2)}, u32[]{:S(2)}) async-start(bf16[16,48,1024]{2,1,0:T(8,128)(2,1)} %bitcast.2), calls=%async_computation | async-start | bytes 3145728 | tf_op jit(solution)/shard_map/all_to_all | solution.py:90
  65.6 16.8 %collective-permute-start.2 = (bf16[1024,256]{1,0:T(8,128)(2,1)S(1)}, bf16[1024,256]{1,0:T(8,128)(2,1)S(1)}, u32[]{:S(2)}, u32[]{:S(2)}) collective-permute-start(bf16[1024,256]{1,0:T(8,128)(2,1)S(1)} %bitcast.56), channel_id=1, source_target_pairs={{0,256},{16,272},{32,288},{48,304},{64,320},{80,336},{96,352},{112... | collective-permute-start | bytes 1572872 | tf_op jit(solution)/shard_map/ppermute | solution.py:12
  67.8 25.8 %collective-permute-start.1 = (bf16[1024,256]{1,0:T(8,128)(2,1)S(1)}, bf16[1024,256]{1,0:T(8,128)(2,1)S(1)}, u32[]{:S(2)}, u32[]{:S(2)}) collective-permute-start(bf16[1024,256]{1,0:T(8,128)(2,1)S(1)} %bitcast.53), channel_id=1, source_target_pairs={{0,256},{16,272},{32,288},{48,304},{64,320},{80,336},{96,352},{112... | collective-permute-start | bytes 1572872 | tf_op jit(solution)/shard_map/ppermute | solution.py:12
  72.4 32.5 %collective-permute-start = (bf16[256,1024]{1,0:T(8,128)(2,1)}, bf16[256,1024]{1,0:T(8,128)(2,1)}, u32[]{:S(2)}, u32[]{:S(2)}) collective-permute-start(bf16[256,1024]{1,0:T(8,128)(2,1)} %bitcast.62), channel_id=1, source_target_pairs={{0,256},{16,272},{32,288},{48,304},{64,320},{80,336},{96,352},{112... | collective-permute-start | bytes 1572872 | tf_op jit(solution)/shard_map/ppermute | solution.py:12
  93.6 3.7 %copy-start.6 = (bf16[1024,256]{1,0:T(8,128)(2,1)}, bf16[1024,256]{1,0:T(8,128)(2,1)S(1)}, u32[]{:S(2)}) copy-start(bf16[1024,256]{1,0:T(8,128)(2,1)S(1)} %collective-permute-done.1) | copy-start | bytes 1572868
  104.9 3.8 %copy-start.7 = (bf16[1024,256]{1,0:T(8,128)(2,1)S(1)}, bf16[1024,256]{1,0:T(8,128)(2,1)}, u32[]{:S(2)}) copy-start(bf16[1024,256]{1,0:T(8,128)(2,1)} %copy-done.6) | copy-start | bytes 1572868
  108.7 1.0 copy-start
  108.7 1.1 copy-start.2
  112.0 51.4 %all-to-all-start.2 = ((bf16[16,48,1024]{2,1,0:T(8,128)(2,1)}), bf16[16,48,1024]{2,1,0:T(8,128)(2,1)S(1)}, u32[]{:S(2)}, u32[]{:S(2)}) async-start(bf16[16,48,1024]{2,1,0:T(8,128)(2,1)} %bitcast.10), calls=%async_computation.2 | async-start | bytes 3145728 | tf_op jit(solution)/shard_map/all_to_all | solution.py:119
  119.8 5.6 %copy-start.1 = (bf16[768,512]{1,0:T(8,128)(2,1)S(1)}, bf16[768,512]{1,0:T(8,128)(2,1)}, u32[]{:S(2)}) copy-start(bf16[768,512]{1,0:T(8,128)(2,1)} %copy-done) | copy-start | bytes 2359300
  123.0 9.5 %copy-start.3 = (bf16[768,512]{1,0:T(8,128)(2,1)S(1)}, bf16[768,512]{1,0:T(8,128)(2,1)}, u32[]{:S(2)}) copy-start(bf16[768,512]{1,0:T(8,128)(2,1)} %copy-done.2) | copy-start | bytes 2359300
  123.0 16.9 %collective-permute-start.5 = (bf16[256,1024]{1,0:T(8,128)(2,1)S(1)}, bf16[256,1024]{1,0:T(8,128)(2,1)S(1)}, u32[]{:S(2)}, u32[]{:S(2)}) collective-permute-start(bf16[256,1024]{1,0:T(8,128)(2,1)S(1)} %slice.73), channel_id=1, source_target_pairs={{0,256},{16,272},{32,288},{48,304},{64,320},{80,336},{96,352},{112... | collective-permute-start | bytes 1572872 | tf_op jit(solution)/shard_map/ppermute | solution.py:12
  127.9 23.2 %collective-permute-start.4 = (bf16[1024,256]{1,0:T(8,128)(2,1)S(1)}, bf16[1024,256]{1,0:T(8,128)(2,1)S(1)}, u32[]{:S(2)}, u32[]{:S(2)}) collective-permute-start(bf16[1024,256]{1,0:T(8,128)(2,1)S(1)} %slice.74), channel_id=1, source_target_pairs={{0,256},{16,272},{32,288},{48,304},{64,320},{80,336},{96,352},{112... | collective-permute-start | bytes 1572872 | tf_op jit(solution)/shard_map/ppermute | solution.py:12
  134.9 27.4 %collective-permute-start.3 = (bf16[1024,256]{1,0:T(8,128)(2,1)S(1)}, bf16[1024,256]{1,0:T(8,128)(2,1)S(1)}, u32[]{:S(2)}, u32[]{:S(2)}) collective-permute-start(bf16[1024,256]{1,0:T(8,128)(2,1)S(1)} %slice.75), channel_id=1, source_target_pairs={{0,256},{16,272},{32,288},{48,304},{64,320},{80,336},{96,352},{112... | collective-permute-start | bytes 1572872 | tf_op jit(solution)/shard_map/ppermute | solution.py:12
where the time goes:
time: 169 us
  waiting for transfers between devices  79.1 us (47%)
  starting transfers between devices  41.3 us (24%)
  matrix products  22.1 us (13%)
  local copies, waits for them, and re-layouts  17.2 us (10%)
  other arithmetic  7.83 us (5%)
    ppermute x6, waiting for transfers between devices, partner(): return lax.ppermute(value, axis, pairs)  46.2 us
    all_to_all x1, waiting for transfers between devices, per_device(): lax.all_to_all(slot_in, 'expert', split_axis=0, concat_axis=0, tiled=True)  32.9 us
    ppermute x6, starting transfers between devices, partner(): return lax.ppermute(value, axis, pairs)  18.2 us
    all_to_all x1, starting transfers between devices, per_device(): lax.all_to_all(slot_in, 'expert', split_axis=0, concat_axis=0, tiled=True)  11.1 us
    all_to_all x1, starting transfers between devices, per_device(): lax.all_to_all(back_slots, 'expert', split_axis=0, concat_axis=0, tiled=T...  7.79 us
    all_to_all x1, starting transfers between devices, per_device(): lax.all_to_all(slot_grad, 'expert', split_axis=0, concat_axis=0, tiled=True)  4.27 us
    dot_general x1, matrix products, expert_grads(): up_pre = jnp.dot(rows_in, up_w, preferred_element_type=jnp.float32)  3.74 us
    dot_general x1, matrix products, expert_grads(): lax.dot_general(rows_grad, down_w, contract_last, preferred_element_type=...  3.73 us
  transfers between devices with their start and end apart: 9, of which 7 were waited for; matrix products, arithmetic and copies ran while one was open for 14% of the time, Pallas kernels for 0%

commit v1 on v0

v1 whole, which is shorter than its diff:
```python
import math

import jax
import jax.numpy as jnp
from jax import lax
from jax.sharding import PartitionSpec as P

CHUNKS = 2


def partner(value, axis, bit):
    mask = 2**bit
    pairs = [(source, source ^ mask) for source in range(lax.axis_size(axis))]
    return lax.ppermute(value, axis, pairs)


def dispatch_matrix(ids, cap, experts):
    tok, topk = ids.shape
    count = tok * topk
    flat = ids.reshape(count)
    onehot = (flat[:, None] == jnp.arange(experts, dtype=jnp.int32)[None, :]).astype(jnp.int32)
    before = jnp.cumsum(onehot, axis=0) - onehot
    rank = jnp.sum(before * onehot, axis=1)
    slot = flat * cap + rank
    hit = slot[None, :] == jnp.arange(experts * cap, dtype=jnp.int32)[:, None]
    return hit


def expert_grads(rows_in, rows_grad, gate_w, up_w, down_w):
    contract_last = (((1,), (1,)), ((), ()))
    contract_rows = (((0,), (0,)), ((), ()))
    gate_pre = jnp.dot(rows_in, gate_w, preferred_element_type=jnp.float32)
    up_pre = jnp.dot(rows_in, up_w, preferred_element_type=jnp.float32)
    sigmoid_g = jax.nn.sigmoid(gate_pre)
    swish_val = gate_pre * sigmoid_g
    act = (swish_val * up_pre).astype(jnp.bfloat16)
    act_grad = lax.dot_general(rows_grad, down_w, contract_last, preferred_element_type=jnp.float32)
    gate_grad = (act_grad * up_pre * sigmoid_g * (1.0 + gate_pre * (1.0 - sigmoid_g))).astype(
        jnp.bfloat16
    )
    up_grad = (act_grad * swish_val).astype(jnp.bfloat16)
    pair_grad = lax.dot_general(
        gate_grad, gate_w, contract_last, preferred_element_type=jnp.float32
    )
    pair_grad = pair_grad + lax.dot_general(
        up_grad, up_w, contract_last, preferred_element_type=jnp.float32
    )
    grad_g = lax.dot_general(rows_in, gate_grad, contract_rows, preferred_element_type=jnp.float32)
    grad_u = lax.dot_general(rows_in, up_grad, contract_rows, preferred_element_type=jnp.float32)
    grad_d = lax.dot_general(act, rows_grad, contract_rows, preferred_element_type=jnp.float32)
    return (pair_grad, grad_g, grad_u, grad_d)


def per_device(tokens, out_grad, expert_ids, gate_weights, w_gate, w_up, w_down):
    inputs = tokens[0]
    grads = out_grad[0]
    ids = expert_ids[0]
    gates = gate_weights[0]
    tok, topk = ids.shape
    width = inputs.shape[1]
    experts = lax.axis_size("expert")
    cap = 2 * topk * tok // experts
    scale = 1.0 / math.sqrt(2 * topk * tok)
    pair_bit = lax.axis_size("section").bit_length() - 2

    own_gate = w_gate[0, 0]
    own_up = w_up[0, 0]
    own_down = w_down[0, 0]
    half = own_gate.shape[1]
    other_gate, other_up, other_down = partner((own_gate, own_up, own_down), "section", pair_bit)

    hit = dispatch_matrix(ids, cap, experts)
    pair_gate = jnp.sum(jnp.where(hit, gates.reshape(tok * topk)[None, :], 0.0), axis=1)
    token_hit = hit.reshape(experts * cap, tok, topk).any(axis=2).astype(jnp.bfloat16)
    both = jnp.concatenate([inputs, grads], axis=1)

    token_hit = token_hit.reshape(experts, cap, tok)
    pair_gate = pair_gate.reshape(experts, cap)
    step = cap // CHUNKS
    chunk_rows = experts * step

    full_gate = full_up = full_down = None
    token_acc = jnp.zeros((tok, width), jnp.float32)
    acc_g = acc_u = acc_d = None
    for c in range(CHUNKS):
        sel = token_hit[:, c * step:(c + 1) * step, :].reshape(chunk_rows, tok)
        sgate = pair_gate[:, c * step:(c + 1) * step].reshape(chunk_rows, 1)
        picked = jnp.dot(sel, both, preferred_element_type=jnp.float32)
        slot_in = picked[:, :width].astype(jnp.bfloat16)
        slot_grad = (picked[:, width:] * sgate).astype(jnp.bfloat16)
        send = jnp.concatenate([slot_in, slot_grad], axis=1).reshape(experts, step, 2 * width)
        recv = lax.all_to_all(send, "expert", split_axis=0, concat_axis=0, tiled=True)
        recv = recv.reshape(chunk_rows, 2 * width)
        if full_gate is None:
            full_gate = jnp.concatenate([own_gate, other_gate], axis=1)
            full_up = jnp.concatenate([own_up, other_up], axis=1)
            full_down = jnp.concatenate([own_down, other_down], axis=0)
        pair_grad, grad_g, grad_u, grad_d = expert_grads(
            recv[:, :width], recv[:, width:], full_gate, full_up, full_down
        )
        if acc_g is None:
            acc_g, acc_u, acc_d = grad_g, grad_u, grad_d
        else:
            acc_g, acc_u, acc_d = acc_g + grad_g, acc_u + grad_u, acc_d + grad_d
        back = pair_grad.astype(jnp.bfloat16).reshape(experts, step, width)
        home = lax.all_to_all(back, "expert", split_axis=0, concat_axis=0, tiled=True)
        home = home.reshape(chunk_rows, width)
        token_acc = token_acc + lax.dot_general(
            sel, home, (((0,), (0,)), ((), ())), preferred_element_type=jnp.float32
        )

    peer_g, peer_u, peer_d = partner(
        (
            acc_g[:, half:].astype(jnp.bfloat16),
            acc_u[:, half:].astype(jnp.bfloat16),
            acc_d[half:, :].astype(jnp.bfloat16),
        ),
        "section",
        pair_bit,
    )
    mine_g = acc_g[:, :half] + peer_g.astype(jnp.float32)
    mine_u = acc_u[:, :half] + peer_u.astype(jnp.float32)
    mine_d = acc_d[:half, :] + peer_d.astype(jnp.float32)
    token_grad = token_acc.astype(jnp.bfloat16)
    out_g = (mine_g * scale).astype(jnp.bfloat16)
    out_u = (mine_u * scale).astype(jnp.bfloat16)
    out_d = (mine_d * scale).astype(jnp.bfloat16)
    return (token_grad[None], out_g[None, None], out_u[None, None], out_d[None, None])


def solution(mesh):
    in_specs = (
        P("section", "expert", None),
        P("section", "expert", None),
        P("section", "expert", None),
        P("section", "expert", None),
        P("section", "expert", None, None),
        P("section", "expert", None, None),
        P("section", "expert", None, None),
    )
    out_specs = (
        P("section", "expert", None),
        P("section", "expert", None, None),
        P("section", "expert", None, None),
        P("section", "expert", None, None),
    )
    return jax.shard_map(
        per_device, mesh=mesh, in_specs=in_specs, out_specs=out_specs, check_vma=False
    )
```

time: 169 us -> 180 us (1.065)
  waiting for transfers between devices: 79.1 us -> 90.9 us
  local copies, waits for them, and re-layouts: 17.2 us -> 10.5 us
  matrix products: 22.1 us -> 25.6 us
    all_to_all x3 -> x4, waiting for transfers between devices: 32.9 us -> 57.2 us  [the longest x2 42.8 us: per_device(): lax.all_to_all(send, 'expert', split_axis=0, concat_axis=0, tiled=True)]
    ppermute x6, waiting for transfers between devices: 46.2 us -> 33.7 us  [partner(): return lax.ppermute(value, axis, pairs)]
    gather x3 -> x0, local copies, waits for them, and re-layouts: 9.18 us -> none  [the longest x1 3.56 us: make_slots(): slot_in = padded_in[token].reshape(experts, cap, width)]
    unnamed x22 -> x54, local copies, waits for them, and re-layouts: 1.02 us -> 7.66 us
    dot_general x0 -> x4, matrix products: none -> 4.98 us  [the longest x2 3.85 us: per_device(): lax.dot_general(sel, home, (((0,), (0,)), ((), ())), preferred_element_ty...]
    scatter x1 -> x0, local copies, waits for them, and re-layouts: 2.92 us -> none  [make_slots(): source = jnp.full((experts * cap,), count, jnp.int32).at[slot].set(jnp.ar...]
    reduce_sum x2, other arithmetic: 3.02 us -> 0.3 us  [the longest x1 0.2 us: per_device(): jnp.sum(jnp.where(hit, gates.reshape(tok * topk)[None, :], 0.0), axis=1)]
    dot_general x1 -> x2, matrix products: 3.74 us -> 1.14 us  [expert_grads(): up_pre = jnp.dot(rows_in, up_w, preferred_element_type=jnp.float32)]
  transfers between devices with their start and end apart: 9 -> 10, of which waited for: 7 -> 7; matrix products, arithmetic and copies ran while one was open for 14% -> 16% of each run, Pallas kernels for 0% -> 0%
where the time goes in v1:
time: 180 us; the launch traced here: 179 us
  waiting for transfers between devices  90.9 us (50%)
  starting transfers between devices  42.8 us (24%)
  matrix products  25.6 us (14%)
  local copies, waits for them, and re-layouts  10.5 us (6%)
  other arithmetic  8.17 us (5%)
    all_to_all x2, waiting for transfers between devices, per_device(): lax.all_to_all(send, 'expert', split_axis=0, concat_axis=0, tiled=True)  42.8 us
    ppermute x6, waiting for transfers between devices, partner(): return lax.ppermute(value, axis, pairs)  33.7 us
    ppermute x6, starting transfers between devices, partner(): return lax.ppermute(value, axis, pairs)  19.6 us
    all_to_all x2, waiting for transfers between devices, per_device(): lax.all_to_all(back, 'expert', split_axis=0, concat_axis=0, tiled=True)  14.5 us
    all_to_all x2, starting transfers between devices, per_device(): lax.all_to_all(send, 'expert', split_axis=0, concat_axis=0, tiled=True)  14.5 us
    all_to_all x2, starting transfers between devices, per_device(): lax.all_to_all(back, 'expert', split_axis=0, concat_axis=0, tiled=True)  8.78 us
    unnamed x54, local copies, waits for them, and re-layouts  7.66 us
    dot_general x2, matrix products, expert_grads(): lax.dot_general(rows_grad, down_w, contract_last, preferred_element_type=...  4.45 us
  transfers between devices with their start and end apart: 10, of which 7 were waited for; matrix products, arithmetic and copies ran while one was open for 16% of the time, Pallas kernels for 0%

profile of v1, /device:TPU:1, one launch (start us, length us, event | category | flops | bytes accessed | tf_op | source)
XLA Modules:
  0.0 179.2 jit_solution(18194289336439117934)
XLA Ops:
  0.7 0.9 copy.17
  1.5 0.1 eq.49
  1.8 0.9 reduce-window.6
  2.7 0.2 slice_reduce_fusion
  3.0 0.1 reduce_sum.21
  3.3 0.2 fusion.5
  3.5 0.4 copy.22
  3.9 0.8 copy.23
  4.9 0.2 select_reduce_fusion
  5.3 0.6 fusion.25
  6.0 0.1 fusion.1
  6.2 1.3 pad_maximum_fusion
  7.5 10.3 %all-to-all-start = ((bf16[16,24,2048]{2,1,0:T(8,128)(2,1)}), bf16[16,24,2048]{2,1,0:T(8,128)(2,1)S(1)}, u32[]{:S(2)}, u32[]{:S(2)}) async-start(bf16[16,24,2048]{2,1,0:T(8,128)(2,1)} %bitcast.6), calls=%async_computation | async-start | bytes 3145728 | tf_op jit(solution)/shard_map/all_to_all | solution.py:92
  17.9 0.6 fusion.24
  18.6 0.1 fusion
  18.8 1.2 pad_maximum_fusion.1
  20.0 36.4 %all-to-all-done = bf16[16,24,2048]{2,1,0:T(8,128)(2,1)S(1)} async-done(((bf16[16,24,2048]{2,1,0:T(8,128)(2,1)}), bf16[16,24,2048]{2,1,0:T(8,128)(2,1)S(1)}, u32[]{:S(2)}, u32[]{:S(2)}) %all-to-all-start) | async-done | bytes 1572896 | tf_op jit(solution)/shard_map/all_to_all | solution.py:92
  56.4 4.1 %all-to-all-start.2 = ((bf16[16,24,2048]{2,1,0:T(8,128)(2,1)}), bf16[16,24,2048]{2,1,0:T(8,128)(2,1)S(1)}, u32[]{:S(2)}, u32[]{:S(2)}) async-start(bf16[16,24,2048]{2,1,0:T(8,128)(2,1)} %bitcast.14), calls=%async_computation.2 | async-start | bytes 3145728 | tf_op jit(solution)/shard_map/all_to_all | solution.py:92
  60.5 3.0 %collective-permute-start.2 = (bf16[1024,256]{1,0:T(8,128)(2,1)}, bf16[1024,256]{1,0:T(8,128)(2,1)S(1)}, u32[]{:S(2)}, u32[]{:S(2)}) collective-permute-start(bf16[1024,256]{1,0:T(8,128)(2,1)} %bitcast.85), channel_id=1, source_target_pairs={{0,256},{16,272},{32,288},{48,304},{64,320},{80,336},{96,352},{112... | collective-permute-start | bytes 1572872 | tf_op jit(solution)/shard_map/ppermute | solution.py:14
  63.6 3.9 %collective-permute-start.1 = (bf16[1024,256]{1,0:T(8,128)(2,1)}, bf16[1024,256]{1,0:T(8,128)(2,1)S(1)}, u32[]{:S(2)}, u32[]{:S(2)}) collective-permute-start(bf16[1024,256]{1,0:T(8,128)(2,1)} %bitcast.80), channel_id=1, source_target_pairs={{0,256},{16,272},{32,288},{48,304},{64,320},{80,336},{96,352},{112... | collective-permute-start | bytes 1572872 | tf_op jit(solution)/shard_map/ppermute | solution.py:14
  67.5 2.9 %collective-permute-start = (bf16[256,1024]{1,0:T(8,128)(2,1)}, bf16[256,1024]{1,0:T(8,128)(2,1)}, u32[]{:S(2)}, u32[]{:S(2)}) collective-permute-start(bf16[256,1024]{1,0:T(8,128)(2,1)} %bitcast.100), channel_id=1, source_target_pairs={{0,256},{16,272},{32,288},{48,304},{64,320},{80,336},{96,352},{112... | collective-permute-start | bytes 1572872 | tf_op jit(solution)/shard_map/ppermute | solution.py:14
  70.4 7.3 %collective-permute-done.2 = bf16[1024,256]{1,0:T(8,128)(2,1)S(1)} collective-permute-done((bf16[1024,256]{1,0:T(8,128)(2,1)}, bf16[1024,256]{1,0:T(8,128)(2,1)S(1)}, u32[]{:S(2)}, u32[]{:S(2)}) %collective-permute-start.2) | collective-permute-done | bytes 524320 | tf_op jit(solution)/shard_map/ppermute | solution.py:14
  77.7 1.8 %fusion.36 = f32[384,512]{1,0:T(8,128)S(1)} fusion(bf16[384,2048]{1,0:T(8,128)(2,1)S(1)} %bitcast.72, bf16[1024,256]{1,0:T(8,128)(2,1)S(1)} %collective-permute-done.2, bf16[1024,256]{1,0:T(8,128)(2,1)} %bitcast.86), kind=kOutput, calls=%fused_computation.70 | convolution fusion | flops 404750336 | bytes 2621440 | tf_op jit(solution)/shard_map/dot_general | solution.py:32
  79.5 9.4 %collective-permute-done.1 = bf16[1024,256]{1,0:T(8,128)(2,1)S(1)} collective-permute-done((bf16[1024,256]{1,0:T(8,128)(2,1)}, bf16[1024,256]{1,0:T(8,128)(2,1)S(1)}, u32[]{:S(2)}, u32[]{:S(2)}) %collective-permute-start.1) | collective-permute-done | bytes 524320 | tf_op jit(solution)/shard_map/ppermute | solution.py:14
  88.9 0.6 fusion.38
  89.5 0.2 copy-done.7
  89.7 0.9 copy-done.25
  90.6 2.1 %fusion.17 = f32[512,1024]{1,0:T(8,128)} fusion(bf16[384,2048]{1,0:T(8,128)(2,1)S(1)} %bitcast.74, f32[384,512]{1,0:T(8,128)S(1)} %fusion.38, f32[384,512]{1,0:T(8,128)S(1)} %fusion.36), kind=kOutput, calls=%fused_computation.51 | convolution fusion | flops 403832832 | bytes 4456448 | tf_op jit(solution)/shard_map/dot_general | solution.py:50
  92.7 6.4 %all-to-all-done.2 = bf16[16,24,2048]{2,1,0:T(8,128)(2,1)S(1)} async-done(((bf16[16,24,2048]{2,1,0:T(8,128)(2,1)}), bf16[16,24,2048]{2,1,0:T(8,128)(2,1)S(1)}, u32[]{:S(2)}, u32[]{:S(2)}) %all-to-all-start.2) | async-done | bytes 1572896 | tf_op jit(solution)/shard_map/all_to_all | solution.py:92
  99.1 1.9 %fusion.28 = f32[384,512]{1,0:T(8,128)S(1)} fusion(bf16[384,2048]{1,0:T(8,128)(2,1)S(1)} %bitcast.66, bf16[1024,256]{1,0:T(8,128)(2,1)} %copy-done.12, bf16[1024,256]{1,0:T(8,128)(2,1)} %bitcast.87), kind=kOutput, calls=%fused_computation.62 | convolution fusion | flops 404750336 | bytes 2621440 | tf_op jit(solution)/shard_map/dot_general | solution.py:32
  101.0 0.6 fusion.30
  101.5 1.0 copy-done.3
  102.5 0.8 convolution_add_fusion
  103.4 1.3 copy-done
  104.7 0.9 slice.167
  105.5 2.9 %collective-permute-start.5 = (bf16[256,1024]{1,0:T(8,128)(2,1)}, bf16[256,1024]{1,0:T(8,128)(2,1)}, u32[]{:S(2)}, u32[]{:S(2)}) collective-permute-start(bf16[256,1024]{1,0:T(8,128)(2,1)} %slice.167), channel_id=1, source_target_pairs={{0,256},{16,272},{32,288},{48,304},{64,320},{80,336},{96,352},{112... | collective-permute-start | bytes 1572872 | tf_op jit(solution)/shard_map/ppermute | solution.py:14
  108.4 1.9 %multiply_convert_fusion.3 = (bf16[384,512]{1,0:T(8,128)(2,1)S(1)}, bf16[384,512]{1,0:T(8,128)(2,1)S(1)}) fusion(f32[384,512]{1,0:T(8,128)S(1)} %fusion.28, f32[384,512]{1,0:T(8,128)S(1)} %fusion.30, bf16[256,1024]{1,0:T(8,128)(2,1)} %collective-permute-done, bf16[256,1024]{1,0:T(8,128)(2,1)S(1)} %bitcast.102, bf16[384,2048]{1,0:T(8,128)(2,1)S(1)} %bitcast.69), kind=kOutput, calls=%fused_computation.41 | convolution fusion | flops 407306240 | bytes 4194304 | tf_op jit(solution)/shard_map/dot_general | solution.py:37
  110.4 0.6 fusion.52
  111.0 0.7 copy-done.10
  111.7 0.2 copy-done.13
  111.8 1.5 add_convert_fusion
  113.3 4.4 %all-to-all-start.3 = ((bf16[16,24,1024]{2,1,0:T(8,128)(2,1)}), bf16[16,24,1024]{2,1,0:T(8,128)(2,1)}, u32[]{:S(2)}, u32[]{:S(2)}) async-start(bf16[16,24,1024]{2,1,0:T(8,128)(2,1)} %bitcast.79), calls=%async_computation.3 | async-start | bytes 1572864 | tf_op jit(solution)/shard_map/all_to_all | solution.py:106
  117.8 2.6 %multiply_convert_fusion.5 = (bf16[384,512]{1,0:T(8,128)(2,1)S(1)}, bf16[384,512]{1,0:T(8,128)(2,1)S(1)}) fusion(f32[384,512]{1,0:T(8,128)} %copy-done.24, f32[384,512]{1,0:T(8,128)} %copy-done.25, bf16[256,1024]{1,0:T(8,128)(2,1)} %collective-permute-done, bf16[256,1024]{1,0:T(8,128)(2,1)} %bitcast.101, bf16[384,2048]{1,0:T(8,128)(2,1)S(1)} %bitcast.75), kind=kOutput, calls=%fused_computation.45 | convolution fusion | flops 407306240 | bytes 4194304 | tf_op jit(solution)/shard_map/dot_general | solution.py:37
  120.4 0.6 fusion.53
  121.0 0.4 copy-done.11
  121.4 0.2 copy-done.14
  121.5 1.5 add_convert_fusion.1
  123.1 0.8 fusion.32
  123.8 0.2 copy-done.18
  124.1 2.0 %convolution_add_fusion.1 = f32[1024,512]{1,0:T(8,128)} fusion(f32[1024,512]{1,0:T(8,128)S(1)} %fusion.32, bf16[384,512]{1,0:T(8,128)(2,1)S(1)} %copy-done.18, bf16[384,2048]{1,0:T(8,128)(2,1)S(1)} %bitcast.70), kind=kOutput, calls=%fused_computation.1 | convolution fusion | flops 403177472 | bytes 5373952 | tf_op jit(solution)/shard_map/dot_general | solution.py:49
  126.1 14.5 %all-to-all-done.3 = bf16[16,24,1024]{2,1,0:T(8,128)(2,1)} async-done(((bf16[16,24,1024]{2,1,0:T(8,128)(2,1)}), bf16[16,24,1024]{2,1,0:T(8,128)(2,1)}, u32[]{:S(2)}, u32[]{:S(2)}) %all-to-all-start.3) | async-done | bytes 786464 | tf_op jit(solution)/shard_map/all_to_all | solution.py:106
  140.6 4.4 %all-to-all-start.1 = ((bf16[16,24,1024]{2,1,0:T(8,128)(2,1)}), bf16[16,24,1024]{2,1,0:T(8,128)(2,1)}, u32[]{:S(2)}, u32[]{:S(2)}) async-start(bf16[16,24,1024]{2,1,0:T(8,128)(2,1)} %bitcast.78), calls=%async_computation.1 | async-start | bytes 1572864 | tf_op jit(solution)/shard_map/all_to_all | solution.py:106
  145.0 0.7 fusion.34
  145.7 0.8 copy-done.2
  146.6 4.0 %collective-permute-start.4 = (bf16[1024,256]{1,0:T(8,128)(2,1)S(1)}, bf16[1024,256]{1,0:T(8,128)(2,1)S(1)}, u32[]{:S(2)}, u32[]{:S(2)}) collective-permute-start(bf16[1024,256]{1,0:T(8,128)(2,1)S(1)} %slice.168), channel_id=1, source_target_pairs={{0,256},{16,272},{32,288},{48,304},{64,320},{80,336},{96,352},{112... | collective-permute-start | bytes 1572872 | tf_op jit(solution)/shard_map/ppermute | solution.py:14
  150.7 0.7 convolution_add_fusion.2
  151.5 2.9 %collective-permute-start.3 = (bf16[1024,256]{1,0:T(8,128)(2,1)S(1)}, bf16[1024,256]{1,0:T(8,128)(2,1)S(1)}, u32[]{:S(2)}, u32[]{:S(2)}) collective-permute-start(bf16[1024,256]{1,0:T(8,128)(2,1)S(1)} %slice.169), channel_id=1, source_target_pairs={{0,256},{16,272},{32,288},{48,304},{64,320},{80,336},{96,352},{112... | collective-permute-start | bytes 1572872 | tf_op jit(solution)/shard_map/ppermute | solution.py:14
  154.4 2.0 %fusion.23 = bf16[1,1,256,1024]{3,2,1,0:T(8,128)(2,1)} fusion(bf16[256,1024]{1,0:T(8,128)(2,1)} %collective-permute-done.5, f32[512,1024]{1,0:T(8,128)S(1)} %copy-done.1), kind=kLoop, calls=%fused_computation.57 | loop fusion | flops 1048576 | bytes 2097152 | tf_op jit(solution)/shard_map/broadcast_in_dim | solution.py:128
  156.4 7.8 %collective-permute-done.4 = bf16[1024,256]{1,0:T(8,128)(2,1)S(1)} collective-permute-done((bf16[1024,256]{1,0:T(8,128)(2,1)S(1)}, bf16[1024,256]{1,0:T(8,128)(2,1)S(1)}, u32[]{:S(2)}, u32[]{:S(2)}) %collective-permute-start.4) | collective-permute-done | bytes 524320 | tf_op jit(solution)/shard_map/ppermute | solution.py:14
  164.2 1.0 fusion.22
  165.2 9.2 %collective-permute-done.3 = bf16[1024,256]{1,0:T(8,128)(2,1)S(1)} collective-permute-done((bf16[1024,256]{1,0:T(8,128)(2,1)S(1)}, bf16[1024,256]{1,0:T(8,128)(2,1)S(1)}, u32[]{:S(2)}, u32[]{:S(2)}) %collective-permute-start.3) | collective-permute-done | bytes 524320 | tf_op jit(solution)/shard_map/ppermute | solution.py:14
  174.3 1.0 fusion.21
  175.3 1.5 convolution_bitcast_fusion
  176.9 2.3 %fusion.4 = bf16[1,192,1024]{2,1,0:T(8,128)(2,1)} fusion(f32[192,1024]{1,0:T(8,128)S(1)} %convolution_bitcast_fusion, bf16[16,24,1024]{2,1,0:T(8,128)(2,1)} %all-to-all-done.1, pred[16,48,192]{2,1,0:T(8,128)(4,1)S(1)} %bitcast.96), kind=kOutput, calls=%fused_computation.17 | convolution fusion | flops 151388160 | bytes 2064384 | tf_op jit(solution)/shard_map/dot_general | solution.py:108
  (62 shorter events, 1.3 us)
Async XLA Ops:
  0.6 4.7 %copy-start.20 = (bf16[1,192,1024]{2,1,0:T(8,128)(2,1)S(1)}, bf16[1,192,1024]{2,1,0:T(8,128)(2,1)}, u32[]{:S(2)}) copy-start(bf16[1,192,1024]{2,1,0:T(8,128)(2,1)} %param.7) | copy-start | bytes 1179652
  0.6 4.7 %copy-start.19 = (bf16[1,192,1024]{2,1,0:T(8,128)(2,1)S(1)}, bf16[1,192,1024]{2,1,0:T(8,128)(2,1)}, u32[]{:S(2)}) copy-start(bf16[1,192,1024]{2,1,0:T(8,128)(2,1)} %param.8) | copy-start | bytes 1179652
  3.9 2.1 %copy-start.21 = (pred[768,192]{1,0:T(8,128)(4,1)}, pred[768,192]{1,0:T(8,128)(4,1)S(1)}, u32[]{:S(2)}) copy-start(pred[768,192]{1,0:T(8,128)(4,1)S(1)} %copy.22) | copy-start | bytes 442372
  7.5 48.9 %all-to-all-start = ((bf16[16,24,2048]{2,1,0:T(8,128)(2,1)}), bf16[16,24,2048]{2,1,0:T(8,128)(2,1)S(1)}, u32[]{:S(2)}, u32[]{:S(2)}) async-start(bf16[16,24,2048]{2,1,0:T(8,128)(2,1)} %bitcast.6), calls=%async_computation | async-start | bytes 3145728 | tf_op jit(solution)/shard_map/all_to_all | solution.py:92
  56.4 42.7 %all-to-all-start.2 = ((bf16[16,24,2048]{2,1,0:T(8,128)(2,1)}), bf16[16,24,2048]{2,1,0:T(8,128)(2,1)S(1)}, u32[]{:S(2)}, u32[]{:S(2)}) async-start(bf16[16,24,2048]{2,1,0:T(8,128)(2,1)} %bitcast.14), calls=%async_computation.2 | async-start | bytes 3145728 | tf_op jit(solution)/shard_map/all_to_all | solution.py:92
  60.5 28.4 %copy-start.4 = (bf16[1,1,1024,256]{3,2,1,0:T(8,128)(2,1)S(1)}, bf16[1,1,1024,256]{3,2,1,0:T(8,128)(2,1)}, u32[]{:S(2)}) copy-start(bf16[1,1,1024,256]{3,2,1,0:T(8,128)(2,1)} %param.12) | copy-start | bytes 1572868
  60.5 17.1 %collective-permute-start.2 = (bf16[1024,256]{1,0:T(8,128)(2,1)}, bf16[1024,256]{1,0:T(8,128)(2,1)S(1)}, u32[]{:S(2)}, u32[]{:S(2)}) collective-permute-start(bf16[1024,256]{1,0:T(8,128)(2,1)} %bitcast.85), channel_id=1, source_target_pairs={{0,256},{16,272},{32,288},{48,304},{64,320},{80,336},{96,352},{112... | collective-permute-start | bytes 1572872 | tf_op jit(solution)/shard_map/ppermute | solution.py:14
  63.6 25.3 %collective-permute-start.1 = (bf16[1024,256]{1,0:T(8,128)(2,1)}, bf16[1024,256]{1,0:T(8,128)(2,1)S(1)}, u32[]{:S(2)}, u32[]{:S(2)}) collective-permute-start(bf16[1024,256]{1,0:T(8,128)(2,1)} %bitcast.80), channel_id=1, source_target_pairs={{0,256},{16,272},{32,288},{48,304},{64,320},{80,336},{96,352},{112... | collective-permute-start | bytes 1572872 | tf_op jit(solution)/shard_map/ppermute | solution.py:14
  67.5 40.9 %collective-permute-start = (bf16[256,1024]{1,0:T(8,128)(2,1)}, bf16[256,1024]{1,0:T(8,128)(2,1)}, u32[]{:S(2)}, u32[]{:S(2)}) collective-permute-start(bf16[256,1024]{1,0:T(8,128)(2,1)} %bitcast.100), channel_id=1, source_target_pairs={{0,256},{16,272},{32,288},{48,304},{64,320},{80,336},{96,352},{112... | collective-permute-start | bytes 1572872 | tf_op jit(solution)/shard_map/ppermute | solution.py:14
  77.7 11.8 %copy-start.12 = (bf16[1024,256]{1,0:T(8,128)(2,1)}, bf16[1024,256]{1,0:T(8,128)(2,1)S(1)}, u32[]{:S(2)}) copy-start(bf16[1024,256]{1,0:T(8,128)(2,1)S(1)} %collective-permute-done.2) | copy-start | bytes 1572868
  79.5 10.0 %copy-start.24 = (f32[384,512]{1,0:T(8,128)}, f32[384,512]{1,0:T(8,128)S(1)}, u32[]{:S(2)}) copy-start(f32[384,512]{1,0:T(8,128)S(1)} %fusion.36) | copy-start | bytes 2359300
  88.9 0.8 copy-start.7
  89.7 0.9 copy-start.25
  99.1 1.9 %copy-start.5 = (bf16[1,1,1024,256]{3,2,1,0:T(8,128)(2,1)S(1)}, bf16[1,1,1024,256]{3,2,1,0:T(8,128)(2,1)}, u32[]{:S(2)}) copy-start(bf16[1,1,1024,256]{3,2,1,0:T(8,128)(2,1)} %param.12) | copy-start | bytes 1572868
  99.1 1.9 %copy-start.8 = (bf16[1024,256]{1,0:T(8,128)(2,1)S(1)}, bf16[1024,256]{1,0:T(8,128)(2,1)}, u32[]{:S(2)}) copy-start(bf16[1024,256]{1,0:T(8,128)(2,1)} %copy-done.7) | copy-start | bytes 1572868
  100.9 1.6 copy-start.3
  102.5 5.9 %copy-start.23 = (bf16[1,1,256,1024]{3,2,1,0:T(8,128)(2,1)S(1)}, bf16[1,1,256,1024]{3,2,1,0:T(8,128)(2,1)}, u32[]{:S(2)}) copy-start(bf16[1,1,256,1024]{3,2,1,0:T(8,128)(2,1)} %param.13) | copy-start | bytes 1572868
  103.3 1.3 copy-start
  105.5 48.8 %collective-permute-start.5 = (bf16[256,1024]{1,0:T(8,128)(2,1)}, bf16[256,1024]{1,0:T(8,128)(2,1)}, u32[]{:S(2)}, u32[]{:S(2)}) collective-permute-start(bf16[256,1024]{1,0:T(8,128)(2,1)} %slice.167), channel_id=1, source_target_pairs={{0,256},{16,272},{32,288},{48,304},{64,320},{80,336},{96,352},{112... | collective-permute-start | bytes 1572872 | tf_op jit(solution)/shard_map/ppermute | solution.py:14
  110.3 3.0 %copy-start.15 = (bf16[384,512]{1,0:T(8,128)(2,1)}, bf16[384,512]{1,0:T(8,128)(2,1)S(1)}, u32[]{:S(2)}) copy-start(bf16[384,512]{1,0:T(8,128)(2,1)S(1)} %get-tuple-element.6) | copy-start | bytes 1179652
  110.3 3.0 %copy-start.17 = (bf16[384,512]{1,0:T(8,128)(2,1)}, bf16[384,512]{1,0:T(8,128)(2,1)S(1)}, u32[]{:S(2)}) copy-start(bf16[384,512]{1,0:T(8,128)(2,1)S(1)} %get-tuple-element.7) | copy-start | bytes 1179652
  110.4 1.3 copy-start.10
  110.4 1.5 copy-start.13
  113.3 27.2 %all-to-all-start.3 = ((bf16[16,24,1024]{2,1,0:T(8,128)(2,1)}), bf16[16,24,1024]{2,1,0:T(8,128)(2,1)}, u32[]{:S(2)}, u32[]{:S(2)}) async-start(bf16[16,24,1024]{2,1,0:T(8,128)(2,1)} %bitcast.79), calls=%async_computation.3 | async-start | bytes 1572864 | tf_op jit(solution)/shard_map/all_to_all | solution.py:106
  117.7 2.6 %copy-start.6 = (bf16[1,1,1024,256]{3,2,1,0:T(8,128)(2,1)S(1)}, bf16[1,1,1024,256]{3,2,1,0:T(8,128)(2,1)}, u32[]{:S(2)}) copy-start(bf16[1,1,1024,256]{3,2,1,0:T(8,128)(2,1)} %param.12) | copy-start | bytes 1572868
  117.7 2.6 %copy-start.9 = (bf16[1024,256]{1,0:T(8,128)(2,1)S(1)}, bf16[1024,256]{1,0:T(8,128)(2,1)}, u32[]{:S(2)}) copy-start(bf16[1024,256]{1,0:T(8,128)(2,1)} %copy-done.7) | copy-start | bytes 1572868
  120.3 1.0 copy-start.11
  120.3 1.2 copy-start.14
  123.1 1.0 copy-start.18
  140.6 36.3 %all-to-all-start.1 = ((bf16[16,24,1024]{2,1,0:T(8,128)(2,1)}), bf16[16,24,1024]{2,1,0:T(8,128)(2,1)}, u32[]{:S(2)}, u32[]{:S(2)}) async-start(bf16[16,24,1024]{2,1,0:T(8,128)(2,1)} %bitcast.78), calls=%async_computation.1 | async-start | bytes 1572864 | tf_op jit(solution)/shard_map/all_to_all | solution.py:106
  144.9 1.6 copy-start.2
  144.9 5.7 %copy-start.16 = (bf16[384,512]{1,0:T(8,128)(2,1)S(1)}, bf16[384,512]{1,0:T(8,128)(2,1)}, u32[]{:S(2)}) copy-start(bf16[384,512]{1,0:T(8,128)(2,1)} %copy-done.15) | copy-start | bytes 1179652
  146.6 7.8 %copy-start.1 = (f32[512,1024]{1,0:T(8,128)S(1)}, f32[512,1024]{1,0:T(8,128)}, u32[]{:S(2)}) copy-start(f32[512,1024]{1,0:T(8,128)} %copy-done) | copy-start | bytes 6291460
  146.6 17.6 %collective-permute-start.4 = (bf16[1024,256]{1,0:T(8,128)(2,1)S(1)}, bf16[1024,256]{1,0:T(8,128)(2,1)S(1)}, u32[]{:S(2)}, u32[]{:S(2)}) collective-permute-start(bf16[1024,256]{1,0:T(8,128)(2,1)S(1)} %slice.168), channel_id=1, source_target_pairs={{0,256},{16,272},{32,288},{48,304},{64,320},{80,336},{96,352},{112... | collective-permute-start | bytes 1572872 | tf_op jit(solution)/shard_map/ppermute | solution.py:14
  151.5 22.8 %collective-permute-start.3 = (bf16[1024,256]{1,0:T(8,128)(2,1)S(1)}, bf16[1024,256]{1,0:T(8,128)(2,1)S(1)}, u32[]{:S(2)}, u32[]{:S(2)}) collective-permute-start(bf16[1024,256]{1,0:T(8,128)(2,1)S(1)} %slice.169), channel_id=1, source_target_pairs={{0,256},{16,272},{32,288},{48,304},{64,320},{80,336},{96,352},{112... | collective-permute-start | bytes 1572872 | tf_op jit(solution)/shard_map/ppermute | solution.py:14
  156.4 18.9 %copy-start.22 = (pred[768,192]{1,0:T(8,128)(4,1)S(1)}, pred[768,192]{1,0:T(8,128)(4,1)}, u32[]{:S(2)}) copy-start(pred[768,192]{1,0:T(8,128)(4,1)} %copy-done.21) | copy-start | bytes 442372

commit v2 on v1

--- a/solution.py
+++ b/solution.py
@@ -66,8 +66,12 @@
     own_gate = w_gate[0, 0]
     own_up = w_up[0, 0]
     own_down = w_down[0, 0]
-    half = own_gate.shape[1]
-    other_gate, other_up, other_down = partner((own_gate, own_up, own_down), "section", pair_bit)
+    dim, half = own_gate.shape
+    packed = jnp.stack([own_gate, own_up, own_down.reshape(dim, half)])
+    other = partner(packed, "section", pair_bit)
+    full_gate = jnp.concatenate([own_gate, other[0]], axis=1)
+    full_up = jnp.concatenate([own_up, other[1]], axis=1)
+    full_down = jnp.concatenate([own_down, other[2].reshape(half, dim)], axis=0)
 
     hit = dispatch_matrix(ids, cap, experts)
     pair_gate = jnp.sum(jnp.where(hit, gates.reshape(tok * topk)[None, :], 0.0), axis=1)
@@ -79,9 +83,7 @@
     step = cap // CHUNKS
     chunk_rows = experts * step
 
-    full_gate = full_up = full_down = None
-    token_acc = jnp.zeros((tok, width), jnp.float32)
-    acc_g = acc_u = acc_d = None
+    recv_all = []
     for c in range(CHUNKS):
         sel = token_hit[:, c * step:(c + 1) * step, :].reshape(chunk_rows, tok)
         sgate = pair_gate[:, c * step:(c + 1) * step].reshape(chunk_rows, 1)
@@ -90,11 +92,12 @@
         slot_grad = (picked[:, width:] * sgate).astype(jnp.bfloat16)
         send = jnp.concatenate([slot_in, slot_grad], axis=1).reshape(experts, step, 2 * width)
         recv = lax.all_to_all(send, "expert", split_axis=0, concat_axis=0, tiled=True)
-        recv = recv.reshape(chunk_rows, 2 * width)
-        if full_gate is None:
-            full_gate = jnp.concatenate([own_gate, other_gate], axis=1)
-            full_up = jnp.concatenate([own_up, other_up], axis=1)
-            full_down = jnp.concatenate([own_down, other_down], axis=0)
+        recv_all.append(recv)
+
+    acc_g = acc_u = acc_d = None
+    backs = []
+    for c in range(CHUNKS):
+        recv = recv_all[c].reshape(chunk_rows, 2 * width)
         pair_grad, grad_g, grad_u, grad_d = expert_grads(
             recv[:, :width], recv[:, width:], full_gate, full_up, full_down
         )
@@ -102,25 +105,27 @@
             acc_g, acc_u, acc_d = grad_g, grad_u, grad_d
         else:
             acc_g, acc_u, acc_d = acc_g + grad_g, acc_u + grad_u, acc_d + grad_d
-        back = pair_grad.astype(jnp.bfloat16).reshape(experts, step, width)
-        home = lax.all_to_all(back, "expert", split_axis=0, concat_axis=0, tiled=True)
-        home = home.reshape(chunk_rows, width)
-        token_acc = token_acc + lax.dot_general(
-            sel, home, (((0,), (0,)), ((), ())), preferred_element_type=jnp.float32
-        )
+        backs.append(pair_grad.astype(jnp.bfloat16).reshape(experts, step, width))
 
-    peer_g, peer_u, peer_d = partner(
-        (
+    back = jnp.concatenate(backs, axis=1)
+    home = lax.all_to_all(back, "expert", split_axis=0, concat_axis=0, tiled=True)
+    home = home.reshape(experts * cap, width)
+    token_acc = lax.dot_general(
+        token_hit.reshape(experts * cap, tok), home, (((0,), (0,)), ((), ())),
+        preferred_element_type=jnp.float32,
+    )
+
+    peer_packed = jnp.stack(
+        [
             acc_g[:, half:].astype(jnp.bfloat16),
             acc_u[:, half:].astype(jnp.bfloat16),
-            acc_d[half:, :].astype(jnp.bfloat16),
-        ),
-        "section",
-        pair_bit,
+            acc_d[half:, :].astype(jnp.bfloat16).reshape(dim, half),
+        ]
     )
-    mine_g = acc_g[:, :half] + peer_g.astype(jnp.float32)
-    mine_u = acc_u[:, :half] + peer_u.astype(jnp.float32)
-    mine_d = acc_d[:half, :] + peer_d.astype(jnp.float32)
+    peer = partner(peer_packed, "section", pair_bit).astype(jnp.float32)
+    mine_g = acc_g[:, :half] + peer[0]
+    mine_u = acc_u[:, :half] + peer[1]
+    mine_d = acc_d[:half, :] + peer[2].reshape(half, dim)
     token_grad = token_acc.astype(jnp.bfloat16)
     out_g = (mine_g * scale).astype(jnp.bfloat16)
     out_u = (mine_u * scale).astype(jnp.bfloat16)

time: 180 us -> 196 us (1.089)
  waiting for transfers between devices: 90.9 us -> 109 us
  starting transfers between devices: 42.8 us -> 28.3 us
  local copies, waits for them, and re-layouts: 10.5 us -> 21.1 us
    ppermute x6 -> x2, waiting for transfers between devices: 33.7 us -> 72.5 us  [partner(): return lax.ppermute(value, axis, pairs)]
    all_to_all x2 -> x1, waiting for transfers between devices: 14.5 us -> 0.01 us  [per_device(): lax.all_to_all(back, 'expert', split_axis=0, concat_axis=0, tiled=True)]
    ppermute x6 -> x2, starting transfers between devices: 19.6 us -> 5.93 us  [partner(): return lax.ppermute(value, axis, pairs)]
    another operation x0 -> x6, local copies, waits for them, and re-layouts: none -> 8.13 us  [the longest x3 2.29 us: per_device(): jnp.stack([acc_g[:, half:].astype(jnp.bfloat16), acc_u[:, half:].astype(j...]
    all_to_all x2, waiting for transfers between devices: 42.8 us -> 36.4 us  [per_device(): lax.all_to_all(send, 'expert', split_axis=0, concat_axis=0, tiled=True)]
    dot_general x2, matrix products: 1.2 us -> 3.61 us  [expert_grads(): lax.dot_general(up_grad, up_w, contract_last, preferred_element_type=jnp....]
    dot_general x2, matrix products: 4.45 us -> 2.47 us  [expert_grads(): lax.dot_general(rows_grad, down_w, contract_last, preferred_element_type=...]
    all_to_all x2 -> x1, starting transfers between devices: 8.78 us -> 7.91 us  [per_device(): lax.all_to_all(back, 'expert', split_axis=0, concat_axis=0, tiled=True)]
  transfers between devices with their start and end apart: 10 -> 5, of which waited for: 7 -> 3; matrix products, arithmetic and copies ran while one was open for 16% -> 11% of each run, Pallas kernels for 0% -> 0%
where the time goes in v2:
time: 196 us; the launch traced here: 195 us
  waiting for transfers between devices  109 us (56%)
  starting transfers between devices  28.3 us (14%)
  matrix products  25.7 us (13%)
  local copies, waits for them, and re-layouts  21.1 us (11%)
  other arithmetic  10.1 us (5%)
    ppermute x2, waiting for transfers between devices, partner(): return lax.ppermute(value, axis, pairs)  72.5 us
    all_to_all x2, waiting for transfers between devices, per_device(): lax.all_to_all(send, 'expert', split_axis=0, concat_axis=0, tiled=True)  36.4 us
    all_to_all x2, starting transfers between devices, per_device(): lax.all_to_all(send, 'expert', split_axis=0, concat_axis=0, tiled=True)  14.5 us
    unnamed x50, local copies, waits for them, and re-layouts  8.04 us
    all_to_all x1, starting transfers between devices, per_device(): lax.all_to_all(back, 'expert', split_axis=0, concat_axis=0, tiled=True)  7.91 us
    ppermute x2, starting transfers between devices, partner(): return lax.ppermute(value, axis, pairs)  5.93 us
    dot_general x2, matrix products, expert_grads(): lax.dot_general(rows_in, up_grad, contract_rows, preferred_element_type=j...  4.55 us
    dot_general x2, matrix products, expert_grads(): gate_pre = jnp.dot(rows_in, gate_w, preferred_element_type=jnp.float32)  4.52 us
  transfers between devices with their start and end apart: 5, of which 3 were waited for; matrix products, arithmetic and copies ran while one was open for 11% of the time, Pallas kernels for 0%

profile of v2, /device:TPU:1, one launch (start us, length us, event | category | flops | bytes accessed | tf_op | source)
XLA Modules:
  0.0 195.1 jit_solution(13490893247215182566)
XLA Ops:
  0.7 0.9 copy.23
  1.5 0.1 eq.45
  1.7 0.1 eq.49
  1.8 0.9 reduce-window.6
  2.7 0.2 slice_reduce_fusion
  3.1 0.1 reduce_sum.21
  3.3 0.8 copy.29
  4.1 0.1 broadcast_in_dim.29
  4.3 0.2 select_reduce_fusion
  4.7 0.2 fusion.3
  4.9 0.4 copy.28
  5.3 0.6 fusion.26
  6.0 0.1 fusion
  6.2 1.2 pad_maximum_fusion.2
  7.4 10.3 %all-to-all-start.1 = ((bf16[16,24,2048]{2,1,0:T(8,128)(2,1)}), bf16[16,24,2048]{2,1,0:T(8,128)(2,1)S(1)}, u32[]{:S(2)}, u32[]{:S(2)}) async-start(bf16[16,24,2048]{2,1,0:T(8,128)(2,1)} %bitcast.17), calls=%async_computation.1 | async-start | bytes 3145728 | tf_op jit(solution)/shard_map/all_to_all | solution.py:94
  17.8 0.6 fusion.27
  18.5 0.1 fusion.1
  18.7 1.3 pad_maximum_fusion
  20.0 36.4 %all-to-all-done.1 = bf16[16,24,2048]{2,1,0:T(8,128)(2,1)S(1)} async-done(((bf16[16,24,2048]{2,1,0:T(8,128)(2,1)}), bf16[16,24,2048]{2,1,0:T(8,128)(2,1)S(1)}, u32[]{:S(2)}, u32[]{:S(2)}) %all-to-all-start.1) | async-done | bytes 1572896 | tf_op jit(solution)/shard_map/all_to_all | solution.py:94
  56.3 4.1 %all-to-all-start = ((bf16[16,24,2048]{2,1,0:T(8,128)(2,1)}), bf16[16,24,2048]{2,1,0:T(8,128)(2,1)S(1)}, u32[]{:S(2)}, u32[]{:S(2)}) async-start(bf16[16,24,2048]{2,1,0:T(8,128)(2,1)} %bitcast.6), calls=%async_computation | async-start | bytes 3145728 | tf_op jit(solution)/shard_map/all_to_all | solution.py:94
  60.5 2.1 %stack_reshape_squeeze.3 = bf16[1,1024,256]{2,1,0:T(8,128)(2,1)} reshape(bf16[1,1,256,1024]{3,2,1,0:T(8,128)(2,1)} %param.13) | data formatting | bytes 1048576 | tf_op jit(solution)/shard_map/stack;reshape;squeeze | solution.py:70
  62.6 1.5 pad_maximum_fusion.1
  64.1 3.1 %collective-permute-start = (bf16[3,1024,256]{2,1,0:T(8,128)(2,1)S(1)}, bf16[3,1024,256]{2,1,0:T(8,128)(2,1)S(1)}, u32[]{:S(2)}, u32[]{:S(2)}) collective-permute-start(bf16[3,1024,256]{2,1,0:T(8,128)(2,1)S(1)} %pad_maximum_fusion.1), channel_id=1, source_target_pairs={{0,256},{16,272},{32,288},{48,304},{64,320},{80,336},{96,352},{112... | collective-permute-start | bytes 4718600 | tf_op jit(solution)/shard_map/ppermute | solution.py:14
  67.2 36.2 %collective-permute-done = bf16[3,1024,256]{2,1,0:T(8,128)(2,1)S(1)} collective-permute-done((bf16[3,1024,256]{2,1,0:T(8,128)(2,1)S(1)}, bf16[3,1024,256]{2,1,0:T(8,128)(2,1)S(1)}, u32[]{:S(2)}, u32[]{:S(2)}) %collective-permute-start) | collective-permute-done | bytes 1572896 | tf_op jit(solution)/shard_map/ppermute | solution.py:14
  103.4 1.2 slice_bitcast_fusion.3
  104.6 2.2 %reshape_squeeze.7 = bf16[256,1024]{1,0:T(8,128)(2,1)} reshape(bf16[1,1024,256]{2,1,0:T(8,128)(2,1)} %get-tuple-element.12) | data formatting | bytes 1048576 | tf_op jit(solution)/shard_map/reshape;squeeze | solution.py:74
  106.7 2.7 %fusion.30 = f32[384,512]{1,0:T(8,128)} fusion(bf16[384,2048]{1,0:T(8,128)(2,1)S(1)} %bitcast.89, bf16[1024,256]{1,0:T(8,128)(2,1)} %get-tuple-element.11, bf16[1024,256]{1,0:T(8,128)(2,1)} %bitcast.107), kind=kOutput, calls=%fused_computation.68 | convolution fusion | flops 404750336 | bytes 2621440 | tf_op jit(solution)/shard_map/dot_general | solution.py:32
  109.4 1.9 fusion.38
  111.3 0.6 fusion.32
  111.9 0.6 fusion.40
  112.5 0.8 fusion.17
  113.3 0.2 copy-done.22
  113.5 0.2 copy-done.23
  113.7 0.9 multiply_convert_fusion.5
  114.5 1.8 fusion.55
  116.3 2.1 %fusion.34 = f32[1024,512]{1,0:T(8,128)} fusion(bf16[384,512]{1,0:T(8,128)(2,1)S(1)} %get-tuple-element.7, bf16[384,2048]{1,0:T(8,128)(2,1)S(1)} %bitcast.99), kind=kOutput, calls=%fused_computation.72 | convolution fusion | flops 402653184 | bytes 3276800 | tf_op jit(solution)/shard_map/dot_general | solution.py:49
  118.4 1.6 multiply_convert_fusion.3
  120.0 1.9 fusion.54
  121.8 0.8 convolution_add_fusion
  122.7 1.3 copy-done.1
  124.0 0.9 slice.209
  124.9 2.1 %stack_reshape.3 = bf16[1,1024,256]{2,1,0:T(8,128)(2,1)} reshape(bf16[256,1024]{1,0:T(8,128)(2,1)} %slice.209) | data formatting | bytes 1048576 | tf_op jit(solution)/shard_map/stack;reshape | solution.py:118
  127.0 2.1 %fusion.36 = f32[1024,512]{1,0:T(8,128)} fusion(bf16[384,512]{1,0:T(8,128)(2,1)S(1)} %get-tuple-element.6, bf16[384,2048]{1,0:T(8,128)(2,1)S(1)} %bitcast.100), kind=kOutput, calls=%fused_computation.74 | convolution fusion | flops 402653184 | bytes 3276800 | tf_op jit(solution)/shard_map/dot_general | solution.py:48
  129.1 0.6 add_convert_fusion.1
  129.8 0.8 copy-done.8
  130.6 0.6 add_convert_fusion
  131.2 1.4 pad_maximum_fusion.3
  132.6 7.9 %all-to-all-start.2 = ((bf16[16,48,1024]{2,1,0:T(8,128)(2,1)}), bf16[16,48,1024]{2,1,0:T(8,128)(2,1)}, u32[]{:S(2)}, u32[]{:S(2)}) async-start(bf16[16,48,1024]{2,1,0:T(8,128)(2,1)} %pad_maximum_fusion.3), calls=%async_computation.2 | async-start | bytes 3145728 | tf_op jit(solution)/shard_map/all_to_all | solution.py:111
  140.5 2.5 %convolution_add_fusion.1 = f32[1024,512]{1,0:T(8,128)S(1)} fusion(f32[1024,512]{1,0:T(8,128)} %fusion.34, bf16[384,512]{1,0:T(8,128)(2,1)S(1)} %copy-done.16, bf16[384,2048]{1,0:T(8,128)(2,1)S(1)} %bitcast.93), kind=kOutput, calls=%fused_computation.1 | convolution fusion | flops 403177472 | bytes 5373952 | tf_op jit(solution)/shard_map/dot_general | solution.py:49
  143.1 0.7 convolution_add_fusion.2
  143.9 0.5 copy-done.3
  144.4 0.1 copy-done.13
  144.6 0.2 pad_maximum_fusion.4
  144.7 1.0 copy-done.5
  145.7 2.9 %collective-permute-start.1 = (bf16[3,1024,256]{2,1,0:T(8,128)(2,1)S(1)}, bf16[3,1024,256]{2,1,0:T(8,128)(2,1)S(1)}, u32[]{:S(2)}, u32[]{:S(2)}) collective-permute-start(bf16[3,1024,256]{2,1,0:T(8,128)(2,1)S(1)} %pad_maximum_fusion.4), channel_id=1, source_target_pairs={{0,256},{16,272},{32,288},{48,304},{64,320},{80,336},{96,352},{112... | collective-permute-start | bytes 4718600 | tf_op jit(solution)/shard_map/ppermute | solution.py:14
  148.6 36.3 %collective-permute-done.1 = bf16[3,1024,256]{2,1,0:T(8,128)(2,1)S(1)} collective-permute-done((bf16[3,1024,256]{2,1,0:T(8,128)(2,1)S(1)}, bf16[3,1024,256]{2,1,0:T(8,128)(2,1)S(1)}, u32[]{:S(2)}, u32[]{:S(2)}) %collective-permute-start.1) | collective-permute-done | bytes 1572896 | tf_op jit(solution)/shard_map/ppermute | solution.py:14
  184.9 1.1 slice.133
  186.0 1.5 reshape_squeeze.8
  187.5 0.3 convert_element_type.71
  187.8 1.3 copy-done.2
  189.1 1.0 fusion.25
  190.1 0.9 copy-done.4
  191.0 1.4 fusion.24
  192.5 2.6 %fusion.2 = bf16[1,192,1024]{2,1,0:T(8,128)(2,1)} fusion(pred[768,192]{0,1:T(8,128)(4,1)S(1)} %copy-done.21, bf16[768,1024]{1,0:T(8,128)(2,1)} %bitcast.20), kind=kOutput, calls=%fused_computation.17 | convolution fusion | flops 302186496 | bytes 2113536 | tf_op jit(solution)/shard_map/dot_general | solution.py:113
  (56 shorter events, 1.1 us)
Async XLA Ops:
  0.6 4.7 %copy-start.17 = (bf16[1,192,1024]{2,1,0:T(8,128)(2,1)S(1)}, bf16[1,192,1024]{2,1,0:T(8,128)(2,1)}, u32[]{:S(2)}) copy-start(bf16[1,192,1024]{2,1,0:T(8,128)(2,1)} %param.8) | copy-start | bytes 1179652
  0.6 4.7 %copy-start.18 = (bf16[1,192,1024]{2,1,0:T(8,128)(2,1)S(1)}, bf16[1,192,1024]{2,1,0:T(8,128)(2,1)}, u32[]{:S(2)}) copy-start(bf16[1,192,1024]{2,1,0:T(8,128)(2,1)} %param.7) | copy-start | bytes 1179652
  4.9 1.0 copy-start.20
  7.4 48.9 %all-to-all-start.1 = ((bf16[16,24,2048]{2,1,0:T(8,128)(2,1)}), bf16[16,24,2048]{2,1,0:T(8,128)(2,1)S(1)}, u32[]{:S(2)}, u32[]{:S(2)}) async-start(bf16[16,24,2048]{2,1,0:T(8,128)(2,1)} %bitcast.17), calls=%async_computation.1 | async-start | bytes 3145728 | tf_op jit(solution)/shard_map/all_to_all | solution.py:94
  56.3 53.1 %all-to-all-start = ((bf16[16,24,2048]{2,1,0:T(8,128)(2,1)}), bf16[16,24,2048]{2,1,0:T(8,128)(2,1)S(1)}, u32[]{:S(2)}, u32[]{:S(2)}) async-start(bf16[16,24,2048]{2,1,0:T(8,128)(2,1)} %bitcast.6), calls=%async_computation | async-start | bytes 3145728 | tf_op jit(solution)/shard_map/all_to_all | solution.py:94
  64.1 39.2 %collective-permute-start = (bf16[3,1024,256]{2,1,0:T(8,128)(2,1)S(1)}, bf16[3,1024,256]{2,1,0:T(8,128)(2,1)S(1)}, u32[]{:S(2)}, u32[]{:S(2)}) collective-permute-start(bf16[3,1024,256]{2,1,0:T(8,128)(2,1)S(1)} %pad_maximum_fusion.1), channel_id=1, source_target_pairs={{0,256},{16,272},{32,288},{48,304},{64,320},{80,336},{96,352},{112... | collective-permute-start | bytes 4718600 | tf_op jit(solution)/shard_map/ppermute | solution.py:14
  109.4 1.9 copy-start.9
  109.4 1.9 copy-start.10
  112.5 1.0 copy-start.22
  112.5 1.2 copy-start.23
  116.3 2.1 %copy-start.19 = (f32[384,512]{1,0:T(8,128)S(1)}, f32[384,512]{1,0:T(8,128)}, u32[]{:S(2)}) copy-start(f32[384,512]{1,0:T(8,128)} %fusion.30) | copy-start | bytes 2359300
  120.0 2.7 %copy-start.15 = (bf16[384,512]{1,0:T(8,128)(2,1)}, bf16[384,512]{1,0:T(8,128)(2,1)S(1)}, u32[]{:S(2)}) copy-start(bf16[384,512]{1,0:T(8,128)(2,1)S(1)} %get-tuple-element.9) | copy-start | bytes 1179652
  122.6 1.3 copy-start.1
  127.0 2.1 %copy-start.7 = (f32[384,1024]{1,0:T(8,128)S(1)}, f32[384,1024]{1,0:T(8,128)}, u32[]{:S(2)}) copy-start(f32[384,1024]{1,0:T(8,128)} %fusion.55) | copy-start | bytes 4718596
  127.0 2.1 %copy-start.11 = (bf16[1,1,1024,256]{3,2,1,0:T(8,128)(2,1)S(1)}, bf16[1,1,1024,256]{3,2,1,0:T(8,128)(2,1)}, u32[]{:S(2)}) copy-start(bf16[1,1,1024,256]{3,2,1,0:T(8,128)(2,1)} %param.11) | copy-start | bytes 1572868
  127.0 2.1 %copy-start.12 = (bf16[1024,256]{1,0:T(8,128)(2,1)S(1)}, bf16[1024,256]{1,0:T(8,128)(2,1)}, u32[]{:S(2)}) copy-start(bf16[1024,256]{1,0:T(8,128)(2,1)} %get-tuple-element.11) | copy-start | bytes 1572868
  129.1 1.4 copy-start.8
  129.1 1.5 copy-start.14
  132.6 7.9 %copy-start.16 = (bf16[384,512]{1,0:T(8,128)(2,1)S(1)}, bf16[384,512]{1,0:T(8,128)(2,1)}, u32[]{:S(2)}) copy-start(bf16[384,512]{1,0:T(8,128)(2,1)} %copy-done.15) | copy-start | bytes 1179652
  132.6 59.8 %all-to-all-start.2 = ((bf16[16,48,1024]{2,1,0:T(8,128)(2,1)}), bf16[16,48,1024]{2,1,0:T(8,128)(2,1)}, u32[]{:S(2)}, u32[]{:S(2)}) async-start(bf16[16,48,1024]{2,1,0:T(8,128)(2,1)} %pad_maximum_fusion.3), calls=%async_computation.2 | async-start | bytes 3145728 | tf_op jit(solution)/shard_map/all_to_all | solution.py:111
  140.5 2.6 %copy-start = (f32[1024,512]{1,0:T(8,128)S(1)}, f32[1024,512]{1,0:T(8,128)}, u32[]{:S(2)}) copy-start(f32[1024,512]{1,0:T(8,128)} %fusion.36) | copy-start | bytes 6291460
  143.0 1.3 copy-start.3
  143.1 1.4 copy-start.13
  144.3 1.4 copy-start.5
  145.7 39.2 %collective-permute-start.1 = (bf16[3,1024,256]{2,1,0:T(8,128)(2,1)S(1)}, bf16[3,1024,256]{2,1,0:T(8,128)(2,1)S(1)}, u32[]{:S(2)}, u32[]{:S(2)}) collective-permute-start(bf16[3,1024,256]{2,1,0:T(8,128)(2,1)S(1)} %pad_maximum_fusion.4), channel_id=1, source_target_pairs={{0,256},{16,272},{32,288},{48,304},{64,320},{80,336},{96,352},{112... | collective-permute-start | bytes 4718600 | tf_op jit(solution)/shard_map/ppermute | solution.py:14
  187.5 1.6 copy-start.2
  187.5 2.6 %copy-start.6 = (f32[1024,512]{1,0:T(8,128)S(1)}, f32[1024,512]{1,0:T(8,128)}, u32[]{:S(2)}) copy-start(f32[1024,512]{1,0:T(8,128)} %copy-done.5) | copy-start | bytes 6291460
  189.1 1.9 copy-start.4
  191.0 1.5 copy-start.21

commit v3 on v2

--- a/solution.py
+++ b/solution.py
@@ -4,6 +4,7 @@
 import jax.numpy as jnp
 from jax import lax
 from jax.sharding import PartitionSpec as P
+
 
 CHUNKS = 2
 
@@ -26,7 +27,7 @@
     return hit
 
 
-def expert_grads(rows_in, rows_grad, gate_w, up_w, down_w):
+def grad_terms(rows_in, rows_grad, gate_w, up_w, down_w):
     contract_last = (((1,), (1,)), ((), ()))
     contract_rows = (((0,), (0,)), ((), ()))
     gate_pre = jnp.dot(rows_in, gate_w, preferred_element_type=jnp.float32)
@@ -39,16 +40,24 @@
         jnp.bfloat16
     )
     up_grad = (act_grad * swish_val).astype(jnp.bfloat16)
-    pair_grad = lax.dot_general(
-        gate_grad, gate_w, contract_last, preferred_element_type=jnp.float32
-    )
-    pair_grad = pair_grad + lax.dot_general(
-        up_grad, up_w, contract_last, preferred_element_type=jnp.float32
-    )
-    grad_g = lax.dot_general(rows_in, gate_grad, contract_rows, preferred_element_type=jnp.float32)
-    grad_u = lax.dot_general(rows_in, up_grad, contract_rows, preferred_element_type=jnp.float32)
-    grad_d = lax.dot_general(act, rows_grad, contract_rows, preferred_element_type=jnp.float32)
-    return (pair_grad, grad_g, grad_u, grad_d)
+
+    def weight_part(lo, hi):
+        return (
+            lax.dot_general(rows_in, gate_grad[:, lo:hi], contract_rows, preferred_element_type=jnp.float32),
+            lax.dot_general(rows_in, up_grad[:, lo:hi], contract_rows, preferred_element_type=jnp.float32),
+            lax.dot_general(act[:, lo:hi], rows_grad, contract_rows, preferred_element_type=jnp.float32),
+        )
+
+    def pair_part():
+        pair_grad = lax.dot_general(
+            gate_grad, gate_w, contract_last, preferred_element_type=jnp.float32
+        )
+        pair_grad = pair_grad + lax.dot_general(
+            up_grad, up_w, contract_last, preferred_element_type=jnp.float32
+        )
+        return pair_grad
+
+    return weight_part, pair_part
 
 
 def per_device(tokens, out_grad, expert_ids, gate_weights, w_gate, w_up, w_down):
@@ -84,6 +93,7 @@
     chunk_rows = experts * step
 
     recv_all = []
+    sels = []
     for c in range(CHUNKS):
         sel = token_hit[:, c * step:(c + 1) * step, :].reshape(chunk_rows, tok)
         sgate = pair_gate[:, c * step:(c + 1) * step].reshape(chunk_rows, 1)
@@ -93,39 +103,42 @@
         send = jnp.concatenate([slot_in, slot_grad], axis=1).reshape(experts, step, 2 * width)
         recv = lax.all_to_all(send, "expert", split_axis=0, concat_axis=0, tiled=True)
         recv_all.append(recv)
+        sels.append(sel)
 
-    acc_g = acc_u = acc_d = None
-    backs = []
+    peer_acc = own_acc = None
+    token_acc = None
     for c in range(CHUNKS):
         recv = recv_all[c].reshape(chunk_rows, 2 * width)
-        pair_grad, grad_g, grad_u, grad_d = expert_grads(
+        weight_part, pair_part = grad_terms(
             recv[:, :width], recv[:, width:], full_gate, full_up, full_down
         )
-        if acc_g is None:
-            acc_g, acc_u, acc_d = grad_g, grad_u, grad_d
-        else:
-            acc_g, acc_u, acc_d = acc_g + grad_g, acc_u + grad_u, acc_d + grad_d
-        backs.append(pair_grad.astype(jnp.bfloat16).reshape(experts, step, width))
+        peer_terms = weight_part(half, 2 * half)
+        if peer_acc is not None:
+            peer_terms = tuple(a + b for a, b in zip(peer_acc, peer_terms))
+        peer_acc = peer_terms
+        back = pair_part().astype(jnp.bfloat16).reshape(experts, step, width)
+        home = lax.all_to_all(back, "expert", split_axis=0, concat_axis=0, tiled=True)
+        own_terms = weight_part(0, half)
+        own_acc = own_terms if own_acc is None else tuple(a + b for a, b in zip(own_acc, own_terms))
+        part = lax.dot_general(
+            sels[c], home.reshape(chunk_rows, width), (((0,), (0,)), ((), ())),
+            preferred_element_type=jnp.float32,
+        )
+        token_acc = part if token_acc is None else token_acc + part
 
-    back = jnp.concatenate(backs, axis=1)
-    home = lax.all_to_all(back, "expert", split_axis=0, concat_axis=0, tiled=True)
-    home = home.reshape(experts * cap, width)
-    token_acc = lax.dot_general(
-        token_hit.reshape(experts * cap, tok), home, (((0,), (0,)), ((), ())),
-        preferred_element_type=jnp.float32,
-    )
-
+    peer_g, peer_u, peer_d = peer_acc
     peer_packed = jnp.stack(
         [
-            acc_g[:, half:].astype(jnp.bfloat16),
-            acc_u[:, half:].astype(jnp.bfloat16),
-            acc_d[half:, :].astype(jnp.bfloat16).reshape(dim, half),
+            peer_g.astype(jnp.bfloat16),
+            peer_u.astype(jnp.bfloat16),
+            peer_d.astype(jnp.bfloat16).reshape(dim, half),
         ]
     )
     peer = partner(peer_packed, "section", pair_bit).astype(jnp.float32)
-    mine_g = acc_g[:, :half] + peer[0]
-    mine_u = acc_u[:, :half] + peer[1]
-    mine_d = acc_d[:half, :] + peer[2].reshape(half, dim)
+    own_g, own_u, own_d = own_acc
+    mine_g = own_g + peer[0]
+    mine_u = own_u + peer[1]
+    mine_d = own_d + peer[2].reshape(half, dim)
     token_grad = token_acc.astype(jnp.bfloat16)
     out_g = (mine_g * scale).astype(jnp.bfloat16)
     out_u = (mine_u * scale).astype(jnp.bfloat16)

time: 196 us -> 213 us (1.087)
  matrix products: 25.7 us -> 34.3 us
  waiting for transfers between devices: 109 us -> 115 us
  starting transfers between devices: 28.3 us -> 32.4 us
  local copies, waits for them, and re-layouts: 21.1 us -> 17.6 us
    all_to_all x1 -> x2, waiting for transfers between devices: 0.01 us -> 24.5 us  [per_device(): lax.all_to_all(back, 'expert', split_axis=0, concat_axis=0, tiled=True)]
    ppermute x2, waiting for transfers between devices: 72.5 us -> 54.6 us  [partner(): return lax.ppermute(value, axis, pairs)]
    dot_general x17 -> x24, matrix products: 24.6 us -> 32.1 us  [the longest x4 5.41 us: weight_part(): lax.dot_general(rows_in, gate_grad[:, lo:hi], contract_rows, preferred_el...]
    all_to_all x1 -> x2, starting transfers between devices: 7.91 us -> 12 us  [per_device(): lax.all_to_all(back, 'expert', split_axis=0, concat_axis=0, tiled=True)]
    unnamed x50 -> x64, local copies, waits for them, and re-layouts: 8.04 us -> 5.01 us
    another operation x3, other arithmetic: 1.08 us -> 3.66 us  [the longest x1 2.75 us: per_device(): jnp.stack([peer_g.astype(jnp.bfloat16), peer_u.astype(jnp.bfloat16), peer...]
  transfers between devices with their start and end apart: 5 -> 6, of which waited for: 3 -> 5; matrix products, arithmetic and copies ran while one was open for 11% -> 14% of each run, Pallas kernels for 0% -> 0%
where the time goes in v3:
time: 213 us; the launch traced here: 212 us
  waiting for transfers between devices  115 us (54%)
  matrix products  34.3 us (16%)
  starting transfers between devices  32.4 us (15%)
  local copies, waits for them, and re-layouts  17.6 us (8%)
  other arithmetic  11.4 us (5%)
    ppermute x2, waiting for transfers between devices, partner(): return lax.ppermute(value, axis, pairs)  54.6 us
    all_to_all x2, waiting for transfers between devices, per_device(): lax.all_to_all(send, 'expert', split_axis=0, concat_axis=0, tiled=True)  36.3 us
    all_to_all x2, waiting for transfers between devices, per_device(): lax.all_to_all(back, 'expert', split_axis=0, concat_axis=0, tiled=True)  24.5 us
    all_to_all x2, starting transfers between devices, per_device(): lax.all_to_all(send, 'expert', split_axis=0, concat_axis=0, tiled=True)  14.6 us
    all_to_all x2, starting transfers between devices, per_device(): lax.all_to_all(back, 'expert', split_axis=0, concat_axis=0, tiled=True)  12 us
    ppermute x2, starting transfers between devices, partner(): return lax.ppermute(value, axis, pairs)  5.87 us
    dot_general x4, matrix products, weight_part(): lax.dot_general(rows_in, gate_grad[:, lo:hi], contract_rows, preferred_el...  5.41 us
    unnamed x64, local copies, waits for them, and re-layouts  5.01 us
  transfers between devices with their start and end apart: 6, of which 5 were waited for; matrix products, arithmetic and copies ran while one was open for 14% of the time, Pallas kernels for 0%

profile of v3, /device:TPU:1, one launch (start us, length us, event | category | flops | bytes accessed | tf_op | source)
XLA Modules:
  0.0 212.2 jit_solution(8852513496212930868)
XLA Ops:
  0.7 0.8 copy.17
  1.8 0.9 reduce-window.6
  2.7 0.2 slice_reduce_fusion
  3.3 0.2 fusion.10
  3.5 0.4 copy.22
  3.9 0.7 fusion.82
  4.9 0.2 select_reduce_fusion
  5.3 1.6 fusion.33
  7.2 1.2 pad_maximum_fusion
  8.5 10.5 %all-to-all-start = ((bf16[16,24,2048]{2,1,0:T(8,128)(2,1)}), bf16[16,24,2048]{2,1,0:T(8,128)(2,1)S(1)}, u32[]{:S(2)}, u32[]{:S(2)}) async-start(bf16[16,24,2048]{2,1,0:T(8,128)(2,1)} %bitcast.6), calls=%async_computation | async-start | bytes 3145728 | tf_op jit(solution)/shard_map/all_to_all | solution.py:104
  19.0 0.6 fusion.32
  19.9 1.3 pad_maximum_fusion.2
  21.2 36.3 %all-to-all-done = bf16[16,24,2048]{2,1,0:T(8,128)(2,1)S(1)} async-done(((bf16[16,24,2048]{2,1,0:T(8,128)(2,1)}), bf16[16,24,2048]{2,1,0:T(8,128)(2,1)S(1)}, u32[]{:S(2)}, u32[]{:S(2)}) %all-to-all-start) | async-done | bytes 1572896 | tf_op jit(solution)/shard_map/all_to_all | solution.py:104
  57.5 4.1 %all-to-all-start.2 = ((bf16[16,24,2048]{2,1,0:T(8,128)(2,1)}), bf16[16,24,2048]{2,1,0:T(8,128)(2,1)S(1)}, u32[]{:S(2)}, u32[]{:S(2)}) async-start(bf16[16,24,2048]{2,1,0:T(8,128)(2,1)} %bitcast.112), calls=%async_computation.2 | async-start | bytes 3145728 | tf_op jit(solution)/shard_map/all_to_all | solution.py:104
  61.7 2.1 %stack_reshape_squeeze.3 = bf16[1,1024,256]{2,1,0:T(8,128)(2,1)} reshape(bf16[1,1,256,1024]{3,2,1,0:T(8,128)(2,1)} %param.13) | data formatting | bytes 1048576 | tf_op jit(solution)/shard_map/stack;reshape;squeeze | solution.py:79
  63.8 1.5 pad_maximum_fusion.1
  65.3 2.9 %collective-permute-start = (bf16[3,1024,256]{2,1,0:T(8,128)(2,1)S(1)}, bf16[3,1024,256]{2,1,0:T(8,128)(2,1)S(1)}, u32[]{:S(2)}, u32[]{:S(2)}) collective-permute-start(bf16[3,1024,256]{2,1,0:T(8,128)(2,1)S(1)} %pad_maximum_fusion.1), channel_id=1, source_target_pairs={{0,256},{16,272},{32,288},{48,304},{64,320},{80,336},{96,352},{112... | collective-permute-start | bytes 4718600 | tf_op jit(solution)/shard_map/ppermute | solution.py:15
  68.2 36.4 %collective-permute-done = bf16[3,1024,256]{2,1,0:T(8,128)(2,1)S(1)} collective-permute-done((bf16[3,1024,256]{2,1,0:T(8,128)(2,1)S(1)}, bf16[3,1024,256]{2,1,0:T(8,128)(2,1)S(1)}, u32[]{:S(2)}, u32[]{:S(2)}) %collective-permute-start) | collective-permute-done | bytes 1572896 | tf_op jit(solution)/shard_map/ppermute | solution.py:15
  104.6 1.2 slice_bitcast_fusion.3
  105.8 2.2 %reshape_squeeze.7 = bf16[256,1024]{1,0:T(8,128)(2,1)} reshape(bf16[1,1024,256]{2,1,0:T(8,128)(2,1)} %get-tuple-element.12) | data formatting | bytes 1048576 | tf_op jit(solution)/shard_map/reshape;squeeze | solution.py:83
  107.9 2.7 %fusion.54 = f32[384,512]{1,0:T(8,128)} fusion(bf16[384,2048]{1,0:T(8,128)(2,1)S(1)} %bitcast.103, bf16[1024,256]{1,0:T(8,128)(2,1)} %get-tuple-element.11, bf16[1024,256]{1,0:T(8,128)(2,1)} %bitcast.119), kind=kOutput, calls=%fused_computation.88 | convolution fusion | flops 404750336 | bytes 2621440 | tf_op jit(solution)/shard_map/dot_general | solution.py:33
  110.6 1.9 fusion.38
  112.5 0.6 fusion.20
  113.1 0.6 fusion.19
  113.8 0.4 copy-done
  114.2 0.2 copy-done.2
  114.3 0.3 copy-done.30
  114.6 1.7 multiply_convert_fusion.2
  116.3 0.7 copy-done.27
  117.1 0.5 fusion.26
  117.5 1.6 multiply_convert_fusion.1
  119.1 0.8 copy-done.24
  119.9 1.3 fusion.4
  121.2 2.1 %stack_reshape.3 = bf16[1,1024,256]{2,1,0:T(8,128)(2,1)} reshape(bf16[256,1024]{1,0:T(8,128)(2,1)} %fusion.4) | data formatting | bytes 1048576 | tf_op jit(solution)/shard_map/stack;reshape | solution.py:130
  123.3 2.0 fusion.78
  125.3 1.5 add_convert_fusion
  126.9 7.8 %all-to-all-start.3 = ((bf16[16,24,1024]{2,1,0:T(8,128)(2,1)}), bf16[16,24,1024]{2,1,0:T(8,128)(2,1)}, u32[]{:S(2)}, u32[]{:S(2)}) async-start(bf16[16,24,1024]{2,1,0:T(8,128)(2,1)} %bitcast.124), calls=%async_computation.3 | async-start | bytes 1572864 | tf_op jit(solution)/shard_map/all_to_all | solution.py:120
  134.7 1.4 fusion.50
  136.1 1.3 fusion.8
  137.4 0.5 fusion.48
  137.8 0.5 copy-done.12
  138.4 1.3 fusion.7
  139.6 0.6 fusion.79
  140.3 0.4 copy-done.5
  140.9 1.5 add_convert_fusion.1
  142.4 15.0 %all-to-all-done.3 = bf16[16,24,1024]{2,1,0:T(8,128)(2,1)} async-done(((bf16[16,24,1024]{2,1,0:T(8,128)(2,1)}), bf16[16,24,1024]{2,1,0:T(8,128)(2,1)}, u32[]{:S(2)}, u32[]{:S(2)}) %all-to-all-start.3) | async-done | bytes 786464 | tf_op jit(solution)/shard_map/all_to_all | solution.py:120
  157.5 4.2 %all-to-all-start.1 = ((bf16[16,24,1024]{2,1,0:T(8,128)(2,1)}), bf16[16,24,1024]{2,1,0:T(8,128)(2,1)}, u32[]{:S(2)}, u32[]{:S(2)}) async-start(bf16[16,24,1024]{2,1,0:T(8,128)(2,1)} %bitcast.123), calls=%async_computation.1 | async-start | bytes 1572864 | tf_op jit(solution)/shard_map/all_to_all | solution.py:120
  161.7 2.8 %pad_maximum_fusion.3 = bf16[3,1024,256]{2,1,0:T(8,128)(2,1)} fusion(bf16[1,1024,256]{2,1,0:T(8,128)(2,1)} %stack_reshape.3, bf16[1,1024,256]{2,1,0:T(8,128)(2,1)} %fusion.7, bf16[1,1024,256]{2,1,0:T(8,128)(2,1)} %fusion.8), kind=kLoop, calls=%fused_computation.9 | loop fusion | flops 1572864 | bytes 3145728 | tf_op jit(solution)/shard_map/stack | solution.py:130
  164.4 3.0 %collective-permute-start.1 = (bf16[3,1024,256]{2,1,0:T(8,128)(2,1)}, bf16[3,1024,256]{2,1,0:T(8,128)(2,1)}, u32[]{:S(2)}, u32[]{:S(2)}) collective-permute-start(bf16[3,1024,256]{2,1,0:T(8,128)(2,1)} %pad_maximum_fusion.3), channel_id=1, source_target_pairs={{0,256},{16,272},{32,288},{48,304},{64,320},{80,336},{96,352},{112... | collective-permute-start | bytes 4718600 | tf_op jit(solution)/shard_map/ppermute | solution.py:15
  167.5 0.5 fusion.24
  168.0 1.5 fusion.46
  169.5 1.4 fusion.52
  170.9 1.4 convolution_add_fusion
  172.3 1.5 convolution_bitcast_fusion
  173.9 9.4 %all-to-all-done.1 = bf16[16,24,1024]{2,1,0:T(8,128)(2,1)} async-done(((bf16[16,24,1024]{2,1,0:T(8,128)(2,1)}), bf16[16,24,1024]{2,1,0:T(8,128)(2,1)}, u32[]{:S(2)}, u32[]{:S(2)}) %all-to-all-start.1) | async-done | bytes 786464 | tf_op jit(solution)/shard_map/all_to_all | solution.py:120
  183.3 2.3 %fusion.9 = bf16[1,192,1024]{2,1,0:T(8,128)(2,1)} fusion(f32[192,1024]{1,0:T(8,128)S(1)} %convolution_bitcast_fusion, bf16[16,24,1024]{2,1,0:T(8,128)(2,1)} %all-to-all-done.1, pred[16,48,192]{2,1,0:T(8,128)(4,1)S(1)} %bitcast.131), kind=kOutput, calls=%fused_computation.27 | convolution fusion | flops 151388160 | bytes 2064384 | tf_op jit(solution)/shard_map/dot_general | solution.py:123
  185.6 18.3 %collective-permute-done.1 = bf16[3,1024,256]{2,1,0:T(8,128)(2,1)} collective-permute-done((bf16[3,1024,256]{2,1,0:T(8,128)(2,1)}, bf16[3,1024,256]{2,1,0:T(8,128)(2,1)}, u32[]{:S(2)}, u32[]{:S(2)}) %collective-permute-start.1) | collective-permute-done | bytes 1572896 | tf_op jit(solution)/shard_map/ppermute | solution.py:15
  203.9 1.1 slice.160
  205.0 1.3 reshape_squeeze.8
  206.3 1.8 convert_element_type.80
  208.1 1.3 fusion.31
  209.4 1.3 fusion.30
  210.7 0.4 copy-done.11
  211.2 1.0 fusion.29
  (74 shorter events, 2.1 us)
Async XLA Ops:
  0.6 4.0 %copy-start.29 = (f32[1,192,2]{1,2,0:T(2,128)S(1)}, f32[1,192,2]{1,2,0:T(2,128)}, u32[]{:S(2)}) copy-start(f32[1,192,2]{1,2,0:T(2,128)} %param.10) | copy-start | bytes 4612
  0.6 4.7 %copy-start.18 = (bf16[1,192,1024]{2,1,0:T(8,128)(2,1)S(1)}, bf16[1,192,1024]{2,1,0:T(8,128)(2,1)}, u32[]{:S(2)}) copy-start(bf16[1,192,1024]{2,1,0:T(8,128)(2,1)} %param.8) | copy-start | bytes 1179652
  3.8 1.5 copy-start.20
  8.5 10.6 %copy-start.19 = (bf16[1,192,1024]{2,1,0:T(8,128)(2,1)S(1)}, bf16[1,192,1024]{2,1,0:T(8,128)(2,1)}, u32[]{:S(2)}) copy-start(bf16[1,192,1024]{2,1,0:T(8,128)(2,1)} %param.7) | copy-start | bytes 1179652
  8.5 10.6 %copy-start.26 = (pred[16,24,192]{2,1,0:T(8,128)(4,1)S(1)}, pred[16,24,192]{2,1,0:T(8,128)(4,1)}, u32[]{:S(2)}) copy-start(pred[16,24,192]{2,1,0:T(8,128)(4,1)} %get-tuple-element.14) | copy-start | bytes 221188
  8.5 49.0 %all-to-all-start = ((bf16[16,24,2048]{2,1,0:T(8,128)(2,1)}), bf16[16,24,2048]{2,1,0:T(8,128)(2,1)S(1)}, u32[]{:S(2)}, u32[]{:S(2)}) async-start(bf16[16,24,2048]{2,1,0:T(8,128)(2,1)} %bitcast.6), calls=%async_computation | async-start | bytes 3145728 | tf_op jit(solution)/shard_map/all_to_all | solution.py:104
  57.5 53.1 %all-to-all-start.2 = ((bf16[16,24,2048]{2,1,0:T(8,128)(2,1)}), bf16[16,24,2048]{2,1,0:T(8,128)(2,1)S(1)}, u32[]{:S(2)}, u32[]{:S(2)}) async-start(bf16[16,24,2048]{2,1,0:T(8,128)(2,1)} %bitcast.112), calls=%async_computation.2 | async-start | bytes 3145728 | tf_op jit(solution)/shard_map/all_to_all | solution.py:104
  65.3 39.2 %collective-permute-start = (bf16[3,1024,256]{2,1,0:T(8,128)(2,1)S(1)}, bf16[3,1024,256]{2,1,0:T(8,128)(2,1)S(1)}, u32[]{:S(2)}, u32[]{:S(2)}) collective-permute-start(bf16[3,1024,256]{2,1,0:T(8,128)(2,1)S(1)} %pad_maximum_fusion.1), channel_id=1, source_target_pairs={{0,256},{16,272},{32,288},{48,304},{64,320},{80,336},{96,352},{112... | collective-permute-start | bytes 4718600 | tf_op jit(solution)/shard_map/ppermute | solution.py:15
  110.6 1.9 copy-start.22
  110.6 1.9 copy-start.23
  113.1 1.0 copy-start
  113.1 1.2 copy-start.2
  113.1 1.4 copy-start.30
  116.3 0.7 copy-start.27
  119.1 0.8 copy-start.24
  123.3 2.0 copy-start.4
  123.3 2.0 copy-start.6
  126.9 30.6 %all-to-all-start.3 = ((bf16[16,24,1024]{2,1,0:T(8,128)(2,1)}), bf16[16,24,1024]{2,1,0:T(8,128)(2,1)}, u32[]{:S(2)}, u32[]{:S(2)}) async-start(bf16[16,24,1024]{2,1,0:T(8,128)(2,1)} %bitcast.124), calls=%async_computation.3 | async-start | bytes 1572864 | tf_op jit(solution)/shard_map/all_to_all | solution.py:120
  136.1 1.3 copy-start.16
  137.4 1.0 copy-start.12
  138.3 1.3 copy-start.1
  138.4 1.3 copy-start.3
  139.6 1.0 copy-start.5
  139.6 1.2 copy-start.7
  139.6 1.3 copy-start.14
  157.5 25.8 %all-to-all-start.1 = ((bf16[16,24,1024]{2,1,0:T(8,128)(2,1)}), bf16[16,24,1024]{2,1,0:T(8,128)(2,1)}, u32[]{:S(2)}, u32[]{:S(2)}) async-start(bf16[16,24,1024]{2,1,0:T(8,128)(2,1)} %bitcast.123), calls=%async_computation.1 | async-start | bytes 1572864 | tf_op jit(solution)/shard_map/all_to_all | solution.py:120
  161.7 5.8 %copy-start.28 = (bf16[384,512]{1,0:T(8,128)(2,1)S(1)}, bf16[384,512]{1,0:T(8,128)(2,1)}, u32[]{:S(2)}) copy-start(bf16[384,512]{1,0:T(8,128)(2,1)} %copy-done.27) | copy-start | bytes 1179652
  164.4 3.5 %copy-start.17 = (bf16[384,512]{1,0:T(8,128)(2,1)S(1)}, bf16[384,512]{1,0:T(8,128)(2,1)}, u32[]{:S(2)}) copy-start(bf16[384,512]{1,0:T(8,128)(2,1)} %get-tuple-element.9) | copy-start | bytes 1179652
  164.4 5.0 %copy-start.15 = (bf16[384,512]{1,0:T(8,128)(2,1)S(1)}, bf16[384,512]{1,0:T(8,128)(2,1)}, u32[]{:S(2)}) copy-start(bf16[384,512]{1,0:T(8,128)(2,1)} %get-tuple-element.8) | copy-start | bytes 1179652
  164.4 39.5 %collective-permute-start.1 = (bf16[3,1024,256]{2,1,0:T(8,128)(2,1)}, bf16[3,1024,256]{2,1,0:T(8,128)(2,1)}, u32[]{:S(2)}, u32[]{:S(2)}) collective-permute-start(bf16[3,1024,256]{2,1,0:T(8,128)(2,1)} %pad_maximum_fusion.3), channel_id=1, source_target_pairs={{0,256},{16,272},{32,288},{48,304},{64,320},{80,336},{96,352},{112... | collective-permute-start | bytes 4718600 | tf_op jit(solution)/shard_map/ppermute | solution.py:15
  167.9 3.0 %copy-start.25 = (bf16[384,512]{1,0:T(8,128)(2,1)S(1)}, bf16[384,512]{1,0:T(8,128)(2,1)}, u32[]{:S(2)}) copy-start(bf16[384,512]{1,0:T(8,128)(2,1)} %copy-done.24) | copy-start | bytes 1179652
  170.9 1.4 copy-start.21
  206.3 1.8 copy-start.10
  206.3 1.8 copy-start.13
  208.1 1.3 copy-start.8
  209.4 1.3 copy-start.9
  209.4 1.7 copy-start.11

commit v4 on v1

--- a/solution.py
+++ b/solution.py
@@ -4,8 +4,6 @@
 import jax.numpy as jnp
 from jax import lax
 from jax.sharding import PartitionSpec as P
-
-CHUNKS = 2
 
 
 def partner(value, axis, bit):
@@ -62,6 +60,7 @@
     cap = 2 * topk * tok // experts
     scale = 1.0 / math.sqrt(2 * topk * tok)
     pair_bit = lax.axis_size("section").bit_length() - 2
+    rows = experts * cap
 
     own_gate = w_gate[0, 0]
     own_up = w_up[0, 0]
@@ -71,56 +70,39 @@
 
     hit = dispatch_matrix(ids, cap, experts)
     pair_gate = jnp.sum(jnp.where(hit, gates.reshape(tok * topk)[None, :], 0.0), axis=1)
-    token_hit = hit.reshape(experts * cap, tok, topk).any(axis=2).astype(jnp.bfloat16)
+    sel = hit.reshape(rows, tok, topk).any(axis=2).astype(jnp.bfloat16)
     both = jnp.concatenate([inputs, grads], axis=1)
+    picked = jnp.dot(sel, both, preferred_element_type=jnp.float32)
+    slot_in = picked[:, :width].astype(jnp.bfloat16)
+    slot_grad = (picked[:, width:] * pair_gate[:, None]).astype(jnp.bfloat16)
+    send = jnp.concatenate([slot_in, slot_grad], axis=1).reshape(experts, cap, 2 * width)
+    recv = lax.all_to_all(send, "expert", split_axis=0, concat_axis=0, tiled=True)
+    sel_t = lax.optimization_barrier(
+        jnp.transpose(hit.reshape(rows, tok, topk).any(axis=2)).astype(jnp.bfloat16)
+    )
+    recv = recv.reshape(rows, 2 * width)
 
-    token_hit = token_hit.reshape(experts, cap, tok)
-    pair_gate = pair_gate.reshape(experts, cap)
-    step = cap // CHUNKS
-    chunk_rows = experts * step
-
-    full_gate = full_up = full_down = None
-    token_acc = jnp.zeros((tok, width), jnp.float32)
-    acc_g = acc_u = acc_d = None
-    for c in range(CHUNKS):
-        sel = token_hit[:, c * step:(c + 1) * step, :].reshape(chunk_rows, tok)
-        sgate = pair_gate[:, c * step:(c + 1) * step].reshape(chunk_rows, 1)
-        picked = jnp.dot(sel, both, preferred_element_type=jnp.float32)
-        slot_in = picked[:, :width].astype(jnp.bfloat16)
-        slot_grad = (picked[:, width:] * sgate).astype(jnp.bfloat16)
-        send = jnp.concatenate([slot_in, slot_grad], axis=1).reshape(experts, step, 2 * width)
-        recv = lax.all_to_all(send, "expert", split_axis=0, concat_axis=0, tiled=True)
-        recv = recv.reshape(chunk_rows, 2 * width)
-        if full_gate is None:
-            full_gate = jnp.concatenate([own_gate, other_gate], axis=1)
-            full_up = jnp.concatenate([own_up, other_up], axis=1)
-            full_down = jnp.concatenate([own_down, other_down], axis=0)
-        pair_grad, grad_g, grad_u, grad_d = expert_grads(
-            recv[:, :width], recv[:, width:], full_gate, full_up, full_down
-        )
-        if acc_g is None:
-            acc_g, acc_u, acc_d = grad_g, grad_u, grad_d
-        else:
-            acc_g, acc_u, acc_d = acc_g + grad_g, acc_u + grad_u, acc_d + grad_d
-        back = pair_grad.astype(jnp.bfloat16).reshape(experts, step, width)
-        home = lax.all_to_all(back, "expert", split_axis=0, concat_axis=0, tiled=True)
-        home = home.reshape(chunk_rows, width)
-        token_acc = token_acc + lax.dot_general(
-            sel, home, (((0,), (0,)), ((), ())), preferred_element_type=jnp.float32
-        )
-
+    full_gate = jnp.concatenate([own_gate, other_gate], axis=1)
+    full_up = jnp.concatenate([own_up, other_up], axis=1)
+    full_down = jnp.concatenate([own_down, other_down], axis=0)
+    pair_grad, grad_g, grad_u, grad_d = expert_grads(
+        recv[:, :width], recv[:, width:], full_gate, full_up, full_down
+    )
+    back = pair_grad.astype(jnp.bfloat16).reshape(experts, cap, width)
+    home = lax.all_to_all(back, "expert", split_axis=0, concat_axis=0, tiled=True)
     peer_g, peer_u, peer_d = partner(
         (
-            acc_g[:, half:].astype(jnp.bfloat16),
-            acc_u[:, half:].astype(jnp.bfloat16),
-            acc_d[half:, :].astype(jnp.bfloat16),
+            grad_g[:, half:].astype(jnp.bfloat16),
+            grad_u[:, half:].astype(jnp.bfloat16),
+            grad_d[half:, :].astype(jnp.bfloat16),
         ),
         "section",
         pair_bit,
     )
-    mine_g = acc_g[:, :half] + peer_g.astype(jnp.float32)
-    mine_u = acc_u[:, :half] + peer_u.astype(jnp.float32)
-    mine_d = acc_d[:half, :] + peer_d.astype(jnp.float32)
+    token_acc = jnp.dot(sel_t, home.reshape(rows, width), preferred_element_type=jnp.float32)
+    mine_g = grad_g[:, :half] + peer_g.astype(jnp.float32)
+    mine_u = grad_u[:, :half] + peer_u.astype(jnp.float32)
+    mine_d = grad_d[:half, :] + peer_d.astype(jnp.float32)
     token_grad = token_acc.astype(jnp.bfloat16)
     out_g = (mine_g * scale).astype(jnp.bfloat16)
     out_u = (mine_u * scale).astype(jnp.bfloat16)
@@ -144,6 +126,4 @@
         P("section", "expert", None, None),
         P("section", "expert", None, None),
     )
-    return jax.shard_map(
-        per_device, mesh=mesh, in_specs=in_specs, out_specs=out_specs, check_vma=False
-    )
+    return jax.shard_map(per_device, mesh=mesh, in_specs=in_specs, out_specs=out_specs, check_vma=False)

time: 180 us -> 156 us (0.87)
  local copies, waits for them, and re-layouts: 10.5 us -> 2.94 us
  starting transfers between devices: 42.8 us -> 35.3 us
  waiting for transfers between devices: 90.9 us -> 86.7 us
  matrix products: 25.6 us -> 23.2 us
    all_to_all x2 -> x1, waiting for transfers between devices: 14.5 us -> 0.01 us  [per_device(): lax.all_to_all(back, 'expert', split_axis=0, concat_axis=0, tiled=True)]
    all_to_all x2 -> x1, waiting for transfers between devices: 42.8 us -> 54 us  [per_device(): lax.all_to_all(send, 'expert', split_axis=0, concat_axis=0, tiled=True)]
    unnamed x54 -> x24, local copies, waits for them, and re-layouts: 7.66 us -> 1.64 us
    all_to_all x2 -> x1, starting transfers between devices: 14.5 us -> 10.4 us  [per_device(): lax.all_to_all(send, 'expert', split_axis=0, concat_axis=0, tiled=True)]
    all_to_all x2 -> x1, starting transfers between devices: 8.78 us -> 5.45 us  [per_device(): lax.all_to_all(back, 'expert', split_axis=0, concat_axis=0, tiled=True)]
    dot_general x2 -> x1, matrix products: 3.85 us -> 1.23 us  [per_device(): jnp.dot(sel_t, home.reshape(rows, width), preferred_element_type=jnp.floa...]
    dot_general x2 -> x1, matrix products: 4.45 us -> 2.94 us  [expert_grads(): lax.dot_general(rows_grad, down_w, contract_last, preferred_element_type=...]
    dot_general x2 -> x1, matrix products: 3.65 us -> 3.03 us  [expert_grads(): gate_pre = jnp.dot(rows_in, gate_w, preferred_element_type=jnp.float32)]
  transfers between devices with their start and end apart: 10 -> 8, of which waited for: 7 -> 5; matrix products, arithmetic and copies ran while one was open for 16% -> 9% of each run, Pallas kernels for 0% -> 0%
where the time goes in v4:
time: 156 us
  waiting for transfers between devices  86.7 us (56%)
  starting transfers between devices  35.3 us (23%)
  matrix products  23.2 us (15%)
  other arithmetic  6.55 us (4%)
  local copies, waits for them, and re-layouts  2.94 us (2%)
    all_to_all x1, waiting for transfers between devices, per_device(): lax.all_to_all(send, 'expert', split_axis=0, concat_axis=0, tiled=True)  54 us
    ppermute x6, waiting for transfers between devices, partner(): return lax.ppermute(value, axis, pairs)  32.7 us
    ppermute x6, starting transfers between devices, partner(): return lax.ppermute(value, axis, pairs)  19.5 us
    all_to_all x1, starting transfers between devices, per_device(): lax.all_to_all(send, 'expert', split_axis=0, concat_axis=0, tiled=True)  10.4 us
    all_to_all x1, starting transfers between devices, per_device(): lax.all_to_all(back, 'expert', split_axis=0, concat_axis=0, tiled=True)  5.45 us
    dot_general x1, matrix products, expert_grads(): lax.dot_general(act, rows_grad, contract_rows, preferred_element_type=jnp...  3.57 us
    dot_general x1, matrix products, expert_grads(): lax.dot_general(gate_grad, gate_w, contract_last, preferred_element_type=...  3.21 us
  transfers between devices with their start and end apart: 8, of which 5 were waited for; matrix products, arithmetic and copies ran while one was open for 9% of the time, Pallas kernels for 0%

profile of v4, /device:TPU:1, one launch (start us, length us, event | category | flops | bytes accessed | tf_op | source)
XLA Modules:
  0.0 155.7 jit_solution(13751795921424942265)
XLA Ops:
  0.6 0.8 copy.17
  1.4 0.1 eq.49
  1.6 0.1 eq.45
  1.7 0.9 reduce-window.6
  2.6 0.2 slice_reduce_fusion
  2.9 0.1 fusion.36
  3.0 0.1 reduce_sum.21
  3.1 0.1 copy.21
  3.2 0.2 fusion.7
  3.4 0.8 copy.22
  4.2 0.1 broadcast_in_dim.30
  4.4 2.1 %fusion.25 = f32[768,2048]{1,0:T(8,128)S(1)} fusion(pred[768,192]{0,1:T(8,128)(4,1)S(1)} %fusion.7, bf16[192,1024]{1,0:T(8,128)(2,1)} %bitcast.61, bf16[192,1024]{1,0:T(8,128)(2,1)} %bitcast.62), kind=kOutput, calls=%fused_computation.45 | convolution fusion | flops 605552640 | bytes 7225344 | tf_op jit(solution)/shard_map/dot_general | solution.py:75
  6.5 0.2 slice.104
  6.8 0.2 select_reduce_fusion
  7.0 0.2 fusion
  7.2 1.9 %pad_maximum_fusion = bf16[768,2048]{1,0:T(8,128)(2,1)} fusion(bf16[768,1024]{1,0:T(8,128)(2,1)S(1)} %fusion, bf16[768,1024]{1,0:T(8,128)(2,1)S(1)} %slice.104), kind=kLoop, calls=%fused_computation.3 | loop fusion | flops 6291456 | bytes 6291456 | tf_op jit(solution)/shard_map/concatenate | solution.py:78
  9.1 10.4 %all-to-all-start = ((bf16[16,48,2048]{2,1,0:T(8,128)(2,1)}), bf16[16,48,2048]{2,1,0:T(8,128)(2,1)S(1)}, u32[]{:S(2)}, u32[]{:S(2)}) async-start(bf16[16,48,2048]{2,1,0:T(8,128)(2,1)} %bitcast.5), calls=%async_computation | async-start | bytes 6291456 | tf_op jit(solution)/shard_map/all_to_all | solution.py:79
  19.5 2.9 %collective-permute-start.2 = (bf16[1024,256]{1,0:T(8,128)(2,1)}, bf16[1024,256]{1,0:T(8,128)(2,1)}, u32[]{:S(2)}, u32[]{:S(2)}) collective-permute-start(bf16[1024,256]{1,0:T(8,128)(2,1)} %bitcast.58), channel_id=1, source_target_pairs={{0,256},{16,272},{32,288},{48,304},{64,320},{80,336},{96,352},{112... | collective-permute-start | bytes 1572872 | tf_op jit(solution)/shard_map/ppermute | solution.py:12
  22.4 3.9 %collective-permute-start.1 = (bf16[1024,256]{1,0:T(8,128)(2,1)}, bf16[1024,256]{1,0:T(8,128)(2,1)}, u32[]{:S(2)}, u32[]{:S(2)}) collective-permute-start(bf16[1024,256]{1,0:T(8,128)(2,1)} %bitcast.55), channel_id=1, source_target_pairs={{0,256},{16,272},{32,288},{48,304},{64,320},{80,336},{96,352},{112... | collective-permute-start | bytes 1572872 | tf_op jit(solution)/shard_map/ppermute | solution.py:12
  26.3 2.9 %collective-permute-start = (bf16[256,1024]{1,0:T(8,128)(2,1)}, bf16[256,1024]{1,0:T(8,128)(2,1)}, u32[]{:S(2)}, u32[]{:S(2)}) collective-permute-start(bf16[256,1024]{1,0:T(8,128)(2,1)} %bitcast.64), channel_id=1, source_target_pairs={{0,256},{16,272},{32,288},{48,304},{64,320},{80,336},{96,352},{112... | collective-permute-start | bytes 1572872 | tf_op jit(solution)/shard_map/ppermute | solution.py:12
  29.2 7.3 %collective-permute-done.2 = bf16[1024,256]{1,0:T(8,128)(2,1)} collective-permute-done((bf16[1024,256]{1,0:T(8,128)(2,1)}, bf16[1024,256]{1,0:T(8,128)(2,1)}, u32[]{:S(2)}, u32[]{:S(2)}) %collective-permute-start.2) | collective-permute-done | bytes 524320 | tf_op jit(solution)/shard_map/ppermute | solution.py:12
  36.5 54.0 %all-to-all-done = bf16[16,48,2048]{2,1,0:T(8,128)(2,1)S(1)} async-done(((bf16[16,48,2048]{2,1,0:T(8,128)(2,1)}), bf16[16,48,2048]{2,1,0:T(8,128)(2,1)S(1)}, u32[]{:S(2)}, u32[]{:S(2)}) %all-to-all-start) | async-done | bytes 3145760 | tf_op jit(solution)/shard_map/all_to_all | solution.py:79
  90.5 3.0 %fusion.21 = f32[768,512]{1,0:T(8,128)S(1)} fusion(bf16[768,2048]{1,0:T(8,128)(2,1)S(1)} %bitcast.49, bf16[1024,256]{1,0:T(8,128)(2,1)} %collective-permute-done.2, bf16[1024,256]{1,0:T(8,128)(2,1)} %bitcast.59), kind=kOutput, calls=%fused_computation.41 | convolution fusion | flops 807403520 | bytes 4194304 | tf_op jit(solution)/shard_map/dot_general | solution.py:30
  93.5 0.0 copy-start.9
  93.5 0.0 copy-start.8
  93.5 0.0 collective-permute-done.1
  93.6 0.0 copy-done.6
  93.6 2.6 %fusion.23 = f32[768,512]{1,0:T(8,128)S(1)} fusion(bf16[768,2048]{1,0:T(8,128)(2,1)S(1)} %bitcast.50, bf16[1024,256]{1,0:T(8,128)(2,1)} %collective-permute-done.1, bf16[1024,256]{1,0:T(8,128)(2,1)S(1)} %bitcast.56), kind=kOutput, calls=%fused_computation.43 | convolution fusion | flops 807403520 | bytes 4194304 | tf_op jit(solution)/shard_map/dot_general | solution.py:31
  96.1 0.0 copy-start.10
  96.1 0.0 collective-permute-done
  96.2 0.0 copy-done
  96.2 0.0 copy-done.9
  96.2 0.0 copy-done.8
  96.2 2.9 %multiply_convert_fusion.2 = (bf16[768,512]{1,0:T(8,128)(2,1)S(1)}, bf16[768,512]{1,0:T(8,128)(2,1)S(1)}) fusion(f32[768,512]{1,0:T(8,128)S(1)} %fusion.21, f32[768,512]{1,0:T(8,128)S(1)} %fusion.23, bf16[256,1024]{1,0:T(8,128)(2,1)} %collective-permute-done, bf16[256,1024]{1,0:T(8,128)(2,1)S(1)} %bitcast.65, bf16[768,2048]{1,0:T(8,128)(2,1)S(1)} %bitcast.51), kind=kOutput, calls=%fused_computation.7 | convolution fusion | flops 812515328 | bytes 7340032 | tf_op jit(solution)/shard_map/dot_general | solution.py:35
  99.1 0.0 copy-done.10
  99.1 0.0 copy-start.2
  99.2 0.0 copy-start.4
  99.2 0.0 copy-start.7
  99.2 2.5 %fusion.29 = f32[768,1024]{1,0:T(8,128)S(1)} fusion(bf16[768,512]{1,0:T(8,128)(2,1)S(1)} %get-tuple-element.5, bf16[1024,256]{1,0:T(8,128)(2,1)} %collective-permute-done.1, bf16[1024,256]{1,0:T(8,128)(2,1)S(1)} %bitcast.57), kind=kOutput, calls=%fused_computation.49 | convolution fusion | flops 807403520 | bytes 4980736 | tf_op jit(solution)/shard_map/dot_general | solution.py:43
  101.7 0.0 copy-done.2
  101.7 0.0 copy-done.4
  101.7 0.0 copy-done.7
  101.7 3.2 %add_convert_fusion = bf16[768,1024]{1,0:T(8,128)(2,1)} fusion(f32[768,1024]{1,0:T(8,128)S(1)} %fusion.29, bf16[768,512]{1,0:T(8,128)(2,1)S(1)} %get-tuple-element.4, bf16[1024,256]{1,0:T(8,128)(2,1)} %collective-permute-done.2, bf16[1024,256]{1,0:T(8,128)(2,1)S(1)} %bitcast.60), kind=kOutput, calls=%fused_computation.4 | convolution fusion | flops 808976384 | bytes 6553600 | tf_op jit(solution)/shard_map/dot_general | solution.py:40
  104.9 5.4 %all-to-all-start.1 = ((bf16[16,48,1024]{2,1,0:T(8,128)(2,1)}), bf16[16,48,1024]{2,1,0:T(8,128)(2,1)S(1)}, u32[]{:S(2)}, u32[]{:S(2)}) async-start(bf16[16,48,1024]{2,1,0:T(8,128)(2,1)} %bitcast.10), calls=%async_computation.1 | async-start | bytes 3145728 | tf_op jit(solution)/shard_map/all_to_all | solution.py:92
  110.4 3.6 %fusion.2 = f32[512,1024]{1,0:T(8,128)S(1)} fusion(bf16[768,2048]{1,0:T(8,128)(2,1)} %bitcast.52, f32[768,512]{1,0:T(8,128)} %copy-done.10, f32[768,512]{1,0:T(8,128)} %copy-done.9), kind=kOutput, calls=%fused_computation.10 | convolution fusion | flops 807665664 | bytes 6815744 | tf_op jit(solution)/shard_map/dot_general | solution.py:48
  114.0 0.1 slice.105
  114.1 3.0 %collective-permute-start.5 = (bf16[256,1024]{1,0:T(8,128)(2,1)S(1)}, bf16[256,1024]{1,0:T(8,128)(2,1)S(1)}, u32[]{:S(2)}, u32[]{:S(2)}) collective-permute-start(bf16[256,1024]{1,0:T(8,128)(2,1)S(1)} %slice.105), channel_id=1, source_target_pairs={{0,256},{16,272},{32,288},{48,304},{64,320},{80,336},{96,352},{112... | collective-permute-start | bytes 1572872 | tf_op jit(solution)/shard_map/ppermute | solution.py:12
  117.1 0.0 copy-done.1
  117.1 0.0 copy-done.3
  117.1 1.0 fusion.17
  118.1 0.1 slice.106
  118.2 3.9 %collective-permute-start.4 = (bf16[1024,256]{1,0:T(8,128)(2,1)S(1)}, bf16[1024,256]{1,0:T(8,128)(2,1)S(1)}, u32[]{:S(2)}, u32[]{:S(2)}) collective-permute-start(bf16[1024,256]{1,0:T(8,128)(2,1)S(1)} %slice.106), channel_id=1, source_target_pairs={{0,256},{16,272},{32,288},{48,304},{64,320},{80,336},{96,352},{112... | collective-permute-start | bytes 1572872 | tf_op jit(solution)/shard_map/ppermute | solution.py:12
  122.1 0.0 copy-done.5
  122.1 1.0 fusion.19
  123.1 0.1 slice.107
  123.2 2.9 %collective-permute-start.3 = (bf16[1024,256]{1,0:T(8,128)(2,1)S(1)}, bf16[1024,256]{1,0:T(8,128)(2,1)S(1)}, u32[]{:S(2)}, u32[]{:S(2)}) collective-permute-start(bf16[1024,256]{1,0:T(8,128)(2,1)S(1)} %slice.107), channel_id=1, source_target_pairs={{0,256},{16,272},{32,288},{48,304},{64,320},{80,336},{96,352},{112... | collective-permute-start | bytes 1572872 | tf_op jit(solution)/shard_map/ppermute | solution.py:12
  126.1 4.9 %collective-permute-done.5 = bf16[256,1024]{1,0:T(8,128)(2,1)S(1)} collective-permute-done((bf16[256,1024]{1,0:T(8,128)(2,1)S(1)}, bf16[256,1024]{1,0:T(8,128)(2,1)S(1)}, u32[]{:S(2)}, u32[]{:S(2)}) %collective-permute-start.5) | collective-permute-done | bytes 524320 | tf_op jit(solution)/shard_map/ppermute | solution.py:12
  131.0 1.0 fusion.32
  132.0 10.3 %collective-permute-done.4 = bf16[1024,256]{1,0:T(8,128)(2,1)S(1)} collective-permute-done((bf16[1024,256]{1,0:T(8,128)(2,1)S(1)}, bf16[1024,256]{1,0:T(8,128)(2,1)S(1)}, u32[]{:S(2)}, u32[]{:S(2)}) %collective-permute-start.4) | collective-permute-done | bytes 524320 | tf_op jit(solution)/shard_map/ppermute | solution.py:12
  142.2 1.0 fusion.31
  143.2 10.2 %collective-permute-done.3 = bf16[1024,256]{1,0:T(8,128)(2,1)S(1)} collective-permute-done((bf16[1024,256]{1,0:T(8,128)(2,1)S(1)}, bf16[1024,256]{1,0:T(8,128)(2,1)S(1)}, u32[]{:S(2)}, u32[]{:S(2)}) %collective-permute-start.3) | collective-permute-done | bytes 524320 | tf_op jit(solution)/shard_map/ppermute | solution.py:12
  153.5 1.0 fusion.30
  154.4 0.0 all-to-all-done.1
  154.4 1.2 fusion.6
  (10 shorter events, 0.1 us)
Async XLA Ops:
  9.1 81.4 %all-to-all-start = ((bf16[16,48,2048]{2,1,0:T(8,128)(2,1)}), bf16[16,48,2048]{2,1,0:T(8,128)(2,1)S(1)}, u32[]{:S(2)}, u32[]{:S(2)}) async-start(bf16[16,48,2048]{2,1,0:T(8,128)(2,1)} %bitcast.5), calls=%async_computation | async-start | bytes 6291456 | tf_op jit(solution)/shard_map/all_to_all | solution.py:79
  19.5 17.0 %collective-permute-start.2 = (bf16[1024,256]{1,0:T(8,128)(2,1)}, bf16[1024,256]{1,0:T(8,128)(2,1)}, u32[]{:S(2)}, u32[]{:S(2)}) collective-permute-start(bf16[1024,256]{1,0:T(8,128)(2,1)} %bitcast.58), channel_id=1, source_target_pairs={{0,256},{16,272},{32,288},{48,304},{64,320},{80,336},{96,352},{112... | collective-permute-start | bytes 1572872 | tf_op jit(solution)/shard_map/ppermute | solution.py:12
  22.4 71.2 %collective-permute-start.1 = (bf16[1024,256]{1,0:T(8,128)(2,1)}, bf16[1024,256]{1,0:T(8,128)(2,1)}, u32[]{:S(2)}, u32[]{:S(2)}) collective-permute-start(bf16[1024,256]{1,0:T(8,128)(2,1)} %bitcast.55), channel_id=1, source_target_pairs={{0,256},{16,272},{32,288},{48,304},{64,320},{80,336},{96,352},{112... | collective-permute-start | bytes 1572872 | tf_op jit(solution)/shard_map/ppermute | solution.py:12
  26.3 69.9 %collective-permute-start = (bf16[256,1024]{1,0:T(8,128)(2,1)}, bf16[256,1024]{1,0:T(8,128)(2,1)}, u32[]{:S(2)}, u32[]{:S(2)}) collective-permute-start(bf16[256,1024]{1,0:T(8,128)(2,1)} %bitcast.64), channel_id=1, source_target_pairs={{0,256},{16,272},{32,288},{48,304},{64,320},{80,336},{96,352},{112... | collective-permute-start | bytes 1572872 | tf_op jit(solution)/shard_map/ppermute | solution.py:12
  90.5 5.7 %copy-start = (bf16[16,48,2048]{2,1,0:T(8,128)(2,1)}, bf16[16,48,2048]{2,1,0:T(8,128)(2,1)S(1)}, u32[]{:S(2)}) copy-start(bf16[16,48,2048]{2,1,0:T(8,128)(2,1)S(1)} %all-to-all-done) | copy-start | bytes 9437188
  90.5 3.1 %copy-start.6 = (bf16[1,1,1024,256]{3,2,1,0:T(8,128)(2,1)S(1)}, bf16[1,1,1024,256]{3,2,1,0:T(8,128)(2,1)}, u32[]{:S(2)}) copy-start(bf16[1,1,1024,256]{3,2,1,0:T(8,128)(2,1)} %param.12) | copy-start | bytes 1572868
  93.5 2.6 %copy-start.9 = (f32[768,512]{1,0:T(8,128)}, f32[768,512]{1,0:T(8,128)S(1)}, u32[]{:S(2)}) copy-start(f32[768,512]{1,0:T(8,128)S(1)} %fusion.21) | copy-start | bytes 4718596
  93.5 2.6 %copy-start.8 = (bf16[1,1,256,1024]{3,2,1,0:T(8,128)(2,1)S(1)}, bf16[1,1,256,1024]{3,2,1,0:T(8,128)(2,1)}, u32[]{:S(2)}) copy-start(bf16[1,1,256,1024]{3,2,1,0:T(8,128)(2,1)} %param.13) | copy-start | bytes 1572868
  96.1 3.0 %copy-start.10 = (f32[768,512]{1,0:T(8,128)}, f32[768,512]{1,0:T(8,128)S(1)}, u32[]{:S(2)}) copy-start(f32[768,512]{1,0:T(8,128)S(1)} %fusion.23) | copy-start | bytes 4718596
  99.1 2.5 %copy-start.2 = (bf16[768,512]{1,0:T(8,128)(2,1)}, bf16[768,512]{1,0:T(8,128)(2,1)S(1)}, u32[]{:S(2)}) copy-start(bf16[768,512]{1,0:T(8,128)(2,1)S(1)} %get-tuple-element.5) | copy-start | bytes 2359300
  99.2 2.5 %copy-start.4 = (bf16[768,512]{1,0:T(8,128)(2,1)}, bf16[768,512]{1,0:T(8,128)(2,1)S(1)}, u32[]{:S(2)}) copy-start(bf16[768,512]{1,0:T(8,128)(2,1)S(1)} %get-tuple-element.4) | copy-start | bytes 2359300
  99.2 2.5 %copy-start.7 = (bf16[1,1,1024,256]{3,2,1,0:T(8,128)(2,1)S(1)}, bf16[1,1,1024,256]{3,2,1,0:T(8,128)(2,1)}, u32[]{:S(2)}) copy-start(bf16[1,1,1024,256]{3,2,1,0:T(8,128)(2,1)} %param.11) | copy-start | bytes 1572868
  104.9 49.5 %all-to-all-start.1 = ((bf16[16,48,1024]{2,1,0:T(8,128)(2,1)}), bf16[16,48,1024]{2,1,0:T(8,128)(2,1)S(1)}, u32[]{:S(2)}, u32[]{:S(2)}) async-start(bf16[16,48,1024]{2,1,0:T(8,128)(2,1)} %bitcast.10), calls=%async_computation.1 | async-start | bytes 3145728 | tf_op jit(solution)/shard_map/all_to_all | solution.py:92
  110.4 6.7 %copy-start.1 = (bf16[16,48,2048]{2,1,0:T(8,128)(2,1)S(1)}, bf16[16,48,2048]{2,1,0:T(8,128)(2,1)}, u32[]{:S(2)}) copy-start(bf16[16,48,2048]{2,1,0:T(8,128)(2,1)} %copy-done) | copy-start | bytes 9437188
  110.4 6.7 %copy-start.3 = (bf16[768,512]{1,0:T(8,128)(2,1)S(1)}, bf16[768,512]{1,0:T(8,128)(2,1)}, u32[]{:S(2)}) copy-start(bf16[768,512]{1,0:T(8,128)(2,1)} %copy-done.2) | copy-start | bytes 2359300
  114.1 8.1 %copy-start.5 = (bf16[768,512]{1,0:T(8,128)(2,1)S(1)}, bf16[768,512]{1,0:T(8,128)(2,1)}, u32[]{:S(2)}) copy-start(bf16[768,512]{1,0:T(8,128)(2,1)} %copy-done.4) | copy-start | bytes 2359300
  114.1 16.9 %collective-permute-start.5 = (bf16[256,1024]{1,0:T(8,128)(2,1)S(1)}, bf16[256,1024]{1,0:T(8,128)(2,1)S(1)}, u32[]{:S(2)}, u32[]{:S(2)}) collective-permute-start(bf16[256,1024]{1,0:T(8,128)(2,1)S(1)} %slice.105), channel_id=1, source_target_pairs={{0,256},{16,272},{32,288},{48,304},{64,320},{80,336},{96,352},{112... | collective-permute-start | bytes 1572872 | tf_op jit(solution)/shard_map/ppermute | solution.py:12
  118.2 24.0 %collective-permute-start.4 = (bf16[1024,256]{1,0:T(8,128)(2,1)S(1)}, bf16[1024,256]{1,0:T(8,128)(2,1)S(1)}, u32[]{:S(2)}, u32[]{:S(2)}) collective-permute-start(bf16[1024,256]{1,0:T(8,128)(2,1)S(1)} %slice.106), channel_id=1, source_target_pairs={{0,256},{16,272},{32,288},{48,304},{64,320},{80,336},{96,352},{112... | collective-permute-start | bytes 1572872 | tf_op jit(solution)/shard_map/ppermute | solution.py:12
  123.2 30.2 %collective-permute-start.3 = (bf16[1024,256]{1,0:T(8,128)(2,1)S(1)}, bf16[1024,256]{1,0:T(8,128)(2,1)S(1)}, u32[]{:S(2)}, u32[]{:S(2)}) collective-permute-start(bf16[1024,256]{1,0:T(8,128)(2,1)S(1)} %slice.107), channel_id=1, source_target_pairs={{0,256},{16,272},{32,288},{48,304},{64,320},{80,336},{96,352},{112... | collective-permute-start | bytes 1572872 | tf_op jit(solution)/shard_map/ppermute | solution.py:12

commit v5 on v4

--- a/solution.py
+++ b/solution.py
@@ -22,31 +22,6 @@
     slot = flat * cap + rank
     hit = slot[None, :] == jnp.arange(experts * cap, dtype=jnp.int32)[:, None]
     return hit
-
-
-def expert_grads(rows_in, rows_grad, gate_w, up_w, down_w):
-    contract_last = (((1,), (1,)), ((), ()))
-    contract_rows = (((0,), (0,)), ((), ()))
-    gate_pre = jnp.dot(rows_in, gate_w, preferred_element_type=jnp.float32)
-    up_pre = jnp.dot(rows_in, up_w, preferred_element_type=jnp.float32)
-    sigmoid_g = jax.nn.sigmoid(gate_pre)
-    swish_val = gate_pre * sigmoid_g
-    act = (swish_val * up_pre).astype(jnp.bfloat16)
-    act_grad = lax.dot_general(rows_grad, down_w, contract_last, preferred_element_type=jnp.float32)
-    gate_grad = (act_grad * up_pre * sigmoid_g * (1.0 + gate_pre * (1.0 - sigmoid_g))).astype(
-        jnp.bfloat16
-    )
-    up_grad = (act_grad * swish_val).astype(jnp.bfloat16)
-    pair_grad = lax.dot_general(
-        gate_grad, gate_w, contract_last, preferred_element_type=jnp.float32
-    )
-    pair_grad = pair_grad + lax.dot_general(
-        up_grad, up_w, contract_last, preferred_element_type=jnp.float32
-    )
-    grad_g = lax.dot_general(rows_in, gate_grad, contract_rows, preferred_element_type=jnp.float32)
-    grad_u = lax.dot_general(rows_in, up_grad, contract_rows, preferred_element_type=jnp.float32)
-    grad_d = lax.dot_general(act, rows_grad, contract_rows, preferred_element_type=jnp.float32)
-    return (pair_grad, grad_g, grad_u, grad_d)
 
 
 def per_device(tokens, out_grad, expert_ids, gate_weights, w_gate, w_up, w_down):
@@ -82,26 +57,39 @@
     )
     recv = recv.reshape(rows, 2 * width)
 
-    full_gate = jnp.concatenate([own_gate, other_gate], axis=1)
-    full_up = jnp.concatenate([own_up, other_up], axis=1)
+    full_gu = jnp.concatenate([own_gate, other_gate, own_up, other_up], axis=1)
     full_down = jnp.concatenate([own_down, other_down], axis=0)
-    pair_grad, grad_g, grad_u, grad_d = expert_grads(
-        recv[:, :width], recv[:, width:], full_gate, full_up, full_down
+    rows_in = recv[:, :width]
+    rows_grad = recv[:, width:]
+    hidden = 2 * half
+    contract_last = (((1,), (1,)), ((), ()))
+    contract_rows = (((0,), (0,)), ((), ()))
+    gu_pre = jnp.dot(rows_in, full_gu, preferred_element_type=jnp.float32)
+    gate_pre = gu_pre[:, :hidden]
+    up_pre = gu_pre[:, hidden:]
+    sigmoid_g = jax.nn.sigmoid(gate_pre)
+    swish_val = gate_pre * sigmoid_g
+    act = (swish_val * up_pre).astype(jnp.bfloat16)
+    act_grad = lax.dot_general(rows_grad, full_down, contract_last, preferred_element_type=jnp.float32)
+    gate_grad = (act_grad * up_pre * sigmoid_g * (1.0 + gate_pre * (1.0 - sigmoid_g))).astype(
+        jnp.bfloat16
     )
+    up_grad = (act_grad * swish_val).astype(jnp.bfloat16)
+    gu_grad = jnp.concatenate([gate_grad, up_grad], axis=1)
+    pair_grad = lax.dot_general(gu_grad, full_gu, contract_last, preferred_element_type=jnp.float32)
     back = pair_grad.astype(jnp.bfloat16).reshape(experts, cap, width)
     home = lax.all_to_all(back, "expert", split_axis=0, concat_axis=0, tiled=True)
-    peer_g, peer_u, peer_d = partner(
-        (
-            grad_g[:, half:].astype(jnp.bfloat16),
-            grad_u[:, half:].astype(jnp.bfloat16),
-            grad_d[half:, :].astype(jnp.bfloat16),
-        ),
+    grad_gu = lax.dot_general(rows_in, gu_grad, contract_rows, preferred_element_type=jnp.float32)
+    grad_d = lax.dot_general(act, rows_grad, contract_rows, preferred_element_type=jnp.float32)
+    split_gu = grad_gu.reshape(width, 2, 2, half)
+    peer_gu, peer_d = partner(
+        (split_gu[:, :, 1, :].astype(jnp.bfloat16), grad_d[half:, :].astype(jnp.bfloat16)),
         "section",
         pair_bit,
     )
     token_acc = jnp.dot(sel_t, home.reshape(rows, width), preferred_element_type=jnp.float32)
-    mine_g = grad_g[:, :half] + peer_g.astype(jnp.float32)
-    mine_u = grad_u[:, :half] + peer_u.astype(jnp.float32)
+    mine_g = split_gu[:, 0, 0, :] + peer_gu[:, 0, :].astype(jnp.float32)
+    mine_u = split_gu[:, 1, 0, :] + peer_gu[:, 1, :].astype(jnp.float32)
     mine_d = grad_d[:half, :] + peer_d.astype(jnp.float32)
     token_grad = token_acc.astype(jnp.bfloat16)
     out_g = (mine_g * scale).astype(jnp.bfloat16)

time: 156 us -> 161 us (1.032)
  local copies, waits for them, and re-layouts: 2.94 us -> 13.4 us
  waiting for transfers between devices: 86.7 us -> 83.2 us
  starting transfers between devices: 35.3 us -> 32.4 us
  other arithmetic: 6.55 us -> 8.42 us
    all_to_all x1, waiting for transfers between devices: 54 us -> 42.8 us  [per_device(): lax.all_to_all(send, 'expert', split_axis=0, concat_axis=0, tiled=True)]
    unnamed x24 -> x35, local copies, waits for them, and re-layouts: 1.64 us -> 9.77 us
    ppermute x6 -> x5, waiting for transfers between devices: 32.7 us -> 40.4 us  [partner(): return lax.ppermute(value, axis, pairs)]
    ppermute x6 -> x5, starting transfers between devices: 19.5 us -> 16.4 us  [partner(): return lax.ppermute(value, axis, pairs)]
    convert_element_type x0 -> x1, other arithmetic: none -> 2.48 us  [per_device(): out_u = (mine_u * scale).astype(jnp.bfloat16)]
    broadcast_in_dim x2 -> x0, other arithmetic: 1.97 us -> none  [the longest x1 0.99 us: per_device(): out_u[None, None]]
    dot_general x8 -> x5, matrix products: 19.8 us -> 18.8 us  [the longest x1 4.52 us: per_device(): gu_pre = jnp.dot(rows_in, full_gu, preferred_element_type=jnp.float32)]
  transfers between devices with their start and end apart: 8 -> 7, of which waited for: 5 -> 4; matrix products, arithmetic and copies ran while one was open for 9% -> 15% of each run, Pallas kernels for 0% -> 0%
where the time goes in v5:
time: 161 us
  waiting for transfers between devices  83.2 us (52%)
  starting transfers between devices  32.4 us (20%)
  matrix products  22.2 us (14%)
  local copies, waits for them, and re-layouts  13.4 us (8%)
  other arithmetic  8.42 us (5%)
    all_to_all x1, waiting for transfers between devices, per_device(): lax.all_to_all(send, 'expert', split_axis=0, concat_axis=0, tiled=True)  42.8 us
    ppermute x5, waiting for transfers between devices, partner(): return lax.ppermute(value, axis, pairs)  40.4 us
    ppermute x5, starting transfers between devices, partner(): return lax.ppermute(value, axis, pairs)  16.4 us
    all_to_all x1, starting transfers between devices, per_device(): lax.all_to_all(send, 'expert', split_axis=0, concat_axis=0, tiled=True)  10.4 us
    unnamed x35, local copies, waits for them, and re-layouts  9.77 us
    all_to_all x1, starting transfers between devices, per_device(): lax.all_to_all(back, 'expert', split_axis=0, concat_axis=0, tiled=True)  5.59 us
    dot_general x1, matrix products, per_device(): gu_pre = jnp.dot(rows_in, full_gu, preferred_element_type=jnp.float32)  4.52 us
    dot_general x1, matrix products, per_device(): lax.dot_general(gu_grad, full_gu, contract_last, preferred_element_type=j...  4.43 us
  transfers between devices with their start and end apart: 7, of which 4 were waited for; matrix products, arithmetic and copies ran while one was open for 15% of the time, Pallas kernels for 0%

profile of v5, /device:TPU:1, one launch (start us, length us, event | category | flops | bytes accessed | tf_op | source)
XLA Modules:
  0.0 160.6 jit_solution(9521044594433903556)
XLA Ops:
  0.6 0.8 copy.27
  1.4 0.1 eq.49
  1.6 0.1 eq.45
  1.7 0.9 reduce-window.6
  2.6 0.2 slice_reduce_fusion
  2.9 0.1 fusion.29
  3.0 0.1 reduce_sum.21
  3.1 0.1 copy.31
  3.2 0.2 fusion.11
  3.4 0.8 copy.32
  4.2 0.1 broadcast_in_dim.26
  4.4 2.1 %fusion.21 = f32[768,2048]{1,0:T(8,128)S(1)} fusion(pred[768,192]{0,1:T(8,128)(4,1)S(1)} %fusion.11, bf16[192,1024]{1,0:T(8,128)(2,1)} %bitcast.66, bf16[192,1024]{1,0:T(8,128)(2,1)} %bitcast.67), kind=kOutput, calls=%fused_computation.40 | convolution fusion | flops 605552640 | bytes 7225344 | tf_op jit(solution)/shard_map/dot_general | solution.py:50
  6.5 0.2 slice.114
  6.8 0.2 select_reduce_fusion
  7.0 0.2 fusion
  7.2 1.9 %pad_maximum_fusion = bf16[768,2048]{1,0:T(8,128)(2,1)} fusion(bf16[768,1024]{1,0:T(8,128)(2,1)S(1)} %fusion, bf16[768,1024]{1,0:T(8,128)(2,1)S(1)} %slice.114), kind=kLoop, calls=%fused_computation.3 | loop fusion | flops 6291456 | bytes 6291456 | tf_op jit(solution)/shard_map/concatenate | solution.py:53
  9.1 10.4 %all-to-all-start = ((bf16[16,48,2048]{2,1,0:T(8,128)(2,1)}), bf16[16,48,2048]{2,1,0:T(8,128)(2,1)S(1)}, u32[]{:S(2)}, u32[]{:S(2)}) async-start(bf16[16,48,2048]{2,1,0:T(8,128)(2,1)} %bitcast.5), calls=%async_computation | async-start | bytes 6291456 | tf_op jit(solution)/shard_map/all_to_all | solution.py:54
  19.5 2.9 %collective-permute-start.1 = (bf16[1024,256]{1,0:T(8,128)(2,1)}, bf16[1024,256]{1,0:T(8,128)(2,1)S(1)}, u32[]{:S(2)}, u32[]{:S(2)}) collective-permute-start(bf16[1024,256]{1,0:T(8,128)(2,1)} %bitcast.74), channel_id=1, source_target_pairs={{0,256},{16,272},{32,288},{48,304},{64,320},{80,336},{96,352},{112... | collective-permute-start | bytes 1572872 | tf_op jit(solution)/shard_map/ppermute | solution.py:12
  22.4 3.9 %collective-permute-start.2 = (bf16[1024,256]{1,0:T(8,128)(2,1)}, bf16[1024,256]{1,0:T(8,128)(2,1)}, u32[]{:S(2)}, u32[]{:S(2)}) collective-permute-start(bf16[1024,256]{1,0:T(8,128)(2,1)} %bitcast.71), channel_id=1, source_target_pairs={{0,256},{16,272},{32,288},{48,304},{64,320},{80,336},{96,352},{112... | collective-permute-start | bytes 1572872 | tf_op jit(solution)/shard_map/ppermute | solution.py:12
  26.3 2.9 %collective-permute-start = (bf16[256,1024]{1,0:T(8,128)(2,1)}, bf16[256,1024]{1,0:T(8,128)(2,1)}, u32[]{:S(2)}, u32[]{:S(2)}) collective-permute-start(bf16[256,1024]{1,0:T(8,128)(2,1)} %bitcast.69), channel_id=1, source_target_pairs={{0,256},{16,272},{32,288},{48,304},{64,320},{80,336},{96,352},{112... | collective-permute-start | bytes 1572872 | tf_op jit(solution)/shard_map/ppermute | solution.py:12
  29.2 7.1 %collective-permute-done.1 = bf16[1024,256]{1,0:T(8,128)(2,1)S(1)} collective-permute-done((bf16[1024,256]{1,0:T(8,128)(2,1)}, bf16[1024,256]{1,0:T(8,128)(2,1)S(1)}, u32[]{:S(2)}, u32[]{:S(2)}) %collective-permute-start.1) | collective-permute-done | bytes 524320 | tf_op jit(solution)/shard_map/ppermute | solution.py:12
  36.3 0.8 copy-done.8
  37.1 10.5 %collective-permute-done.2 = bf16[1024,256]{1,0:T(8,128)(2,1)} collective-permute-done((bf16[1024,256]{1,0:T(8,128)(2,1)}, bf16[1024,256]{1,0:T(8,128)(2,1)}, u32[]{:S(2)}, u32[]{:S(2)}) %collective-permute-start.2) | collective-permute-done | bytes 524320 | tf_op jit(solution)/shard_map/ppermute | solution.py:12
  47.7 42.8 %all-to-all-done = bf16[16,48,2048]{2,1,0:T(8,128)(2,1)S(1)} async-done(((bf16[16,48,2048]{2,1,0:T(8,128)(2,1)}), bf16[16,48,2048]{2,1,0:T(8,128)(2,1)S(1)}, u32[]{:S(2)}, u32[]{:S(2)}) %all-to-all-start) | async-done | bytes 3145760 | tf_op jit(solution)/shard_map/all_to_all | solution.py:54
  90.5 4.5 %fusion.4 = f32[768,1024]{0,1:T(8,128)S(1)} fusion(bf16[768,2048]{1,0:T(8,128)(2,1)S(1)} %bitcast.59, bf16[1024,256]{1,0:T(8,128)(2,1)} %collective-permute-done.2, bf16[1024,256]{1,0:T(8,128)(2,1)} %bitcast.72, bf16[1024,256]{1,0:T(8,128)(2,1)} %copy-done.8, bf16[1024,256]{1,0:T(8,128)(2,1)} %bitcast.75), kind=kOutput, calls=%fused_computation.14 | convolution fusion | flops 1619001344 | bytes 6815744 | tf_op jit(solution)/shard_map/dot_general | solution.py:67
  95.0 0.0 copy-start.10
  95.0 0.0 copy-start.6
  95.0 0.0 copy-start.7
  95.0 0.0 copy-start.9
  95.1 0.0 collective-permute-done
  95.1 0.0 copy-done.1
  95.1 0.0 copy-done.5
  95.1 3.1 %multiply_convert_fusion.2 = (bf16[768,512]{0,1:T(8,128)(2,1)S(1)}, bf16[768,512]{0,1:T(8,128)(2,1)S(1)}) fusion(f32[768,1024]{0,1:T(8,128)S(1)} %fusion.4, bf16[256,1024]{1,0:T(8,128)(2,1)} %collective-permute-done, bf16[256,1024]{1,0:T(8,128)(2,1)S(1)} %bitcast.70, bf16[768,2048]{1,0:T(8,128)(2,1)S(1)} %bitcast.60), kind=kOutput, calls=%fused_computation.9 | convolution fusion | flops 812515328 | bytes 7340032 | tf_op jit(solution)/shard_map/dot_general | solution.py:73
  98.2 0.0 copy-done.10
  98.2 0.0 copy-start.11
  98.2 0.0 copy-start.13
  98.2 0.0 copy-done.6
  98.3 0.0 copy-done.7
  98.3 0.0 copy-done.9
  98.3 4.4 %convolution_convert_fusion = bf16[768,1024]{1,0:T(8,128)(2,1)} fusion(bf16[768,512]{0,1:T(8,128)(2,1)S(1)} %get-tuple-element.5, bf16[768,512]{0,1:T(8,128)(2,1)S(1)} %get-tuple-element.4, bf16[1024,256]{1,0:T(8,128)(2,1)} %collective-permute-done.2, bf16[1024,256]{1,0:T(8,128)(2,1)S(1)} %bitcast.73, bf16[1024,256]{1,0:T(8,128)(2,1)S(1)} %copy-done.9, ...), kind=kOutput, calls=%fused_computation.5 | convolution fusion | flops 1622933504 | bytes 5242880 | tf_op jit(solution)/shard_map/dot_general | solution.py:79
  102.7 0.0 copy-done.11
  102.7 0.0 copy-done.13
  102.7 5.6 %all-to-all-start.1 = ((bf16[16,48,1024]{2,1,0:T(8,128)(2,1)}), bf16[16,48,1024]{2,1,0:T(8,128)(2,1)S(1)}, u32[]{:S(2)}, u32[]{:S(2)}) async-start(bf16[16,48,1024]{2,1,0:T(8,128)(2,1)} %bitcast.10), calls=%async_computation.1 | async-start | bytes 3145728 | tf_op jit(solution)/shard_map/all_to_all | solution.py:81
  108.3 0.0 copy-done.12
  108.3 0.0 copy-done.14
  108.3 3.2 %fusion.2 = f32[1024,1024]{0,1:T(8,128)S(1)} fusion(bf16[768,2048]{1,0:T(8,128)(2,1)} %bitcast.61, bf16[768,512]{0,1:T(8,128)(2,1)S(1)} %copy-done.14, bf16[768,512]{0,1:T(8,128)(2,1)S(1)} %copy-done.12), kind=kOutput, calls=%fused_computation.12 | convolution fusion | flops 1613758464 | bytes 7340032 | tf_op jit(solution)/shard_map/dot_general | solution.py:82
  111.5 1.9 %copy-done.2 = f32[1024,1024]{0,1:T(8,128)} copy-done((f32[1024,1024]{0,1:T(8,128)}, f32[1024,1024]{0,1:T(8,128)S(1)}, u32[]{:S(2)}) %copy-start.2) | copy-done | bytes 4194328
  113.5 0.2 slice.71
  113.6 1.3 copy.41
  114.9 2.8 %collective-permute-start.3 = (bf16[1024,2,256]{2,0,1:T(8,128)(2,1)}, bf16[1024,2,256]{2,0,1:T(8,128)(2,1)}, u32[]{:S(2)}, u32[]{:S(2)}) collective-permute-start(bf16[1024,2,256]{2,0,1:T(8,128)(2,1)} %bitcast.65), channel_id=1, source_target_pairs={{0,256},{16,272},{32,288},{48,304},{64,320},{80,336},{96,352},{112... | collective-permute-start | bytes 3145736 | tf_op jit(solution)/shard_map/ppermute | solution.py:12
  117.8 3.5 %fusion.6 = f32[512,1024]{1,0:T(8,128)S(1)} fusion(bf16[768,2048]{1,0:T(8,128)(2,1)} %bitcast.62, f32[768,1024]{0,1:T(8,128)} %copy-done.10), kind=kOutput, calls=%fused_computation.16 | convolution fusion | flops 807665664 | bytes 6815744 | tf_op jit(solution)/shard_map/dot_general | solution.py:83
  121.3 0.9 slice.115
  122.3 3.9 %collective-permute-start.4 = (bf16[256,1024]{1,0:T(8,128)(2,1)}, bf16[256,1024]{1,0:T(8,128)(2,1)}, u32[]{:S(2)}, u32[]{:S(2)}) collective-permute-start(bf16[256,1024]{1,0:T(8,128)(2,1)} %slice.115), channel_id=1, source_target_pairs={{0,256},{16,272},{32,288},{48,304},{64,320},{80,336},{96,352},{112... | collective-permute-start | bytes 1572872 | tf_op jit(solution)/shard_map/ppermute | solution.py:12
  126.2 1.5 fusion.37
  127.7 0.0 copy-done.4
  127.7 1.6 copy.39
  129.3 2.5 %copy.40 = f32[1024,1,1,256]{3,0,2,1:T(8,128)} copy(f32[1024,1,1,256]{0,3,2,1:T(8,128)} %get-tuple-element.6) | data formatting | bytes 2097152
  131.8 22.7 %collective-permute-done.4 = bf16[256,1024]{1,0:T(8,128)(2,1)} collective-permute-done((bf16[256,1024]{1,0:T(8,128)(2,1)}, bf16[256,1024]{1,0:T(8,128)(2,1)}, u32[]{:S(2)}, u32[]{:S(2)}) %collective-permute-start.4) | collective-permute-done | bytes 524320 | tf_op jit(solution)/shard_map/ppermute | solution.py:12
  154.5 2.3 %fusion.25 = bf16[1,1,256,1024]{3,2,1,0:T(8,128)(2,1)} fusion(bf16[256,1024]{1,0:T(8,128)(2,1)} %collective-permute-done.4, f32[512,1024]{1,0:T(8,128)} %copy-done.4), kind=kLoop, calls=%fused_computation.44 | loop fusion | flops 1048576 | bytes 2097152 | tf_op jit(solution)/shard_map/broadcast_in_dim | solution.py:98
  156.8 0.0 collective-permute-done.3
  156.8 0.0 copy-done
  156.8 2.5 %fusion.18 = (bf16[1,1,1024,256]{3,2,1,0:T(8,128)(2,1)}, bf16[1,1,1024,256]{3,2,1,0:T(8,128)(2,1)}) fusion(f32[1024,1,1,256]{3,0,2,1:T(8,128)S(1)} %copy-done, bf16[1024,2,256]{2,0,1:T(8,128)(2,1)} %collective-permute-done.3, f32[1024,1,1,256]{3,0,2,1:T(8,128)S(1)} %copy.39), kind=kLoop, calls=%fused_computation.35 | loop fusion | flops 2097152 | bytes 4194304 | tf_op jit(solution)/shard_map/convert_element_type | solution.py:96
  159.3 0.0 all-to-all-done.1
  159.3 1.2 fusion.10
  (15 shorter events, 0.1 us)
Async XLA Ops:
  9.1 81.4 %all-to-all-start = ((bf16[16,48,2048]{2,1,0:T(8,128)(2,1)}), bf16[16,48,2048]{2,1,0:T(8,128)(2,1)S(1)}, u32[]{:S(2)}, u32[]{:S(2)}) async-start(bf16[16,48,2048]{2,1,0:T(8,128)(2,1)} %bitcast.5), calls=%async_computation | async-start | bytes 6291456 | tf_op jit(solution)/shard_map/all_to_all | solution.py:54
  19.5 16.8 %collective-permute-start.1 = (bf16[1024,256]{1,0:T(8,128)(2,1)}, bf16[1024,256]{1,0:T(8,128)(2,1)S(1)}, u32[]{:S(2)}, u32[]{:S(2)}) collective-permute-start(bf16[1024,256]{1,0:T(8,128)(2,1)} %bitcast.74), channel_id=1, source_target_pairs={{0,256},{16,272},{32,288},{48,304},{64,320},{80,336},{96,352},{112... | collective-permute-start | bytes 1572872 | tf_op jit(solution)/shard_map/ppermute | solution.py:12
  22.4 25.3 %collective-permute-start.2 = (bf16[1024,256]{1,0:T(8,128)(2,1)}, bf16[1024,256]{1,0:T(8,128)(2,1)}, u32[]{:S(2)}, u32[]{:S(2)}) collective-permute-start(bf16[1024,256]{1,0:T(8,128)(2,1)} %bitcast.71), channel_id=1, source_target_pairs={{0,256},{16,272},{32,288},{48,304},{64,320},{80,336},{96,352},{112... | collective-permute-start | bytes 1572872 | tf_op jit(solution)/shard_map/ppermute | solution.py:12
  26.3 68.8 %collective-permute-start = (bf16[256,1024]{1,0:T(8,128)(2,1)}, bf16[256,1024]{1,0:T(8,128)(2,1)}, u32[]{:S(2)}, u32[]{:S(2)}) collective-permute-start(bf16[256,1024]{1,0:T(8,128)(2,1)} %bitcast.69), channel_id=1, source_target_pairs={{0,256},{16,272},{32,288},{48,304},{64,320},{80,336},{96,352},{112... | collective-permute-start | bytes 1572872 | tf_op jit(solution)/shard_map/ppermute | solution.py:12
  36.3 0.8 copy-start.8
  90.5 4.6 %copy-start.1 = (bf16[16,48,2048]{2,1,0:T(8,128)(2,1)}, bf16[16,48,2048]{2,1,0:T(8,128)(2,1)S(1)}, u32[]{:S(2)}) copy-start(bf16[16,48,2048]{2,1,0:T(8,128)(2,1)S(1)} %all-to-all-done) | copy-start | bytes 9437188
  90.5 4.6 %copy-start.5 = (bf16[1,1,256,1024]{3,2,1,0:T(8,128)(2,1)S(1)}, bf16[1,1,256,1024]{3,2,1,0:T(8,128)(2,1)}, u32[]{:S(2)}) copy-start(bf16[1,1,256,1024]{3,2,1,0:T(8,128)(2,1)} %param.13) | copy-start | bytes 1572868
  95.0 3.2 %copy-start.10 = (f32[768,1024]{0,1:T(8,128)}, f32[768,1024]{0,1:T(8,128)S(1)}, u32[]{:S(2)}) copy-start(f32[768,1024]{0,1:T(8,128)S(1)} %fusion.4) | copy-start | bytes 9437188
  95.0 3.2 %copy-start.6 = (bf16[1,1,1024,256]{3,2,1,0:T(8,128)(2,1)S(1)}, bf16[1,1,1024,256]{3,2,1,0:T(8,128)(2,1)}, u32[]{:S(2)}) copy-start(bf16[1,1,1024,256]{3,2,1,0:T(8,128)(2,1)} %param.12) | copy-start | bytes 1572868
  95.0 3.2 %copy-start.7 = (bf16[1,1,1024,256]{3,2,1,0:T(8,128)(2,1)S(1)}, bf16[1,1,1024,256]{3,2,1,0:T(8,128)(2,1)}, u32[]{:S(2)}) copy-start(bf16[1,1,1024,256]{3,2,1,0:T(8,128)(2,1)} %param.11) | copy-start | bytes 1572868
  95.0 3.2 %copy-start.9 = (bf16[1024,256]{1,0:T(8,128)(2,1)S(1)}, bf16[1024,256]{1,0:T(8,128)(2,1)}, u32[]{:S(2)}) copy-start(bf16[1024,256]{1,0:T(8,128)(2,1)} %copy-done.8) | copy-start | bytes 1572868
  98.2 4.5 %copy-start.11 = (bf16[768,512]{0,1:T(8,128)(2,1)}, bf16[768,512]{0,1:T(8,128)(2,1)S(1)}, u32[]{:S(2)}) copy-start(bf16[768,512]{0,1:T(8,128)(2,1)S(1)} %get-tuple-element.4) | copy-start | bytes 2359300
  98.2 4.5 %copy-start.13 = (bf16[768,512]{0,1:T(8,128)(2,1)}, bf16[768,512]{0,1:T(8,128)(2,1)S(1)}, u32[]{:S(2)}) copy-start(bf16[768,512]{0,1:T(8,128)(2,1)S(1)} %get-tuple-element.5) | copy-start | bytes 2359300
  102.7 5.6 %copy-start.12 = (bf16[768,512]{0,1:T(8,128)(2,1)S(1)}, bf16[768,512]{0,1:T(8,128)(2,1)}, u32[]{:S(2)}) copy-start(bf16[768,512]{0,1:T(8,128)(2,1)} %copy-done.11) | copy-start | bytes 2359300
  102.7 5.6 %copy-start.14 = (bf16[768,512]{0,1:T(8,128)(2,1)S(1)}, bf16[768,512]{0,1:T(8,128)(2,1)}, u32[]{:S(2)}) copy-start(bf16[768,512]{0,1:T(8,128)(2,1)} %copy-done.13) | copy-start | bytes 2359300
  102.7 56.6 %all-to-all-start.1 = ((bf16[16,48,1024]{2,1,0:T(8,128)(2,1)}), bf16[16,48,1024]{2,1,0:T(8,128)(2,1)S(1)}, u32[]{:S(2)}, u32[]{:S(2)}) async-start(bf16[16,48,1024]{2,1,0:T(8,128)(2,1)} %bitcast.10), calls=%async_computation.1 | async-start | bytes 3145728 | tf_op jit(solution)/shard_map/all_to_all | solution.py:81
  111.5 1.9 %copy-start.2 = (f32[1024,1024]{0,1:T(8,128)}, f32[1024,1024]{0,1:T(8,128)S(1)}, u32[]{:S(2)}) copy-start(f32[1024,1024]{0,1:T(8,128)S(1)} %fusion.2) | copy-start | bytes 12582916
  114.9 41.9 %collective-permute-start.3 = (bf16[1024,2,256]{2,0,1:T(8,128)(2,1)}, bf16[1024,2,256]{2,0,1:T(8,128)(2,1)}, u32[]{:S(2)}, u32[]{:S(2)}) collective-permute-start(bf16[1024,2,256]{2,0,1:T(8,128)(2,1)} %bitcast.65), channel_id=1, source_target_pairs={{0,256},{16,272},{32,288},{48,304},{64,320},{80,336},{96,352},{112... | collective-permute-start | bytes 3145736 | tf_op jit(solution)/shard_map/ppermute | solution.py:12
  117.8 8.4 %copy-start.3 = (f32[1024,1024]{0,1:T(8,128)S(1)}, f32[1024,1024]{0,1:T(8,128)}, u32[]{:S(2)}) copy-start(f32[1024,1024]{0,1:T(8,128)} %copy-done.2) | copy-start | bytes 12582916
  121.3 6.4 %copy-start.4 = (f32[512,1024]{1,0:T(8,128)}, f32[512,1024]{1,0:T(8,128)S(1)}, u32[]{:S(2)}) copy-start(f32[512,1024]{1,0:T(8,128)S(1)} %fusion.6) | copy-start | bytes 6291460
  122.3 32.2 %collective-permute-start.4 = (bf16[256,1024]{1,0:T(8,128)(2,1)}, bf16[256,1024]{1,0:T(8,128)(2,1)}, u32[]{:S(2)}, u32[]{:S(2)}) collective-permute-start(bf16[256,1024]{1,0:T(8,128)(2,1)} %slice.115), channel_id=1, source_target_pairs={{0,256},{16,272},{32,288},{48,304},{64,320},{80,336},{96,352},{112... | collective-permute-start | bytes 1572872 | tf_op jit(solution)/shard_map/ppermute | solution.py:12
  131.8 25.1 %copy-start = (f32[1024,1,1,256]{3,0,2,1:T(8,128)S(1)}, f32[1024,1,1,256]{3,0,2,1:T(8,128)}, u32[]{:S(2)}) copy-start(f32[1024,1,1,256]{3,0,2,1:T(8,128)} %copy.40) | copy-start | bytes 3145732

commit v6 on v5

--- a/solution.py
+++ b/solution.py
@@ -81,15 +81,18 @@
     home = lax.all_to_all(back, "expert", split_axis=0, concat_axis=0, tiled=True)
     grad_gu = lax.dot_general(rows_in, gu_grad, contract_rows, preferred_element_type=jnp.float32)
     grad_d = lax.dot_general(act, rows_grad, contract_rows, preferred_element_type=jnp.float32)
-    split_gu = grad_gu.reshape(width, 2, 2, half)
-    peer_gu, peer_d = partner(
-        (split_gu[:, :, 1, :].astype(jnp.bfloat16), grad_d[half:, :].astype(jnp.bfloat16)),
+    peer_g, peer_u, peer_d = partner(
+        (
+            grad_gu[:, half:hidden].astype(jnp.bfloat16),
+            grad_gu[:, hidden + half:].astype(jnp.bfloat16),
+            grad_d[half:, :].astype(jnp.bfloat16),
+        ),
         "section",
         pair_bit,
     )
     token_acc = jnp.dot(sel_t, home.reshape(rows, width), preferred_element_type=jnp.float32)
-    mine_g = split_gu[:, 0, 0, :] + peer_gu[:, 0, :].astype(jnp.float32)
-    mine_u = split_gu[:, 1, 0, :] + peer_gu[:, 1, :].astype(jnp.float32)
+    mine_g = grad_gu[:, :half] + peer_g.astype(jnp.float32)
+    mine_u = grad_gu[:, hidden:hidden + half] + peer_u.astype(jnp.float32)
     mine_d = grad_d[:half, :] + peer_d.astype(jnp.float32)
     token_grad = token_acc.astype(jnp.bfloat16)
     out_g = (mine_g * scale).astype(jnp.bfloat16)

time: 161 us -> 154 us (0.957)
  local copies, waits for them, and re-layouts: 13.4 us -> 3.67 us
  waiting for transfers between devices: 83.2 us -> 87.1 us
  starting transfers between devices: 32.4 us -> 35.1 us
  other arithmetic: 8.42 us -> 5.97 us
    unnamed x35 -> x26, local copies, waits for them, and re-layouts: 9.77 us -> 2.44 us
    ppermute x5 -> x6, waiting for transfers between devices: 40.4 us -> 44.3 us  [partner(): return lax.ppermute(value, axis, pairs)]
    ppermute x5 -> x6, starting transfers between devices: 16.4 us -> 19.3 us  [partner(): return lax.ppermute(value, axis, pairs)]
    convert_element_type x1 -> x0, other arithmetic: 2.48 us -> none  [per_device(): out_u = (mine_u * scale).astype(jnp.bfloat16)]
  transfers between devices with their start and end apart: 7 -> 8, of which waited for: 4 -> 6; matrix products, arithmetic and copies ran while one was open for 15% -> 8% of each run, Pallas kernels for 0% -> 0%
where the time goes in v6:
time: 154 us
  waiting for transfers between devices  87.1 us (57%)
  starting transfers between devices  35.1 us (23%)
  matrix products  20.8 us (14%)
  other arithmetic  5.97 us (4%)
  local copies, waits for them, and re-layouts  3.67 us (2%)
    ppermute x6, waiting for transfers between devices, partner(): return lax.ppermute(value, axis, pairs)  44.3 us
    all_to_all x1, waiting for transfers between devices, per_device(): lax.all_to_all(send, 'expert', split_axis=0, concat_axis=0, tiled=True)  42.8 us
    ppermute x6, starting transfers between devices, partner(): return lax.ppermute(value, axis, pairs)  19.3 us
    all_to_all x1, starting transfers between devices, per_device(): lax.all_to_all(send, 'expert', split_axis=0, concat_axis=0, tiled=True)  10.4 us
    all_to_all x1, starting transfers between devices, per_device(): lax.all_to_all(back, 'expert', split_axis=0, concat_axis=0, tiled=True)  5.45 us
    dot_general x1, matrix products, per_device(): gu_pre = jnp.dot(rows_in, full_gu, preferred_element_type=jnp.float32)  4.52 us
    dot_general x1, matrix products, per_device(): lax.dot_general(gu_grad, full_gu, contract_last, preferred_element_type=j...  4.41 us
    dot_general x1, matrix products, per_device(): lax.dot_general(act, rows_grad, contract_rows, preferred_element_type=jnp...  3.52 us
  transfers between devices with their start and end apart: 8, of which 6 were waited for; matrix products, arithmetic and copies ran while one was open for 8% of the time, Pallas kernels for 0%

profile of v6, /device:TPU:1, one launch (start us, length us, event | category | flops | bytes accessed | tf_op | source)
XLA Modules:
  0.0 153.7 jit_solution(11159185223206227325)
XLA Ops:
  0.6 0.8 copy.21
  1.4 0.1 eq.45
  1.6 0.1 eq.49
  1.7 0.9 reduce-window.6
  2.6 0.2 slice_reduce_fusion
  2.9 0.1 fusion.31
  3.0 0.1 reduce_sum.21
  3.1 0.1 copy.25
  3.2 0.8 copy.26
  4.0 0.1 broadcast_in_dim.30
  4.2 0.2 fusion.11
  4.3 2.1 %fusion.21 = f32[768,2048]{1,0:T(8,128)S(1)} fusion(pred[768,192]{0,1:T(8,128)(4,1)S(1)} %fusion.11, bf16[192,1024]{1,0:T(8,128)(2,1)} %bitcast.49, bf16[192,1024]{1,0:T(8,128)(2,1)} %bitcast.50), kind=kOutput, calls=%fused_computation.39 | convolution fusion | flops 605552640 | bytes 7225344 | tf_op jit(solution)/shard_map/dot_general | solution.py:50
  6.5 0.2 slice.118
  6.7 0.2 select_reduce_fusion
  6.9 0.2 fusion
  7.2 1.9 %pad_maximum_fusion = bf16[768,2048]{1,0:T(8,128)(2,1)} fusion(bf16[768,1024]{1,0:T(8,128)(2,1)S(1)} %fusion, bf16[768,1024]{1,0:T(8,128)(2,1)S(1)} %slice.118), kind=kLoop, calls=%fused_computation.3 | loop fusion | flops 6291456 | bytes 6291456 | tf_op jit(solution)/shard_map/concatenate | solution.py:53
  9.1 10.4 %all-to-all-start = ((bf16[16,48,2048]{2,1,0:T(8,128)(2,1)}), bf16[16,48,2048]{2,1,0:T(8,128)(2,1)S(1)}, u32[]{:S(2)}, u32[]{:S(2)}) async-start(bf16[16,48,2048]{2,1,0:T(8,128)(2,1)} %bitcast.5), calls=%async_computation | async-start | bytes 6291456 | tf_op jit(solution)/shard_map/all_to_all | solution.py:54
  19.5 2.9 %collective-permute-start.1 = (bf16[1024,256]{1,0:T(8,128)(2,1)}, bf16[1024,256]{1,0:T(8,128)(2,1)S(1)}, u32[]{:S(2)}, u32[]{:S(2)}) collective-permute-start(bf16[1024,256]{1,0:T(8,128)(2,1)} %bitcast.57), channel_id=1, source_target_pairs={{0,256},{16,272},{32,288},{48,304},{64,320},{80,336},{96,352},{112... | collective-permute-start | bytes 1572872 | tf_op jit(solution)/shard_map/ppermute | solution.py:12
  22.4 3.9 %collective-permute-start.2 = (bf16[1024,256]{1,0:T(8,128)(2,1)}, bf16[1024,256]{1,0:T(8,128)(2,1)}, u32[]{:S(2)}, u32[]{:S(2)}) collective-permute-start(bf16[1024,256]{1,0:T(8,128)(2,1)} %bitcast.54), channel_id=1, source_target_pairs={{0,256},{16,272},{32,288},{48,304},{64,320},{80,336},{96,352},{112... | collective-permute-start | bytes 1572872 | tf_op jit(solution)/shard_map/ppermute | solution.py:12
  26.3 2.9 %collective-permute-start = (bf16[256,1024]{1,0:T(8,128)(2,1)}, bf16[256,1024]{1,0:T(8,128)(2,1)}, u32[]{:S(2)}, u32[]{:S(2)}) collective-permute-start(bf16[256,1024]{1,0:T(8,128)(2,1)} %bitcast.52), channel_id=1, source_target_pairs={{0,256},{16,272},{32,288},{48,304},{64,320},{80,336},{96,352},{112... | collective-permute-start | bytes 1572872 | tf_op jit(solution)/shard_map/ppermute | solution.py:12
  29.2 7.1 %collective-permute-done.1 = bf16[1024,256]{1,0:T(8,128)(2,1)S(1)} collective-permute-done((bf16[1024,256]{1,0:T(8,128)(2,1)}, bf16[1024,256]{1,0:T(8,128)(2,1)S(1)}, u32[]{:S(2)}, u32[]{:S(2)}) %collective-permute-start.1) | collective-permute-done | bytes 524320 | tf_op jit(solution)/shard_map/ppermute | solution.py:12
  36.3 0.8 copy-done.5
  37.1 10.5 %collective-permute-done.2 = bf16[1024,256]{1,0:T(8,128)(2,1)} collective-permute-done((bf16[1024,256]{1,0:T(8,128)(2,1)}, bf16[1024,256]{1,0:T(8,128)(2,1)}, u32[]{:S(2)}, u32[]{:S(2)}) %collective-permute-start.2) | collective-permute-done | bytes 524320 | tf_op jit(solution)/shard_map/ppermute | solution.py:12
  47.7 42.8 %all-to-all-done = bf16[16,48,2048]{2,1,0:T(8,128)(2,1)S(1)} async-done(((bf16[16,48,2048]{2,1,0:T(8,128)(2,1)}), bf16[16,48,2048]{2,1,0:T(8,128)(2,1)S(1)}, u32[]{:S(2)}, u32[]{:S(2)}) %all-to-all-start) | async-done | bytes 3145760 | tf_op jit(solution)/shard_map/all_to_all | solution.py:54
  90.5 0.0 copy-start
  90.5 0.0 copy-start.2
  90.5 4.5 %fusion.4 = f32[768,1024]{0,1:T(8,128)S(1)} fusion(bf16[768,2048]{1,0:T(8,128)(2,1)S(1)} %bitcast.45, bf16[1024,256]{1,0:T(8,128)(2,1)} %collective-permute-done.2, bf16[1024,256]{1,0:T(8,128)(2,1)} %bitcast.55, bf16[1024,256]{1,0:T(8,128)(2,1)} %copy-done.5, bf16[1024,256]{1,0:T(8,128)(2,1)} %bitcast.58), kind=kOutput, calls=%fused_computation.14 | convolution fusion | flops 1619001344 | bytes 6815744 | tf_op jit(solution)/shard_map/dot_general | solution.py:67
  95.0 0.0 copy-start.11
  95.0 0.0 copy-start.3
  95.0 0.0 copy-start.4
  95.0 0.0 copy-start.6
  95.0 0.0 collective-permute-done
  95.1 0.0 copy-done
  95.1 0.0 copy-done.2
  95.1 3.1 %multiply_convert_fusion.2 = (bf16[768,512]{0,1:T(8,128)(2,1)S(1)}, bf16[768,512]{0,1:T(8,128)(2,1)S(1)}) fusion(f32[768,1024]{0,1:T(8,128)S(1)} %fusion.4, bf16[256,1024]{1,0:T(8,128)(2,1)} %collective-permute-done, bf16[256,1024]{1,0:T(8,128)(2,1)S(1)} %bitcast.53, bf16[768,2048]{1,0:T(8,128)(2,1)S(1)} %bitcast.46), kind=kOutput, calls=%fused_computation.9 | convolution fusion | flops 812515328 | bytes 7340032 | tf_op jit(solution)/shard_map/dot_general | solution.py:73
  98.2 0.0 copy-done.11
  98.2 0.0 copy-start.7
  98.2 0.0 copy-start.9
  98.2 0.0 copy-done.3
  98.2 0.0 copy-done.4
  98.3 0.0 copy-done.6
  98.3 4.4 %convolution_convert_fusion = bf16[768,1024]{1,0:T(8,128)(2,1)} fusion(bf16[768,512]{0,1:T(8,128)(2,1)S(1)} %get-tuple-element.5, bf16[768,512]{0,1:T(8,128)(2,1)S(1)} %get-tuple-element.4, bf16[1024,256]{1,0:T(8,128)(2,1)} %collective-permute-done.2, bf16[1024,256]{1,0:T(8,128)(2,1)S(1)} %bitcast.56, bf16[1024,256]{1,0:T(8,128)(2,1)S(1)} %copy-done.6, ...), kind=kOutput, calls=%fused_computation.5 | convolution fusion | flops 1622933504 | bytes 5242880 | tf_op jit(solution)/shard_map/dot_general | solution.py:79
  102.7 0.0 copy-done.7
  102.7 0.0 copy-done.9
  102.7 5.4 %all-to-all-start.1 = ((bf16[16,48,1024]{2,1,0:T(8,128)(2,1)}), bf16[16,48,1024]{2,1,0:T(8,128)(2,1)S(1)}, u32[]{:S(2)}, u32[]{:S(2)}) async-start(bf16[16,48,1024]{2,1,0:T(8,128)(2,1)} %bitcast.10), calls=%async_computation.1 | async-start | bytes 3145728 | tf_op jit(solution)/shard_map/all_to_all | solution.py:81
  108.1 0.0 copy-start.8
  108.1 0.0 copy-start.10
  108.2 3.5 %fusion.6 = f32[512,1024]{1,0:T(8,128)S(1)} fusion(bf16[768,2048]{1,0:T(8,128)(2,1)} %bitcast.47, f32[768,1024]{0,1:T(8,128)} %copy-done.11), kind=kOutput, calls=%fused_computation.16 | convolution fusion | flops 807665664 | bytes 6815744 | tf_op jit(solution)/shard_map/dot_general | solution.py:83
  111.7 0.1 slice.119
  111.8 2.9 %collective-permute-start.5 = (bf16[256,1024]{1,0:T(8,128)(2,1)S(1)}, bf16[256,1024]{1,0:T(8,128)(2,1)S(1)}, u32[]{:S(2)}, u32[]{:S(2)}) collective-permute-start(bf16[256,1024]{1,0:T(8,128)(2,1)S(1)} %slice.119), channel_id=1, source_target_pairs={{0,256},{16,272},{32,288},{48,304},{64,320},{80,336},{96,352},{112... | collective-permute-start | bytes 1572872 | tf_op jit(solution)/shard_map/ppermute | solution.py:12
  114.6 0.0 copy-done.1
  114.6 0.0 copy-done.8
  114.6 0.0 copy-done.10
  114.7 1.8 %fusion.40 = (bf16[1024,1024]{1,0:T(8,128)(2,1)S(1)}, f32[1024,1024]{1,0:T(8,128)S(1)}) fusion(bf16[768,512]{0,1:T(8,128)(2,1)S(1)} %copy-done.10, bf16[768,512]{0,1:T(8,128)(2,1)S(1)} %copy-done.8, bf16[768,2048]{1,0:T(8,128)(2,1)S(1)} %bitcast.48), kind=kOutput, calls=%fused_computation.65 | convolution fusion | flops 1614807040 | bytes 9437184 | tf_op jit(solution)/shard_map/dot_general | solution.py:82
  116.5 0.1 fusion.39
  116.6 3.9 %collective-permute-start.4 = (bf16[1024,256]{1,0:T(8,128)(2,1)S(1)}, bf16[1024,256]{1,0:T(8,128)(2,1)S(1)}, u32[]{:S(2)}, u32[]{:S(2)}) collective-permute-start(bf16[1024,256]{1,0:T(8,128)(2,1)S(1)} %get-tuple-element.8), channel_id=1, source_target_pairs={{0,256},{16,272},{32,288},{48,304},{64,320},{80,336},{96,352},{112... | collective-permute-start | bytes 1572872 | tf_op jit(solution)/shard_map/ppermute | solution.py:12
  120.5 2.9 %collective-permute-start.3 = (bf16[1024,256]{1,0:T(8,128)(2,1)S(1)}, bf16[1024,256]{1,0:T(8,128)(2,1)S(1)}, u32[]{:S(2)}, u32[]{:S(2)}) collective-permute-start(bf16[1024,256]{1,0:T(8,128)(2,1)S(1)} %get-tuple-element.9), channel_id=1, source_target_pairs={{0,256},{16,272},{32,288},{48,304},{64,320},{80,336},{96,352},{112... | collective-permute-start | bytes 1572872 | tf_op jit(solution)/shard_map/ppermute | solution.py:12
  123.4 5.1 %collective-permute-done.5 = bf16[256,1024]{1,0:T(8,128)(2,1)S(1)} collective-permute-done((bf16[256,1024]{1,0:T(8,128)(2,1)S(1)}, bf16[256,1024]{1,0:T(8,128)(2,1)S(1)}, u32[]{:S(2)}, u32[]{:S(2)}) %collective-permute-start.5) | collective-permute-done | bytes 524320 | tf_op jit(solution)/shard_map/ppermute | solution.py:12
  128.5 1.0 fusion.27
  129.5 10.3 %collective-permute-done.4 = bf16[1024,256]{1,0:T(8,128)(2,1)S(1)} collective-permute-done((bf16[1024,256]{1,0:T(8,128)(2,1)S(1)}, bf16[1024,256]{1,0:T(8,128)(2,1)S(1)}, u32[]{:S(2)}, u32[]{:S(2)}) %collective-permute-start.4) | collective-permute-done | bytes 524320 | tf_op jit(solution)/shard_map/ppermute | solution.py:12
  139.8 11.2 %collective-permute-done.3 = bf16[1024,256]{1,0:T(8,128)(2,1)S(1)} collective-permute-done((bf16[1024,256]{1,0:T(8,128)(2,1)S(1)}, bf16[1024,256]{1,0:T(8,128)(2,1)S(1)}, u32[]{:S(2)}, u32[]{:S(2)}) %collective-permute-start.3) | collective-permute-done | bytes 524320 | tf_op jit(solution)/shard_map/ppermute | solution.py:12
  151.0 1.4 fusion.26
  152.4 0.0 all-to-all-done.1
  152.4 1.2 fusion.10
  (7 shorter events, 0.1 us)
Async XLA Ops:
  9.1 81.4 %all-to-all-start = ((bf16[16,48,2048]{2,1,0:T(8,128)(2,1)}), bf16[16,48,2048]{2,1,0:T(8,128)(2,1)S(1)}, u32[]{:S(2)}, u32[]{:S(2)}) async-start(bf16[16,48,2048]{2,1,0:T(8,128)(2,1)} %bitcast.5), calls=%async_computation | async-start | bytes 6291456 | tf_op jit(solution)/shard_map/all_to_all | solution.py:54
  19.5 16.8 %collective-permute-start.1 = (bf16[1024,256]{1,0:T(8,128)(2,1)}, bf16[1024,256]{1,0:T(8,128)(2,1)S(1)}, u32[]{:S(2)}, u32[]{:S(2)}) collective-permute-start(bf16[1024,256]{1,0:T(8,128)(2,1)} %bitcast.57), channel_id=1, source_target_pairs={{0,256},{16,272},{32,288},{48,304},{64,320},{80,336},{96,352},{112... | collective-permute-start | bytes 1572872 | tf_op jit(solution)/shard_map/ppermute | solution.py:12
  22.4 25.3 %collective-permute-start.2 = (bf16[1024,256]{1,0:T(8,128)(2,1)}, bf16[1024,256]{1,0:T(8,128)(2,1)}, u32[]{:S(2)}, u32[]{:S(2)}) collective-permute-start(bf16[1024,256]{1,0:T(8,128)(2,1)} %bitcast.54), channel_id=1, source_target_pairs={{0,256},{16,272},{32,288},{48,304},{64,320},{80,336},{96,352},{112... | collective-permute-start | bytes 1572872 | tf_op jit(solution)/shard_map/ppermute | solution.py:12
  26.3 68.8 %collective-permute-start = (bf16[256,1024]{1,0:T(8,128)(2,1)}, bf16[256,1024]{1,0:T(8,128)(2,1)}, u32[]{:S(2)}, u32[]{:S(2)}) collective-permute-start(bf16[256,1024]{1,0:T(8,128)(2,1)} %bitcast.52), channel_id=1, source_target_pairs={{0,256},{16,272},{32,288},{48,304},{64,320},{80,336},{96,352},{112... | collective-permute-start | bytes 1572872 | tf_op jit(solution)/shard_map/ppermute | solution.py:12
  36.3 0.8 copy-start.5
  90.5 4.6 %copy-start = (bf16[16,48,2048]{2,1,0:T(8,128)(2,1)}, bf16[16,48,2048]{2,1,0:T(8,128)(2,1)S(1)}, u32[]{:S(2)}) copy-start(bf16[16,48,2048]{2,1,0:T(8,128)(2,1)S(1)} %all-to-all-done) | copy-start | bytes 9437188
  90.5 4.6 %copy-start.2 = (bf16[1,1,256,1024]{3,2,1,0:T(8,128)(2,1)S(1)}, bf16[1,1,256,1024]{3,2,1,0:T(8,128)(2,1)}, u32[]{:S(2)}) copy-start(bf16[1,1,256,1024]{3,2,1,0:T(8,128)(2,1)} %param.13) | copy-start | bytes 1572868
  95.0 3.2 %copy-start.11 = (f32[768,1024]{0,1:T(8,128)}, f32[768,1024]{0,1:T(8,128)S(1)}, u32[]{:S(2)}) copy-start(f32[768,1024]{0,1:T(8,128)S(1)} %fusion.4) | copy-start | bytes 9437188
  95.0 3.2 %copy-start.3 = (bf16[1,1,1024,256]{3,2,1,0:T(8,128)(2,1)S(1)}, bf16[1,1,1024,256]{3,2,1,0:T(8,128)(2,1)}, u32[]{:S(2)}) copy-start(bf16[1,1,1024,256]{3,2,1,0:T(8,128)(2,1)} %param.12) | copy-start | bytes 1572868
  95.0 3.2 %copy-start.4 = (bf16[1,1,1024,256]{3,2,1,0:T(8,128)(2,1)S(1)}, bf16[1,1,1024,256]{3,2,1,0:T(8,128)(2,1)}, u32[]{:S(2)}) copy-start(bf16[1,1,1024,256]{3,2,1,0:T(8,128)(2,1)} %param.11) | copy-start | bytes 1572868
  95.0 3.2 %copy-start.6 = (bf16[1024,256]{1,0:T(8,128)(2,1)S(1)}, bf16[1024,256]{1,0:T(8,128)(2,1)}, u32[]{:S(2)}) copy-start(bf16[1024,256]{1,0:T(8,128)(2,1)} %copy-done.5) | copy-start | bytes 1572868
  98.2 4.5 %copy-start.7 = (bf16[768,512]{0,1:T(8,128)(2,1)}, bf16[768,512]{0,1:T(8,128)(2,1)S(1)}, u32[]{:S(2)}) copy-start(bf16[768,512]{0,1:T(8,128)(2,1)S(1)} %get-tuple-element.4) | copy-start | bytes 2359300
  98.2 4.5 %copy-start.9 = (bf16[768,512]{0,1:T(8,128)(2,1)}, bf16[768,512]{0,1:T(8,128)(2,1)S(1)}, u32[]{:S(2)}) copy-start(bf16[768,512]{0,1:T(8,128)(2,1)S(1)} %get-tuple-element.5) | copy-start | bytes 2359300
  102.7 49.7 %all-to-all-start.1 = ((bf16[16,48,1024]{2,1,0:T(8,128)(2,1)}), bf16[16,48,1024]{2,1,0:T(8,128)(2,1)S(1)}, u32[]{:S(2)}, u32[]{:S(2)}) async-start(bf16[16,48,1024]{2,1,0:T(8,128)(2,1)} %bitcast.10), calls=%async_computation.1 | async-start | bytes 3145728 | tf_op jit(solution)/shard_map/all_to_all | solution.py:81
  108.1 6.5 %copy-start.1 = (bf16[16,48,2048]{2,1,0:T(8,128)(2,1)S(1)}, bf16[16,48,2048]{2,1,0:T(8,128)(2,1)}, u32[]{:S(2)}) copy-start(bf16[16,48,2048]{2,1,0:T(8,128)(2,1)} %copy-done) | copy-start | bytes 9437188
  108.1 6.5 %copy-start.8 = (bf16[768,512]{0,1:T(8,128)(2,1)S(1)}, bf16[768,512]{0,1:T(8,128)(2,1)}, u32[]{:S(2)}) copy-start(bf16[768,512]{0,1:T(8,128)(2,1)} %copy-done.7) | copy-start | bytes 2359300
  108.1 6.5 %copy-start.10 = (bf16[768,512]{0,1:T(8,128)(2,1)S(1)}, bf16[768,512]{0,1:T(8,128)(2,1)}, u32[]{:S(2)}) copy-start(bf16[768,512]{0,1:T(8,128)(2,1)} %copy-done.9) | copy-start | bytes 2359300
  111.8 16.8 %collective-permute-start.5 = (bf16[256,1024]{1,0:T(8,128)(2,1)S(1)}, bf16[256,1024]{1,0:T(8,128)(2,1)S(1)}, u32[]{:S(2)}, u32[]{:S(2)}) collective-permute-start(bf16[256,1024]{1,0:T(8,128)(2,1)S(1)} %slice.119), channel_id=1, source_target_pairs={{0,256},{16,272},{32,288},{48,304},{64,320},{80,336},{96,352},{112... | collective-permute-start | bytes 1572872 | tf_op jit(solution)/shard_map/ppermute | solution.py:12
  116.6 23.2 %collective-permute-start.4 = (bf16[1024,256]{1,0:T(8,128)(2,1)S(1)}, bf16[1024,256]{1,0:T(8,128)(2,1)S(1)}, u32[]{:S(2)}, u32[]{:S(2)}) collective-permute-start(bf16[1024,256]{1,0:T(8,128)(2,1)S(1)} %get-tuple-element.8), channel_id=1, source_target_pairs={{0,256},{16,272},{32,288},{48,304},{64,320},{80,336},{96,352},{112... | collective-permute-start | bytes 1572872 | tf_op jit(solution)/shard_map/ppermute | solution.py:12
  120.5 30.5 %collective-permute-start.3 = (bf16[1024,256]{1,0:T(8,128)(2,1)S(1)}, bf16[1024,256]{1,0:T(8,128)(2,1)S(1)}, u32[]{:S(2)}, u32[]{:S(2)}) collective-permute-start(bf16[1024,256]{1,0:T(8,128)(2,1)S(1)} %get-tuple-element.9), channel_id=1, source_target_pairs={{0,256},{16,272},{32,288},{48,304},{64,320},{80,336},{96,352},{112... | collective-permute-start | bytes 1572872 | tf_op jit(solution)/shard_map/ppermute | solution.py:12

commit v7 on v5

--- a/solution.py
+++ b/solution.py
@@ -79,18 +79,22 @@
     pair_grad = lax.dot_general(gu_grad, full_gu, contract_last, preferred_element_type=jnp.float32)
     back = pair_grad.astype(jnp.bfloat16).reshape(experts, cap, width)
     home = lax.all_to_all(back, "expert", split_axis=0, concat_axis=0, tiled=True)
-    grad_gu = lax.dot_general(rows_in, gu_grad, contract_rows, preferred_element_type=jnp.float32)
-    grad_d = lax.dot_general(act, rows_grad, contract_rows, preferred_element_type=jnp.float32)
-    split_gu = grad_gu.reshape(width, 2, 2, half)
-    peer_gu, peer_d = partner(
-        (split_gu[:, :, 1, :].astype(jnp.bfloat16), grad_d[half:, :].astype(jnp.bfloat16)),
-        "section",
-        pair_bit,
+    def grad_cols(lo, hi):
+        return (
+            lax.dot_general(rows_in, gate_grad[:, lo:hi], contract_rows, preferred_element_type=jnp.float32),
+            lax.dot_general(rows_in, up_grad[:, lo:hi], contract_rows, preferred_element_type=jnp.float32),
+            lax.dot_general(act[:, lo:hi], rows_grad, contract_rows, preferred_element_type=jnp.float32),
+        )
+
+    peer_terms = grad_cols(half, hidden)
+    peer_g, peer_u, peer_d = partner(
+        tuple(t.astype(jnp.bfloat16) for t in peer_terms), "section", pair_bit
     )
+    own_g, own_u, own_d = grad_cols(0, half)
     token_acc = jnp.dot(sel_t, home.reshape(rows, width), preferred_element_type=jnp.float32)
-    mine_g = split_gu[:, 0, 0, :] + peer_gu[:, 0, :].astype(jnp.float32)
-    mine_u = split_gu[:, 1, 0, :] + peer_gu[:, 1, :].astype(jnp.float32)
-    mine_d = grad_d[:half, :] + peer_d.astype(jnp.float32)
+    mine_g = own_g + peer_g.astype(jnp.float32)
+    mine_u = own_u + peer_u.astype(jnp.float32)
+    mine_d = own_d + peer_d.astype(jnp.float32)
     token_grad = token_acc.astype(jnp.bfloat16)
     out_g = (mine_g * scale).astype(jnp.bfloat16)
     out_u = (mine_u * scale).astype(jnp.bfloat16)

time: 161 us -> 154 us (0.957)
  local copies, waits for them, and re-layouts: 13.4 us -> 3.53 us
  other arithmetic: 8.42 us -> 3.62 us
  starting transfers between devices: 32.4 us -> 35.5 us
  matrix products: 22.2 us -> 24.5 us
    unnamed x35 -> x26, local copies, waits for them, and re-layouts: 9.77 us -> 2.43 us
    ppermute x5 -> x6, starting transfers between devices: 16.4 us -> 19.6 us  [partner(): return lax.ppermute(value, axis, pairs)]
    slice x4 -> x1, local copies, waits for them, and re-layouts: 2.75 us -> 0.22 us  [the longest x1 1.45 us: per_device(): mine_u = split_gu[:, 1, 0, :] + peer_gu[:, 1, :].astype(jnp.float32)]
    convert_element_type x1 -> x0, other arithmetic: 2.48 us -> none  [per_device(): out_u = (mine_u * scale).astype(jnp.bfloat16)]
    broadcast_in_dim x1 -> x0, other arithmetic: 2.34 us -> none  [per_device(): out_d[None, None]]
    dot_general x2 -> x6, matrix products: 6.71 us -> 8.65 us  [the longest x2 3.52 us: grad_cols(): lax.dot_general(act[:, lo:hi], rows_grad, contract_rows, preferred_elemen...]
    ppermute x5 -> x6, waiting for transfers between devices: 40.4 us -> 42 us  [partner(): return lax.ppermute(value, axis, pairs)]
  transfers between devices with their start and end apart: 7 -> 8, of which waited for: 4 -> 6; matrix products, arithmetic and copies ran while one was open for 15% -> 9% of each run, Pallas kernels for 0% -> 0%
where the time goes in v7:
time: 154 us; the launch traced here: 153 us
  waiting for transfers between devices  84.8 us (55%)
  starting transfers between devices  35.5 us (23%)
  matrix products  24.5 us (16%)
  other arithmetic  3.62 us (2%)
  local copies, waits for them, and re-layouts  3.53 us (2%)
    all_to_all x1, waiting for transfers between devices, per_device(): lax.all_to_all(send, 'expert', split_axis=0, concat_axis=0, tiled=True)  42.8 us
    ppermute x6, waiting for transfers between devices, partner(): return lax.ppermute(value, axis, pairs)  42 us
    ppermute x6, starting transfers between devices, partner(): return lax.ppermute(value, axis, pairs)  19.6 us
    all_to_all x1, starting transfers between devices, per_device(): lax.all_to_all(send, 'expert', split_axis=0, concat_axis=0, tiled=True)  10.4 us
    all_to_all x1, starting transfers between devices, per_device(): lax.all_to_all(back, 'expert', split_axis=0, concat_axis=0, tiled=True)  5.59 us
    dot_general x1, matrix products, per_device(): gu_pre = jnp.dot(rows_in, full_gu, preferred_element_type=jnp.float32)  4.52 us
    dot_general x1, matrix products, per_device(): lax.dot_general(gu_grad, full_gu, contract_last, preferred_element_type=j...  4.44 us
    dot_general x1, matrix products, per_device(): lax.dot_general(rows_grad, full_down, contract_last, preferred_element_ty...  3.57 us
  transfers between devices with their start and end apart: 8, of which 6 were waited for; matrix products, arithmetic and copies ran while one was open for 9% of the time, Pallas kernels for 0%

profile of v7, /device:TPU:1, one launch (start us, length us, event | category | flops | bytes accessed | tf_op | source)
XLA Modules:
  0.0 153.0 jit_solution(3462566283870084222)
XLA Ops:
  0.6 0.8 copy.21
  1.4 0.1 eq.49
  1.6 0.1 eq.45
  1.7 0.9 reduce-window.6
  2.6 0.2 slice_reduce_fusion
  2.9 0.1 fusion.50
  3.0 0.1 reduce_sum.21
  3.1 0.1 copy.25
  3.2 0.2 fusion.11
  3.4 0.8 copy.26
  4.2 0.1 broadcast_in_dim.30
  4.4 2.1 %fusion.33 = f32[768,2048]{1,0:T(8,128)S(1)} fusion(pred[768,192]{0,1:T(8,128)(4,1)S(1)} %fusion.11, bf16[192,1024]{1,0:T(8,128)(2,1)} %bitcast.53, bf16[192,1024]{1,0:T(8,128)(2,1)} %bitcast.54), kind=kOutput, calls=%fused_computation.44 | convolution fusion | flops 605552640 | bytes 7225344 | tf_op jit(solution)/shard_map/dot_general | solution.py:50
  6.5 0.2 slice.123
  6.8 0.2 select_reduce_fusion
  7.0 0.2 fusion
  7.2 2.0 %pad_maximum_fusion = bf16[768,2048]{1,0:T(8,128)(2,1)} fusion(bf16[768,1024]{1,0:T(8,128)(2,1)S(1)} %fusion, bf16[768,1024]{1,0:T(8,128)(2,1)S(1)} %slice.123), kind=kLoop, calls=%fused_computation.3 | loop fusion | flops 6291456 | bytes 6291456 | tf_op jit(solution)/shard_map/concatenate | solution.py:53
  9.1 10.4 %all-to-all-start = ((bf16[16,48,2048]{2,1,0:T(8,128)(2,1)}), bf16[16,48,2048]{2,1,0:T(8,128)(2,1)S(1)}, u32[]{:S(2)}, u32[]{:S(2)}) async-start(bf16[16,48,2048]{2,1,0:T(8,128)(2,1)} %bitcast.5), calls=%async_computation | async-start | bytes 6291456 | tf_op jit(solution)/shard_map/all_to_all | solution.py:54
  19.5 2.9 %collective-permute-start.1 = (bf16[1024,256]{1,0:T(8,128)(2,1)}, bf16[1024,256]{1,0:T(8,128)(2,1)S(1)}, u32[]{:S(2)}, u32[]{:S(2)}) collective-permute-start(bf16[1024,256]{1,0:T(8,128)(2,1)} %bitcast.61), channel_id=1, source_target_pairs={{0,256},{16,272},{32,288},{48,304},{64,320},{80,336},{96,352},{112... | collective-permute-start | bytes 1572872 | tf_op jit(solution)/shard_map/ppermute | solution.py:12
  22.4 3.9 %collective-permute-start.2 = (bf16[1024,256]{1,0:T(8,128)(2,1)}, bf16[1024,256]{1,0:T(8,128)(2,1)}, u32[]{:S(2)}, u32[]{:S(2)}) collective-permute-start(bf16[1024,256]{1,0:T(8,128)(2,1)} %bitcast.58), channel_id=1, source_target_pairs={{0,256},{16,272},{32,288},{48,304},{64,320},{80,336},{96,352},{112... | collective-permute-start | bytes 1572872 | tf_op jit(solution)/shard_map/ppermute | solution.py:12
  26.3 2.9 %collective-permute-start = (bf16[256,1024]{1,0:T(8,128)(2,1)}, bf16[256,1024]{1,0:T(8,128)(2,1)}, u32[]{:S(2)}, u32[]{:S(2)}) collective-permute-start(bf16[256,1024]{1,0:T(8,128)(2,1)} %bitcast.56), channel_id=1, source_target_pairs={{0,256},{16,272},{32,288},{48,304},{64,320},{80,336},{96,352},{112... | collective-permute-start | bytes 1572872 | tf_op jit(solution)/shard_map/ppermute | solution.py:12
  29.2 7.1 %collective-permute-done.1 = bf16[1024,256]{1,0:T(8,128)(2,1)S(1)} collective-permute-done((bf16[1024,256]{1,0:T(8,128)(2,1)}, bf16[1024,256]{1,0:T(8,128)(2,1)S(1)}, u32[]{:S(2)}, u32[]{:S(2)}) %collective-permute-start.1) | collective-permute-done | bytes 524320 | tf_op jit(solution)/shard_map/ppermute | solution.py:12
  36.4 0.0 copy-start.5
  36.4 0.8 copy-done.5
  37.2 10.5 %collective-permute-done.2 = bf16[1024,256]{1,0:T(8,128)(2,1)} collective-permute-done((bf16[1024,256]{1,0:T(8,128)(2,1)}, bf16[1024,256]{1,0:T(8,128)(2,1)}, u32[]{:S(2)}, u32[]{:S(2)}) %collective-permute-start.2) | collective-permute-done | bytes 524320 | tf_op jit(solution)/shard_map/ppermute | solution.py:12
  47.7 42.8 %all-to-all-done = bf16[16,48,2048]{2,1,0:T(8,128)(2,1)S(1)} async-done(((bf16[16,48,2048]{2,1,0:T(8,128)(2,1)}), bf16[16,48,2048]{2,1,0:T(8,128)(2,1)S(1)}, u32[]{:S(2)}, u32[]{:S(2)}) %all-to-all-start) | async-done | bytes 3145760 | tf_op jit(solution)/shard_map/all_to_all | solution.py:54
  90.5 0.0 copy-start
  90.5 4.5 %fusion.21 = f32[768,1024]{0,1:T(8,128)S(1)} fusion(bf16[768,2048]{1,0:T(8,128)(2,1)S(1)} %bitcast.45, bf16[1024,256]{1,0:T(8,128)(2,1)} %collective-permute-done.2, bf16[1024,256]{1,0:T(8,128)(2,1)} %bitcast.59, bf16[1024,256]{1,0:T(8,128)(2,1)} %copy-done.5, bf16[1024,256]{1,0:T(8,128)(2,1)} %bitcast.62), kind=kOutput, calls=%fused_computation.40 | convolution fusion | flops 1619001344 | bytes 6815744 | tf_op jit(solution)/shard_map/dot_general | solution.py:67
  95.0 0.0 copy-start.3
  95.0 0.0 copy-start.4
  95.1 0.0 copy-start.6
  95.1 0.0 collective-permute-done
  95.1 0.0 copy-done
  95.1 0.0 copy-done.2
  95.1 3.6 %multiply_convert_fusion.2 = (bf16[768,512]{0,1:T(8,128)(2,1)S(1)}, bf16[768,512]{0,1:T(8,128)(2,1)S(1)}, bf16[768,512]{0,1:T(8,128)(2,1)}) fusion(f32[768,1024]{0,1:T(8,128)S(1)} %fusion.21, bf16[256,1024]{1,0:T(8,128)(2,1)} %collective-permute-done, bf16[256,1024]{1,0:T(8,128)(2,1)S(1)} %bitcast.57, bf16[768,2048]{1,0:T(8,128)(2,1)S(1)} %bitcast.46), kind=kOutput, calls=%fused_computation.11 | convolution fusion | flops 813301760 | bytes 8126464 | tf_op jit(solution)/shard_map/dot_general | solution.py:73
  98.7 0.0 copy-start.8
  98.7 0.0 copy-start.10
  98.7 0.0 copy-done.3
  98.7 0.0 copy-done.4
  98.7 0.0 copy-done.6
  98.7 4.4 %convolution_convert_fusion = bf16[768,1024]{1,0:T(8,128)(2,1)} fusion(bf16[768,512]{0,1:T(8,128)(2,1)S(1)} %get-tuple-element.5, bf16[768,512]{0,1:T(8,128)(2,1)S(1)} %get-tuple-element.4, bf16[1024,256]{1,0:T(8,128)(2,1)} %collective-permute-done.2, bf16[1024,256]{1,0:T(8,128)(2,1)S(1)} %bitcast.60, bf16[1024,256]{1,0:T(8,128)(2,1)S(1)} %copy-done.6, ...), kind=kOutput, calls=%fused_computation.5 | convolution fusion | flops 1622933504 | bytes 5242880 | tf_op jit(solution)/shard_map/dot_general | solution.py:79
  103.1 0.0 copy-done.8
  103.1 0.0 copy-done.10
  103.1 0.0 copy-start.7
  103.1 5.6 %all-to-all-start.1 = ((bf16[16,48,1024]{2,1,0:T(8,128)(2,1)}), bf16[16,48,1024]{2,1,0:T(8,128)(2,1)S(1)}, u32[]{:S(2)}, u32[]{:S(2)}) async-start(bf16[16,48,1024]{2,1,0:T(8,128)(2,1)} %bitcast.10), calls=%async_computation.1 | async-start | bytes 3145728 | tf_op jit(solution)/shard_map/all_to_all | solution.py:81
  108.8 0.0 copy-done.7
  108.8 2.1 %convolution_convert_fusion.1 = bf16[256,1024]{1,0:T(8,128)(2,1)S(1)} fusion(bf16[768,2048]{1,0:T(8,128)(2,1)} %bitcast.47, bf16[768,512]{0,1:T(8,128)(2,1)S(1)} %copy-done.7), kind=kOutput, calls=%fused_computation.14 | convolution fusion | flops 402915328 | bytes 2490368 | tf_op jit(solution)/shard_map/dot_general | solution.py:86
  110.9 0.0 copy-start.9
  110.9 3.0 %collective-permute-start.5 = (bf16[256,1024]{1,0:T(8,128)(2,1)S(1)}, bf16[256,1024]{1,0:T(8,128)(2,1)S(1)}, u32[]{:S(2)}, u32[]{:S(2)}) collective-permute-start(bf16[256,1024]{1,0:T(8,128)(2,1)S(1)} %convolution_convert_fusion.1), channel_id=1, source_target_pairs={{0,256},{16,272},{32,288},{48,304},{64,320},{80,336},{96,352},{112... | collective-permute-start | bytes 1572872 | tf_op jit(solution)/shard_map/ppermute | solution.py:12
  113.9 0.0 copy-done.1
  113.9 1.6 %convolution_convert_fusion.2 = bf16[1024,256]{1,0:T(8,128)(2,1)S(1)} fusion(bf16[768,2048]{1,0:T(8,128)(2,1)S(1)} %bitcast.48, bf16[768,512]{0,1:T(8,128)(2,1)} %copy-done.10), kind=kOutput, calls=%fused_computation.15 | convolution fusion | flops 402915328 | bytes 2490368 | tf_op jit(solution)/shard_map/dot_general | solution.py:85
  115.6 3.9 %collective-permute-start.4 = (bf16[1024,256]{1,0:T(8,128)(2,1)S(1)}, bf16[1024,256]{1,0:T(8,128)(2,1)S(1)}, u32[]{:S(2)}, u32[]{:S(2)}) collective-permute-start(bf16[1024,256]{1,0:T(8,128)(2,1)S(1)} %convolution_convert_fusion.2), channel_id=1, source_target_pairs={{0,256},{16,272},{32,288},{48,304},{64,320},{80,336},{96,352},{112... | collective-permute-start | bytes 1572872 | tf_op jit(solution)/shard_map/ppermute | solution.py:12
  119.5 0.0 copy-done.9
  119.5 0.6 convolution_convert_fusion.3
  120.1 0.0 copy-start.11
  120.2 3.0 %collective-permute-start.3 = (bf16[1024,256]{1,0:T(8,128)(2,1)S(1)}, bf16[1024,256]{1,0:T(8,128)(2,1)S(1)}, u32[]{:S(2)}, u32[]{:S(2)}) collective-permute-start(bf16[1024,256]{1,0:T(8,128)(2,1)S(1)} %convolution_convert_fusion.3), channel_id=1, source_target_pairs={{0,256},{16,272},{32,288},{48,304},{64,320},{80,336},{96,352},{112... | collective-permute-start | bytes 1572872 | tf_op jit(solution)/shard_map/ppermute | solution.py:12
  123.1 4.7 %collective-permute-done.5 = bf16[256,1024]{1,0:T(8,128)(2,1)S(1)} collective-permute-done((bf16[256,1024]{1,0:T(8,128)(2,1)S(1)}, bf16[256,1024]{1,0:T(8,128)(2,1)S(1)}, u32[]{:S(2)}, u32[]{:S(2)}) %collective-permute-start.5) | collective-permute-done | bytes 524320 | tf_op jit(solution)/shard_map/ppermute | solution.py:12
  127.8 1.4 fusion.37
  129.2 9.8 %collective-permute-done.4 = bf16[1024,256]{1,0:T(8,128)(2,1)S(1)} collective-permute-done((bf16[1024,256]{1,0:T(8,128)(2,1)S(1)}, bf16[1024,256]{1,0:T(8,128)(2,1)S(1)}, u32[]{:S(2)}, u32[]{:S(2)}) %collective-permute-start.4) | collective-permute-done | bytes 524320 | tf_op jit(solution)/shard_map/ppermute | solution.py:12
  139.1 0.0 copy-done.11
  139.1 1.4 fusion.30
  140.5 9.8 %collective-permute-done.3 = bf16[1024,256]{1,0:T(8,128)(2,1)S(1)} collective-permute-done((bf16[1024,256]{1,0:T(8,128)(2,1)S(1)}, bf16[1024,256]{1,0:T(8,128)(2,1)S(1)}, u32[]{:S(2)}, u32[]{:S(2)}) %collective-permute-start.3) | collective-permute-done | bytes 524320 | tf_op jit(solution)/shard_map/ppermute | solution.py:12
  150.3 1.4 fusion.27
  151.7 0.0 all-to-all-done.1
  151.7 1.2 fusion.5
  (7 shorter events, 0.1 us)
Async XLA Ops:
  9.1 81.4 %all-to-all-start = ((bf16[16,48,2048]{2,1,0:T(8,128)(2,1)}), bf16[16,48,2048]{2,1,0:T(8,128)(2,1)S(1)}, u32[]{:S(2)}, u32[]{:S(2)}) async-start(bf16[16,48,2048]{2,1,0:T(8,128)(2,1)} %bitcast.5), calls=%async_computation | async-start | bytes 6291456 | tf_op jit(solution)/shard_map/all_to_all | solution.py:54
  19.5 16.8 %collective-permute-start.1 = (bf16[1024,256]{1,0:T(8,128)(2,1)}, bf16[1024,256]{1,0:T(8,128)(2,1)S(1)}, u32[]{:S(2)}, u32[]{:S(2)}) collective-permute-start(bf16[1024,256]{1,0:T(8,128)(2,1)} %bitcast.61), channel_id=1, source_target_pairs={{0,256},{16,272},{32,288},{48,304},{64,320},{80,336},{96,352},{112... | collective-permute-start | bytes 1572872 | tf_op jit(solution)/shard_map/ppermute | solution.py:12
  22.4 25.3 %collective-permute-start.2 = (bf16[1024,256]{1,0:T(8,128)(2,1)}, bf16[1024,256]{1,0:T(8,128)(2,1)}, u32[]{:S(2)}, u32[]{:S(2)}) collective-permute-start(bf16[1024,256]{1,0:T(8,128)(2,1)} %bitcast.58), channel_id=1, source_target_pairs={{0,256},{16,272},{32,288},{48,304},{64,320},{80,336},{96,352},{112... | collective-permute-start | bytes 1572872 | tf_op jit(solution)/shard_map/ppermute | solution.py:12
  26.3 68.8 %collective-permute-start = (bf16[256,1024]{1,0:T(8,128)(2,1)}, bf16[256,1024]{1,0:T(8,128)(2,1)}, u32[]{:S(2)}, u32[]{:S(2)}) collective-permute-start(bf16[256,1024]{1,0:T(8,128)(2,1)} %bitcast.56), channel_id=1, source_target_pairs={{0,256},{16,272},{32,288},{48,304},{64,320},{80,336},{96,352},{112... | collective-permute-start | bytes 1572872 | tf_op jit(solution)/shard_map/ppermute | solution.py:12
  36.4 0.8 copy-start.5
  90.5 4.6 %copy-start = (bf16[16,48,2048]{2,1,0:T(8,128)(2,1)}, bf16[16,48,2048]{2,1,0:T(8,128)(2,1)S(1)}, u32[]{:S(2)}) copy-start(bf16[16,48,2048]{2,1,0:T(8,128)(2,1)S(1)} %all-to-all-done) | copy-start | bytes 9437188
  90.5 4.6 %copy-start.2 = (bf16[1,1,256,1024]{3,2,1,0:T(8,128)(2,1)S(1)}, bf16[1,1,256,1024]{3,2,1,0:T(8,128)(2,1)}, u32[]{:S(2)}) copy-start(bf16[1,1,256,1024]{3,2,1,0:T(8,128)(2,1)} %param.13) | copy-start | bytes 1572868
  95.0 3.6 %copy-start.3 = (bf16[1,1,1024,256]{3,2,1,0:T(8,128)(2,1)S(1)}, bf16[1,1,1024,256]{3,2,1,0:T(8,128)(2,1)}, u32[]{:S(2)}) copy-start(bf16[1,1,1024,256]{3,2,1,0:T(8,128)(2,1)} %param.12) | copy-start | bytes 1572868
  95.0 3.6 %copy-start.4 = (bf16[1,1,1024,256]{3,2,1,0:T(8,128)(2,1)S(1)}, bf16[1,1,1024,256]{3,2,1,0:T(8,128)(2,1)}, u32[]{:S(2)}) copy-start(bf16[1,1,1024,256]{3,2,1,0:T(8,128)(2,1)} %param.11) | copy-start | bytes 1572868
  95.1 3.6 %copy-start.6 = (bf16[1024,256]{1,0:T(8,128)(2,1)S(1)}, bf16[1024,256]{1,0:T(8,128)(2,1)}, u32[]{:S(2)}) copy-start(bf16[1024,256]{1,0:T(8,128)(2,1)} %copy-done.5) | copy-start | bytes 1572868
  98.7 4.5 %copy-start.8 = (bf16[768,512]{0,1:T(8,128)(2,1)}, bf16[768,512]{0,1:T(8,128)(2,1)S(1)}, u32[]{:S(2)}) copy-start(bf16[768,512]{0,1:T(8,128)(2,1)S(1)} %get-tuple-element.4) | copy-start | bytes 2359300
  98.7 4.5 %copy-start.10 = (bf16[768,512]{0,1:T(8,128)(2,1)}, bf16[768,512]{0,1:T(8,128)(2,1)S(1)}, u32[]{:S(2)}) copy-start(bf16[768,512]{0,1:T(8,128)(2,1)S(1)} %get-tuple-element.5) | copy-start | bytes 2359300
  103.1 5.6 %copy-start.7 = (bf16[768,512]{0,1:T(8,128)(2,1)S(1)}, bf16[768,512]{0,1:T(8,128)(2,1)}, u32[]{:S(2)}) copy-start(bf16[768,512]{0,1:T(8,128)(2,1)} %get-tuple-element.6) | copy-start | bytes 2359300
  103.1 48.6 %all-to-all-start.1 = ((bf16[16,48,1024]{2,1,0:T(8,128)(2,1)}), bf16[16,48,1024]{2,1,0:T(8,128)(2,1)S(1)}, u32[]{:S(2)}, u32[]{:S(2)}) async-start(bf16[16,48,1024]{2,1,0:T(8,128)(2,1)} %bitcast.10), calls=%async_computation.1 | async-start | bytes 3145728 | tf_op jit(solution)/shard_map/all_to_all | solution.py:81
  108.7 5.2 %copy-start.1 = (bf16[16,48,2048]{2,1,0:T(8,128)(2,1)S(1)}, bf16[16,48,2048]{2,1,0:T(8,128)(2,1)}, u32[]{:S(2)}) copy-start(bf16[16,48,2048]{2,1,0:T(8,128)(2,1)} %copy-done) | copy-start | bytes 9437188
  110.9 8.6 %copy-start.9 = (bf16[768,512]{0,1:T(8,128)(2,1)S(1)}, bf16[768,512]{0,1:T(8,128)(2,1)}, u32[]{:S(2)}) copy-start(bf16[768,512]{0,1:T(8,128)(2,1)} %copy-done.8) | copy-start | bytes 2359300
  110.9 16.9 %collective-permute-start.5 = (bf16[256,1024]{1,0:T(8,128)(2,1)S(1)}, bf16[256,1024]{1,0:T(8,128)(2,1)S(1)}, u32[]{:S(2)}, u32[]{:S(2)}) collective-permute-start(bf16[256,1024]{1,0:T(8,128)(2,1)S(1)} %convolution_convert_fusion.1), channel_id=1, source_target_pairs={{0,256},{16,272},{32,288},{48,304},{64,320},{80,336},{96,352},{112... | collective-permute-start | bytes 1572872 | tf_op jit(solution)/shard_map/ppermute | solution.py:12
  115.6 23.5 %collective-permute-start.4 = (bf16[1024,256]{1,0:T(8,128)(2,1)S(1)}, bf16[1024,256]{1,0:T(8,128)(2,1)S(1)}, u32[]{:S(2)}, u32[]{:S(2)}) collective-permute-start(bf16[1024,256]{1,0:T(8,128)(2,1)S(1)} %convolution_convert_fusion.2), channel_id=1, source_target_pairs={{0,256},{16,272},{32,288},{48,304},{64,320},{80,336},{96,352},{112... | collective-permute-start | bytes 1572872 | tf_op jit(solution)/shard_map/ppermute | solution.py:12
  120.1 18.9 %copy-start.11 = (bf16[768,512]{0,1:T(8,128)(2,1)S(1)}, bf16[768,512]{0,1:T(8,128)(2,1)}, u32[]{:S(2)}) copy-start(bf16[768,512]{0,1:T(8,128)(2,1)} %copy-done.10) | copy-start | bytes 2359300
  120.2 30.1 %collective-permute-start.3 = (bf16[1024,256]{1,0:T(8,128)(2,1)S(1)}, bf16[1024,256]{1,0:T(8,128)(2,1)S(1)}, u32[]{:S(2)}, u32[]{:S(2)}) collective-permute-start(bf16[1024,256]{1,0:T(8,128)(2,1)S(1)} %convolution_convert_fusion.3), channel_id=1, source_target_pairs={{0,256},{16,272},{32,288},{48,304},{64,320},{80,336},{96,352},{112... | collective-permute-start | bytes 1572872 | tf_op jit(solution)/shard_map/ppermute | solution.py:12

commit v8 on v7

--- a/solution.py
+++ b/solution.py
@@ -47,9 +47,9 @@
     pair_gate = jnp.sum(jnp.where(hit, gates.reshape(tok * topk)[None, :], 0.0), axis=1)
     sel = hit.reshape(rows, tok, topk).any(axis=2).astype(jnp.bfloat16)
     both = jnp.concatenate([inputs, grads], axis=1)
-    picked = jnp.dot(sel, both, preferred_element_type=jnp.float32)
-    slot_in = picked[:, :width].astype(jnp.bfloat16)
-    slot_grad = (picked[:, width:] * pair_gate[:, None]).astype(jnp.bfloat16)
+    picked = jnp.dot(sel, both, preferred_element_type=jnp.bfloat16)
+    slot_in = picked[:, :width]
+    slot_grad = (picked[:, width:].astype(jnp.float32) * pair_gate[:, None]).astype(jnp.bfloat16)
     send = jnp.concatenate([slot_in, slot_grad], axis=1).reshape(experts, cap, 2 * width)
     recv = lax.all_to_all(send, "expert", split_axis=0, concat_axis=0, tiled=True)
     sel_t = lax.optimization_barrier(

time: 154 us -> 154 us (level)
  no operation moved by 1% of the time
where the time goes in v8:
time: 154 us; the launch traced here: 153 us
  waiting for transfers between devices  84.8 us (55%)
  starting transfers between devices  35.5 us (23%)
  matrix products  24.5 us (16%)
  other arithmetic  3.71 us (2%)
  local copies, waits for them, and re-layouts  3.45 us (2%)
    all_to_all x1, waiting for transfers between devices, per_device(): lax.all_to_all(send, 'expert', split_axis=0, concat_axis=0, tiled=True)  42.8 us
    ppermute x6, waiting for transfers between devices, partner(): return lax.ppermute(value, axis, pairs)  42 us
    ppermute x6, starting transfers between devices, partner(): return lax.ppermute(value, axis, pairs)  19.6 us
    all_to_all x1, starting transfers between devices, per_device(): lax.all_to_all(send, 'expert', split_axis=0, concat_axis=0, tiled=True)  10.4 us
    all_to_all x1, starting transfers between devices, per_device(): lax.all_to_all(back, 'expert', split_axis=0, concat_axis=0, tiled=True)  5.59 us
    dot_general x1, matrix products, per_device(): gu_pre = jnp.dot(rows_in, full_gu, preferred_element_type=jnp.float32)  4.52 us
    dot_general x1, matrix products, per_device(): lax.dot_general(gu_grad, full_gu, contract_last, preferred_element_type=j...  4.44 us
    dot_general x1, matrix products, per_device(): lax.dot_general(rows_grad, full_down, contract_last, preferred_element_ty...  3.57 us
  transfers between devices with their start and end apart: 8, of which 6 were waited for; matrix products, arithmetic and copies ran while one was open for 9% of the time, Pallas kernels for 0%

profile of v8, /device:TPU:1, one launch (start us, length us, event | category | flops | bytes accessed | tf_op | source)
XLA Modules:
  0.0 153.0 jit_solution(1068327115016987879)
XLA Ops:
  0.6 0.8 copy.21
  1.4 0.1 eq.49
  1.6 0.1 eq.45
  1.7 0.9 reduce-window.6
  2.6 0.2 slice_reduce_fusion
  2.9 0.1 fusion.49
  3.0 0.1 reduce_sum.21
  3.1 0.1 copy.25
  3.2 0.2 fusion.10
  3.4 0.8 copy.26
  4.2 0.1 broadcast_in_dim.30
  4.4 2.1 %fusion.32 = bf16[768,2048]{1,0:T(8,128)(2,1)S(1)} fusion(pred[768,192]{0,1:T(8,128)(4,1)S(1)} %fusion.10, bf16[192,1024]{1,0:T(8,128)(2,1)} %bitcast.53, bf16[192,1024]{1,0:T(8,128)(2,1)} %bitcast.54), kind=kOutput, calls=%fused_computation.42 | convolution fusion | flops 605552640 | bytes 4079616 | tf_op jit(solution)/shard_map/dot_general | solution.py:50
  6.5 0.2 slice.57
  6.7 0.2 select_reduce_fusion
  6.9 0.3 multiply_convert_fusion
  7.2 2.0 %pad_maximum_fusion = bf16[768,2048]{1,0:T(8,128)(2,1)} fusion(bf16[768,1024]{1,0:T(8,128)(2,1)S(1)} %multiply_convert_fusion, bf16[768,1024]{1,0:T(8,128)(2,1)S(1)} %slice.57), kind=kLoop, calls=%fused_computation | loop fusion | flops 6291456 | bytes 6291456 | tf_op jit(solution)/shard_map/concatenate | solution.py:53
  9.1 10.4 %all-to-all-start = ((bf16[16,48,2048]{2,1,0:T(8,128)(2,1)}), bf16[16,48,2048]{2,1,0:T(8,128)(2,1)S(1)}, u32[]{:S(2)}, u32[]{:S(2)}) async-start(bf16[16,48,2048]{2,1,0:T(8,128)(2,1)} %bitcast.5), calls=%async_computation | async-start | bytes 6291456 | tf_op jit(solution)/shard_map/all_to_all | solution.py:54
  19.5 2.9 %collective-permute-start.1 = (bf16[1024,256]{1,0:T(8,128)(2,1)}, bf16[1024,256]{1,0:T(8,128)(2,1)S(1)}, u32[]{:S(2)}, u32[]{:S(2)}) collective-permute-start(bf16[1024,256]{1,0:T(8,128)(2,1)} %bitcast.61), channel_id=1, source_target_pairs={{0,256},{16,272},{32,288},{48,304},{64,320},{80,336},{96,352},{112... | collective-permute-start | bytes 1572872 | tf_op jit(solution)/shard_map/ppermute | solution.py:12
  22.4 3.9 %collective-permute-start.2 = (bf16[1024,256]{1,0:T(8,128)(2,1)}, bf16[1024,256]{1,0:T(8,128)(2,1)}, u32[]{:S(2)}, u32[]{:S(2)}) collective-permute-start(bf16[1024,256]{1,0:T(8,128)(2,1)} %bitcast.58), channel_id=1, source_target_pairs={{0,256},{16,272},{32,288},{48,304},{64,320},{80,336},{96,352},{112... | collective-permute-start | bytes 1572872 | tf_op jit(solution)/shard_map/ppermute | solution.py:12
  26.3 2.9 %collective-permute-start = (bf16[256,1024]{1,0:T(8,128)(2,1)}, bf16[256,1024]{1,0:T(8,128)(2,1)}, u32[]{:S(2)}, u32[]{:S(2)}) collective-permute-start(bf16[256,1024]{1,0:T(8,128)(2,1)} %bitcast.56), channel_id=1, source_target_pairs={{0,256},{16,272},{32,288},{48,304},{64,320},{80,336},{96,352},{112... | collective-permute-start | bytes 1572872 | tf_op jit(solution)/shard_map/ppermute | solution.py:12
  29.2 7.1 %collective-permute-done.1 = bf16[1024,256]{1,0:T(8,128)(2,1)S(1)} collective-permute-done((bf16[1024,256]{1,0:T(8,128)(2,1)}, bf16[1024,256]{1,0:T(8,128)(2,1)S(1)}, u32[]{:S(2)}, u32[]{:S(2)}) %collective-permute-start.1) | collective-permute-done | bytes 524320 | tf_op jit(solution)/shard_map/ppermute | solution.py:12
  36.4 0.0 copy-start.5
  36.4 0.8 copy-done.5
  37.2 10.5 %collective-permute-done.2 = bf16[1024,256]{1,0:T(8,128)(2,1)} collective-permute-done((bf16[1024,256]{1,0:T(8,128)(2,1)}, bf16[1024,256]{1,0:T(8,128)(2,1)}, u32[]{:S(2)}, u32[]{:S(2)}) %collective-permute-start.2) | collective-permute-done | bytes 524320 | tf_op jit(solution)/shard_map/ppermute | solution.py:12
  47.7 42.8 %all-to-all-done = bf16[16,48,2048]{2,1,0:T(8,128)(2,1)S(1)} async-done(((bf16[16,48,2048]{2,1,0:T(8,128)(2,1)}), bf16[16,48,2048]{2,1,0:T(8,128)(2,1)S(1)}, u32[]{:S(2)}, u32[]{:S(2)}) %all-to-all-start) | async-done | bytes 3145760 | tf_op jit(solution)/shard_map/all_to_all | solution.py:54
  90.5 0.0 copy-start
  90.5 0.0 copy-start.2
  90.5 4.5 %fusion.20 = f32[768,1024]{0,1:T(8,128)S(1)} fusion(bf16[768,2048]{1,0:T(8,128)(2,1)S(1)} %bitcast.45, bf16[1024,256]{1,0:T(8,128)(2,1)} %collective-permute-done.2, bf16[1024,256]{1,0:T(8,128)(2,1)} %bitcast.59, bf16[1024,256]{1,0:T(8,128)(2,1)} %copy-done.5, bf16[1024,256]{1,0:T(8,128)(2,1)} %bitcast.62), kind=kOutput, calls=%fused_computation.38 | convolution fusion | flops 1619001344 | bytes 6815744 | tf_op jit(solution)/shard_map/dot_general | solution.py:67
  95.0 0.0 copy-start.3
  95.0 0.0 copy-start.4
  95.1 0.0 copy-start.6
  95.1 0.0 collective-permute-done
  95.1 0.0 copy-done
  95.1 0.0 copy-done.2
  95.1 3.6 %multiply_convert_fusion.3 = (bf16[768,512]{0,1:T(8,128)(2,1)S(1)}, bf16[768,512]{0,1:T(8,128)(2,1)S(1)}, bf16[768,512]{0,1:T(8,128)(2,1)}) fusion(f32[768,1024]{0,1:T(8,128)S(1)} %fusion.20, bf16[256,1024]{1,0:T(8,128)(2,1)} %collective-permute-done, bf16[256,1024]{1,0:T(8,128)(2,1)S(1)} %bitcast.57, bf16[768,2048]{1,0:T(8,128)(2,1)S(1)} %bitcast.46), kind=kOutput, calls=%fused_computation.9 | convolution fusion | flops 813301760 | bytes 8126464 | tf_op jit(solution)/shard_map/dot_general | solution.py:73
  98.7 0.0 copy-start.8
  98.7 0.0 copy-start.10
  98.7 0.0 copy-done.3
  98.7 0.0 copy-done.4
  98.7 0.0 copy-done.6
  98.7 4.4 %convolution_convert_fusion = bf16[768,1024]{1,0:T(8,128)(2,1)} fusion(bf16[768,512]{0,1:T(8,128)(2,1)S(1)} %get-tuple-element.5, bf16[768,512]{0,1:T(8,128)(2,1)S(1)} %get-tuple-element.4, bf16[1024,256]{1,0:T(8,128)(2,1)} %collective-permute-done.2, bf16[1024,256]{1,0:T(8,128)(2,1)S(1)} %bitcast.60, bf16[1024,256]{1,0:T(8,128)(2,1)S(1)} %copy-done.6, ...), kind=kOutput, calls=%fused_computation.3 | convolution fusion | flops 1622933504 | bytes 5242880 | tf_op jit(solution)/shard_map/dot_general | solution.py:79
  103.1 0.0 copy-done.8
  103.1 0.0 copy-done.10
  103.1 5.6 %all-to-all-start.1 = ((bf16[16,48,1024]{2,1,0:T(8,128)(2,1)}), bf16[16,48,1024]{2,1,0:T(8,128)(2,1)S(1)}, u32[]{:S(2)}, u32[]{:S(2)}) async-start(bf16[16,48,1024]{2,1,0:T(8,128)(2,1)} %bitcast.10), calls=%async_computation.1 | async-start | bytes 3145728 | tf_op jit(solution)/shard_map/all_to_all | solution.py:81
  108.8 0.0 copy-done.7
  108.8 2.1 %convolution_convert_fusion.1 = bf16[256,1024]{1,0:T(8,128)(2,1)S(1)} fusion(bf16[768,2048]{1,0:T(8,128)(2,1)} %bitcast.47, bf16[768,512]{0,1:T(8,128)(2,1)S(1)} %copy-done.7), kind=kOutput, calls=%fused_computation.12 | convolution fusion | flops 402915328 | bytes 2490368 | tf_op jit(solution)/shard_map/dot_general | solution.py:86
  110.9 0.0 copy-start.9
  110.9 3.0 %collective-permute-start.5 = (bf16[256,1024]{1,0:T(8,128)(2,1)S(1)}, bf16[256,1024]{1,0:T(8,128)(2,1)S(1)}, u32[]{:S(2)}, u32[]{:S(2)}) collective-permute-start(bf16[256,1024]{1,0:T(8,128)(2,1)S(1)} %convolution_convert_fusion.1), channel_id=1, source_target_pairs={{0,256},{16,272},{32,288},{48,304},{64,320},{80,336},{96,352},{112... | collective-permute-start | bytes 1572872 | tf_op jit(solution)/shard_map/ppermute | solution.py:12
  113.9 0.0 copy-done.1
  113.9 1.6 %convolution_convert_fusion.2 = bf16[1024,256]{1,0:T(8,128)(2,1)S(1)} fusion(bf16[768,2048]{1,0:T(8,128)(2,1)S(1)} %bitcast.48, bf16[768,512]{0,1:T(8,128)(2,1)} %copy-done.10), kind=kOutput, calls=%fused_computation.13 | convolution fusion | flops 402915328 | bytes 2490368 | tf_op jit(solution)/shard_map/dot_general | solution.py:85
  115.6 3.9 %collective-permute-start.4 = (bf16[1024,256]{1,0:T(8,128)(2,1)S(1)}, bf16[1024,256]{1,0:T(8,128)(2,1)S(1)}, u32[]{:S(2)}, u32[]{:S(2)}) collective-permute-start(bf16[1024,256]{1,0:T(8,128)(2,1)S(1)} %convolution_convert_fusion.2), channel_id=1, source_target_pairs={{0,256},{16,272},{32,288},{48,304},{64,320},{80,336},{96,352},{112... | collective-permute-start | bytes 1572872 | tf_op jit(solution)/shard_map/ppermute | solution.py:12
  119.5 0.0 copy-done.9
  119.5 0.6 convolution_convert_fusion.3
  120.2 0.0 copy-start.11
  120.2 3.0 %collective-permute-start.3 = (bf16[1024,256]{1,0:T(8,128)(2,1)S(1)}, bf16[1024,256]{1,0:T(8,128)(2,1)S(1)}, u32[]{:S(2)}, u32[]{:S(2)}) collective-permute-start(bf16[1024,256]{1,0:T(8,128)(2,1)S(1)} %convolution_convert_fusion.3), channel_id=1, source_target_pairs={{0,256},{16,272},{32,288},{48,304},{64,320},{80,336},{96,352},{112... | collective-permute-start | bytes 1572872 | tf_op jit(solution)/shard_map/ppermute | solution.py:12
  123.2 4.7 %collective-permute-done.5 = bf16[256,1024]{1,0:T(8,128)(2,1)S(1)} collective-permute-done((bf16[256,1024]{1,0:T(8,128)(2,1)S(1)}, bf16[256,1024]{1,0:T(8,128)(2,1)S(1)}, u32[]{:S(2)}, u32[]{:S(2)}) %collective-permute-start.5) | collective-permute-done | bytes 524320 | tf_op jit(solution)/shard_map/ppermute | solution.py:12
  127.8 1.4 fusion.36
  129.2 9.8 %collective-permute-done.4 = bf16[1024,256]{1,0:T(8,128)(2,1)S(1)} collective-permute-done((bf16[1024,256]{1,0:T(8,128)(2,1)S(1)}, bf16[1024,256]{1,0:T(8,128)(2,1)S(1)}, u32[]{:S(2)}, u32[]{:S(2)}) %collective-permute-start.4) | collective-permute-done | bytes 524320 | tf_op jit(solution)/shard_map/ppermute | solution.py:12
  139.1 0.0 copy-done.11
  139.1 1.4 fusion.29
  140.5 9.8 %collective-permute-done.3 = bf16[1024,256]{1,0:T(8,128)(2,1)S(1)} collective-permute-done((bf16[1024,256]{1,0:T(8,128)(2,1)S(1)}, bf16[1024,256]{1,0:T(8,128)(2,1)S(1)}, u32[]{:S(2)}, u32[]{:S(2)}) %collective-permute-start.3) | collective-permute-done | bytes 524320 | tf_op jit(solution)/shard_map/ppermute | solution.py:12
  150.3 1.4 fusion.26
  151.7 0.0 all-to-all-done.1
  151.7 1.2 fusion.4
  (7 shorter events, 0.1 us)
Async XLA Ops:
  9.1 81.4 %all-to-all-start = ((bf16[16,48,2048]{2,1,0:T(8,128)(2,1)}), bf16[16,48,2048]{2,1,0:T(8,128)(2,1)S(1)}, u32[]{:S(2)}, u32[]{:S(2)}) async-start(bf16[16,48,2048]{2,1,0:T(8,128)(2,1)} %bitcast.5), calls=%async_computation | async-start | bytes 6291456 | tf_op jit(solution)/shard_map/all_to_all | solution.py:54
  19.5 16.8 %collective-permute-start.1 = (bf16[1024,256]{1,0:T(8,128)(2,1)}, bf16[1024,256]{1,0:T(8,128)(2,1)S(1)}, u32[]{:S(2)}, u32[]{:S(2)}) collective-permute-start(bf16[1024,256]{1,0:T(8,128)(2,1)} %bitcast.61), channel_id=1, source_target_pairs={{0,256},{16,272},{32,288},{48,304},{64,320},{80,336},{96,352},{112... | collective-permute-start | bytes 1572872 | tf_op jit(solution)/shard_map/ppermute | solution.py:12
  22.4 25.3 %collective-permute-start.2 = (bf16[1024,256]{1,0:T(8,128)(2,1)}, bf16[1024,256]{1,0:T(8,128)(2,1)}, u32[]{:S(2)}, u32[]{:S(2)}) collective-permute-start(bf16[1024,256]{1,0:T(8,128)(2,1)} %bitcast.58), channel_id=1, source_target_pairs={{0,256},{16,272},{32,288},{48,304},{64,320},{80,336},{96,352},{112... | collective-permute-start | bytes 1572872 | tf_op jit(solution)/shard_map/ppermute | solution.py:12
  26.3 68.8 %collective-permute-start = (bf16[256,1024]{1,0:T(8,128)(2,1)}, bf16[256,1024]{1,0:T(8,128)(2,1)}, u32[]{:S(2)}, u32[]{:S(2)}) collective-permute-start(bf16[256,1024]{1,0:T(8,128)(2,1)} %bitcast.56), channel_id=1, source_target_pairs={{0,256},{16,272},{32,288},{48,304},{64,320},{80,336},{96,352},{112... | collective-permute-start | bytes 1572872 | tf_op jit(solution)/shard_map/ppermute | solution.py:12
  36.4 0.8 copy-start.5
  90.5 4.6 %copy-start = (bf16[16,48,2048]{2,1,0:T(8,128)(2,1)}, bf16[16,48,2048]{2,1,0:T(8,128)(2,1)S(1)}, u32[]{:S(2)}) copy-start(bf16[16,48,2048]{2,1,0:T(8,128)(2,1)S(1)} %all-to-all-done) | copy-start | bytes 9437188
  90.5 4.6 %copy-start.2 = (bf16[1,1,256,1024]{3,2,1,0:T(8,128)(2,1)S(1)}, bf16[1,1,256,1024]{3,2,1,0:T(8,128)(2,1)}, u32[]{:S(2)}) copy-start(bf16[1,1,256,1024]{3,2,1,0:T(8,128)(2,1)} %param.13) | copy-start | bytes 1572868
  95.0 3.6 %copy-start.3 = (bf16[1,1,1024,256]{3,2,1,0:T(8,128)(2,1)S(1)}, bf16[1,1,1024,256]{3,2,1,0:T(8,128)(2,1)}, u32[]{:S(2)}) copy-start(bf16[1,1,1024,256]{3,2,1,0:T(8,128)(2,1)} %param.12) | copy-start | bytes 1572868
  95.0 3.6 %copy-start.4 = (bf16[1,1,1024,256]{3,2,1,0:T(8,128)(2,1)S(1)}, bf16[1,1,1024,256]{3,2,1,0:T(8,128)(2,1)}, u32[]{:S(2)}) copy-start(bf16[1,1,1024,256]{3,2,1,0:T(8,128)(2,1)} %param.11) | copy-start | bytes 1572868
  95.1 3.6 %copy-start.6 = (bf16[1024,256]{1,0:T(8,128)(2,1)S(1)}, bf16[1024,256]{1,0:T(8,128)(2,1)}, u32[]{:S(2)}) copy-start(bf16[1024,256]{1,0:T(8,128)(2,1)} %copy-done.5) | copy-start | bytes 1572868
  98.7 4.5 %copy-start.8 = (bf16[768,512]{0,1:T(8,128)(2,1)}, bf16[768,512]{0,1:T(8,128)(2,1)S(1)}, u32[]{:S(2)}) copy-start(bf16[768,512]{0,1:T(8,128)(2,1)S(1)} %get-tuple-element.4) | copy-start | bytes 2359300
  98.7 4.5 %copy-start.10 = (bf16[768,512]{0,1:T(8,128)(2,1)}, bf16[768,512]{0,1:T(8,128)(2,1)S(1)}, u32[]{:S(2)}) copy-start(bf16[768,512]{0,1:T(8,128)(2,1)S(1)} %get-tuple-element.5) | copy-start | bytes 2359300
  103.1 5.6 %copy-start.7 = (bf16[768,512]{0,1:T(8,128)(2,1)S(1)}, bf16[768,512]{0,1:T(8,128)(2,1)}, u32[]{:S(2)}) copy-start(bf16[768,512]{0,1:T(8,128)(2,1)} %get-tuple-element.6) | copy-start | bytes 2359300
  103.1 48.6 %all-to-all-start.1 = ((bf16[16,48,1024]{2,1,0:T(8,128)(2,1)}), bf16[16,48,1024]{2,1,0:T(8,128)(2,1)S(1)}, u32[]{:S(2)}, u32[]{:S(2)}) async-start(bf16[16,48,1024]{2,1,0:T(8,128)(2,1)} %bitcast.10), calls=%async_computation.1 | async-start | bytes 3145728 | tf_op jit(solution)/shard_map/all_to_all | solution.py:81
  108.7 5.2 %copy-start.1 = (bf16[16,48,2048]{2,1,0:T(8,128)(2,1)S(1)}, bf16[16,48,2048]{2,1,0:T(8,128)(2,1)}, u32[]{:S(2)}) copy-start(bf16[16,48,2048]{2,1,0:T(8,128)(2,1)} %copy-done) | copy-start | bytes 9437188
  110.9 8.6 %copy-start.9 = (bf16[768,512]{0,1:T(8,128)(2,1)S(1)}, bf16[768,512]{0,1:T(8,128)(2,1)}, u32[]{:S(2)}) copy-start(bf16[768,512]{0,1:T(8,128)(2,1)} %copy-done.8) | copy-start | bytes 2359300
  110.9 16.9 %collective-permute-start.5 = (bf16[256,1024]{1,0:T(8,128)(2,1)S(1)}, bf16[256,1024]{1,0:T(8,128)(2,1)S(1)}, u32[]{:S(2)}, u32[]{:S(2)}) collective-permute-start(bf16[256,1024]{1,0:T(8,128)(2,1)S(1)} %convolution_convert_fusion.1), channel_id=1, source_target_pairs={{0,256},{16,272},{32,288},{48,304},{64,320},{80,336},{96,352},{112... | collective-permute-start | bytes 1572872 | tf_op jit(solution)/shard_map/ppermute | solution.py:12
  115.6 23.5 %collective-permute-start.4 = (bf16[1024,256]{1,0:T(8,128)(2,1)S(1)}, bf16[1024,256]{1,0:T(8,128)(2,1)S(1)}, u32[]{:S(2)}, u32[]{:S(2)}) collective-permute-start(bf16[1024,256]{1,0:T(8,128)(2,1)S(1)} %convolution_convert_fusion.2), channel_id=1, source_target_pairs={{0,256},{16,272},{32,288},{48,304},{64,320},{80,336},{96,352},{112... | collective-permute-start | bytes 1572872 | tf_op jit(solution)/shard_map/ppermute | solution.py:12
  120.2 18.9 %copy-start.11 = (bf16[768,512]{0,1:T(8,128)(2,1)S(1)}, bf16[768,512]{0,1:T(8,128)(2,1)}, u32[]{:S(2)}) copy-start(bf16[768,512]{0,1:T(8,128)(2,1)} %copy-done.10) | copy-start | bytes 2359300
  120.2 30.1 %collective-permute-start.3 = (bf16[1024,256]{1,0:T(8,128)(2,1)S(1)}, bf16[1024,256]{1,0:T(8,128)(2,1)S(1)}, u32[]{:S(2)}, u32[]{:S(2)}) collective-permute-start(bf16[1024,256]{1,0:T(8,128)(2,1)S(1)} %convolution_convert_fusion.3), channel_id=1, source_target_pairs={{0,256},{16,272},{32,288},{48,304},{64,320},{80,336},{96,352},{112... | collective-permute-start | bytes 1572872 | tf_op jit(solution)/shard_map/ppermute | solution.py:12

commit v9 on v7

--- a/solution.py
+++ b/solution.py
@@ -51,40 +51,59 @@
     slot_in = picked[:, :width].astype(jnp.bfloat16)
     slot_grad = (picked[:, width:] * pair_gate[:, None]).astype(jnp.bfloat16)
     send = jnp.concatenate([slot_in, slot_grad], axis=1).reshape(experts, cap, 2 * width)
-    recv = lax.all_to_all(send, "expert", split_axis=0, concat_axis=0, tiled=True)
+    tail = cap // 4
+    recv1 = lax.all_to_all(send[:, :tail], "expert", split_axis=0, concat_axis=0, tiled=True)
+    recv0 = lax.all_to_all(send[:, tail:], "expert", split_axis=0, concat_axis=0, tiled=True)
     sel_t = lax.optimization_barrier(
         jnp.transpose(hit.reshape(rows, tok, topk).any(axis=2)).astype(jnp.bfloat16)
     )
-    recv = recv.reshape(rows, 2 * width)
 
     full_gu = jnp.concatenate([own_gate, other_gate, own_up, other_up], axis=1)
     full_down = jnp.concatenate([own_down, other_down], axis=0)
-    rows_in = recv[:, :width]
-    rows_grad = recv[:, width:]
     hidden = 2 * half
     contract_last = (((1,), (1,)), ((), ()))
     contract_rows = (((0,), (0,)), ((), ()))
-    gu_pre = jnp.dot(rows_in, full_gu, preferred_element_type=jnp.float32)
-    gate_pre = gu_pre[:, :hidden]
-    up_pre = gu_pre[:, hidden:]
-    sigmoid_g = jax.nn.sigmoid(gate_pre)
-    swish_val = gate_pre * sigmoid_g
-    act = (swish_val * up_pre).astype(jnp.bfloat16)
-    act_grad = lax.dot_general(rows_grad, full_down, contract_last, preferred_element_type=jnp.float32)
-    gate_grad = (act_grad * up_pre * sigmoid_g * (1.0 + gate_pre * (1.0 - sigmoid_g))).astype(
-        jnp.bfloat16
+
+    def chunk(recv_part):
+        part = recv_part.reshape(-1, 2 * width)
+        rows_in = part[:, :width]
+        rows_grad = part[:, width:]
+        gu_pre = jnp.dot(rows_in, full_gu, preferred_element_type=jnp.float32)
+        gate_pre = gu_pre[:, :hidden]
+        up_pre = gu_pre[:, hidden:]
+        sigmoid_g = jax.nn.sigmoid(gate_pre)
+        swish_val = gate_pre * sigmoid_g
+        act = (swish_val * up_pre).astype(jnp.bfloat16)
+        act_grad = lax.dot_general(
+            rows_grad, full_down, contract_last, preferred_element_type=jnp.float32
+        )
+        gate_grad = (act_grad * up_pre * sigmoid_g * (1.0 + gate_pre * (1.0 - sigmoid_g))).astype(
+            jnp.bfloat16
+        )
+        up_grad = (act_grad * swish_val).astype(jnp.bfloat16)
+        gu_grad = jnp.concatenate([gate_grad, up_grad], axis=1)
+        pair_grad = lax.dot_general(
+            gu_grad, full_gu, contract_last, preferred_element_type=jnp.float32
+        )
+        return rows_in, rows_grad, gate_grad, up_grad, act, pair_grad.astype(jnp.bfloat16)
+
+    c0 = chunk(recv0)
+    c1 = chunk(recv1)
+    back = jnp.concatenate(
+        [c1[5].reshape(experts, tail, width), c0[5].reshape(experts, cap - tail, width)], axis=1
     )
-    up_grad = (act_grad * swish_val).astype(jnp.bfloat16)
-    gu_grad = jnp.concatenate([gate_grad, up_grad], axis=1)
-    pair_grad = lax.dot_general(gu_grad, full_gu, contract_last, preferred_element_type=jnp.float32)
-    back = pair_grad.astype(jnp.bfloat16).reshape(experts, cap, width)
     home = lax.all_to_all(back, "expert", split_axis=0, concat_axis=0, tiled=True)
+
     def grad_cols(lo, hi):
-        return (
-            lax.dot_general(rows_in, gate_grad[:, lo:hi], contract_rows, preferred_element_type=jnp.float32),
-            lax.dot_general(rows_in, up_grad[:, lo:hi], contract_rows, preferred_element_type=jnp.float32),
-            lax.dot_general(act[:, lo:hi], rows_grad, contract_rows, preferred_element_type=jnp.float32),
-        )
+        total = None
+        for rows_in, rows_grad, gate_grad, up_grad, act, _ in (c0, c1):
+            terms = (
+                lax.dot_general(rows_in, gate_grad[:, lo:hi], contract_rows, preferred_element_type=jnp.float32),
+                lax.dot_general(rows_in, up_grad[:, lo:hi], contract_rows, preferred_element_type=jnp.float32),
+                lax.dot_general(act[:, lo:hi], rows_grad, contract_rows, preferred_element_type=jnp.float32),
+            )
+            total = terms if total is None else tuple(x + y for x, y in zip(total, terms))
+        return total
 
     peer_terms = grad_cols(half, hidden)
     peer_g, peer_u, peer_d = partner(

time: 154 us -> 178 us (1.16)
  local copies, waits for them, and re-layouts: 3.53 us -> 15.3 us
  matrix products: 24.5 us -> 30.9 us
  starting transfers between devices: 35.5 us -> 38.6 us
  waiting for transfers between devices: 84.8 us -> 87.3 us
    ppermute x6, waiting for transfers between devices: 42 us -> 52.4 us  [partner(): return lax.ppermute(value, axis, pairs)]
    all_to_all x1 -> x2, waiting for transfers between devices: 42.8 us -> 34.9 us  [the longest x1 25.7 us: per_device(): lax.all_to_all(send[:, :tail], 'expert', split_axis=0, concat_axis=0, til...]
    reshape x0 -> x4, local copies, waits for them, and re-layouts: none -> 6.69 us  [the longest x2 3.39 us: chunk(): part = recv_part.reshape(-1, 2 * width)]
    dot_general x3 -> x6, matrix products: 12.5 us -> 17.5 us  [the longest x2 7.06 us: chunk(): lax.dot_general(gu_grad, full_gu, contract_last, preferred_element_type=j...]
    all_to_all x1 -> x2, starting transfers between devices: 10.4 us -> 14.5 us  [the longest x1 10.9 us: per_device(): lax.all_to_all(send[:, :tail], 'expert', split_axis=0, concat_axis=0, til...]
    slice x1 -> x3, local copies, waits for them, and re-layouts: 0.22 us -> 3.76 us  [the longest x1 2.47 us: per_device(): send[:, tail:]]
    unnamed x26 -> x30, local copies, waits for them, and re-layouts: 2.43 us -> 3.97 us
    dot_general x2 -> x4, matrix products: 3.52 us -> 4.49 us  [grad_cols(): lax.dot_general(act[:, lo:hi], rows_grad, contract_rows, preferred_elemen...]
  transfers between devices with their start and end apart: 8 -> 9, of which waited for: 6 -> 8; matrix products, arithmetic and copies ran while one was open for 9% -> 14% of each run, Pallas kernels for 0% -> 0%
where the time goes in v9:
time: 178 us; the launch traced here: 177 us
  waiting for transfers between devices  87.3 us (49%)
  starting transfers between devices  38.6 us (22%)
  matrix products  30.9 us (17%)
  local copies, waits for them, and re-layouts  15.3 us (9%)
  other arithmetic  4.31 us (2%)
    ppermute x6, waiting for transfers between devices, partner(): return lax.ppermute(value, axis, pairs)  52.4 us
    all_to_all x1, waiting for transfers between devices, per_device(): lax.all_to_all(send[:, :tail], 'expert', split_axis=0, concat_axis=0, til...  25.7 us
    ppermute x6, starting transfers between devices, partner(): return lax.ppermute(value, axis, pairs)  18.4 us
    all_to_all x1, starting transfers between devices, per_device(): lax.all_to_all(send[:, :tail], 'expert', split_axis=0, concat_axis=0, til...  10.9 us
    all_to_all x1, waiting for transfers between devices, per_device(): lax.all_to_all(send[:, tail:], 'expert', split_axis=0, concat_axis=0, til...  9.25 us
    dot_general x2, matrix products, chunk(): lax.dot_general(gu_grad, full_gu, contract_last, preferred_element_type=j...  7.06 us
    all_to_all x1, starting transfers between devices, per_device(): lax.all_to_all(back, 'expert', split_axis=0, concat_axis=0, tiled=True)  5.67 us
    dot_general x2, matrix products, chunk(): gu_pre = jnp.dot(rows_in, full_gu, preferred_element_type=jnp.float32)  5.49 us
  transfers between devices with their start and end apart: 9, of which 8 were waited for; matrix products, arithmetic and copies ran while one was open for 14% of the time, Pallas kernels for 0%

profile of v9, /device:TPU:1, one launch (start us, length us, event | category | flops | bytes accessed | tf_op | source)
XLA Modules:
  0.0 177.4 jit_solution(16079862826931270998)
XLA Ops:
  0.6 0.8 copy.17
  1.4 0.1 eq.49
  1.6 0.1 eq.45
  1.7 0.9 reduce-window.6
  2.6 0.2 slice_reduce_fusion
  2.9 0.1 fusion.73
  3.0 0.1 reduce_sum.21
  3.1 0.1 copy.21
  3.2 0.2 fusion.9
  3.4 0.8 copy.22
  4.2 0.1 broadcast_in_dim.30
  4.4 2.1 %fusion.19 = f32[768,2048]{1,0:T(8,128)S(1)} fusion(pred[768,192]{0,1:T(8,128)(4,1)S(1)} %fusion.9, bf16[192,1024]{1,0:T(8,128)(2,1)} %bitcast.45, bf16[192,1024]{1,0:T(8,128)(2,1)} %bitcast.46), kind=kOutput, calls=%fused_computation.40 | convolution fusion | flops 605552640 | bytes 7225344 | tf_op jit(solution)/shard_map/dot_general | solution.py:50
  6.5 0.2 slice.219
  6.8 0.2 select_reduce_fusion
  7.0 0.2 fusion
  7.2 0.3 pad_maximum_fusion
  7.5 1.1 slice.108
  8.6 10.9 %all-to-all-start = ((bf16[16,12,2048]{2,1,0:T(8,128)(2,1)}), bf16[16,12,2048]{2,1,0:T(8,128)(2,1)}, u32[]{:S(2)}, u32[]{:S(2)}) async-start(bf16[16,12,2048]{2,1,0:T(8,128)(2,1)} %slice.108), calls=%async_computation | async-start | bytes 2097152 | tf_op jit(solution)/shard_map/all_to_all | solution.py:55
  19.5 2.5 %slice.113 = bf16[16,36,2048]{2,1,0:T(8,128)(2,1)} slice(bf16[16,48,2048]{2,1,0:T(8,128)(2,1)S(1)} %bitcast.43), slice={[0:16], [12:48], [0:2048]} | slice | bytes 4718592 | tf_op jit(solution)/shard_map/slice | solution.py:56
  22.0 25.7 %all-to-all-done = bf16[16,12,2048]{2,1,0:T(8,128)(2,1)} async-done(((bf16[16,12,2048]{2,1,0:T(8,128)(2,1)}), bf16[16,12,2048]{2,1,0:T(8,128)(2,1)}, u32[]{:S(2)}, u32[]{:S(2)}) %all-to-all-start) | async-done | bytes 786464 | tf_op jit(solution)/shard_map/all_to_all | solution.py:55
  47.6 3.6 %all-to-all-start.1 = ((bf16[16,36,2048]{2,1,0:T(8,128)(2,1)}), bf16[16,36,2048]{2,1,0:T(8,128)(2,1)S(1)}, u32[]{:S(2)}, u32[]{:S(2)}) async-start(bf16[16,36,2048]{2,1,0:T(8,128)(2,1)} %slice.113), calls=%async_computation.1 | async-start | bytes 5242880 | tf_op jit(solution)/shard_map/all_to_all | solution.py:56
  51.3 2.3 %collective-permute-start.1 = (bf16[1024,256]{1,0:T(8,128)(2,1)}, bf16[1024,256]{1,0:T(8,128)(2,1)}, u32[]{:S(2)}, u32[]{:S(2)}) collective-permute-start(bf16[1024,256]{1,0:T(8,128)(2,1)} %bitcast.7), channel_id=1, source_target_pairs={{0,256},{16,272},{32,288},{48,304},{64,320},{80,336},{96,352},{112... | collective-permute-start | bytes 1572872 | tf_op jit(solution)/shard_map/ppermute | solution.py:12
  53.6 4.5 %collective-permute-start.2 = (bf16[1024,256]{1,0:T(8,128)(2,1)}, bf16[1024,256]{1,0:T(8,128)(2,1)}, u32[]{:S(2)}, u32[]{:S(2)}) collective-permute-start(bf16[1024,256]{1,0:T(8,128)(2,1)} %bitcast.8), channel_id=1, source_target_pairs={{0,256},{16,272},{32,288},{48,304},{64,320},{80,336},{96,352},{112... | collective-permute-start | bytes 1572872 | tf_op jit(solution)/shard_map/ppermute | solution.py:12
  58.1 2.3 %collective-permute-start = (bf16[256,1024]{1,0:T(8,128)(2,1)}, bf16[256,1024]{1,0:T(8,128)(2,1)}, u32[]{:S(2)}, u32[]{:S(2)}) collective-permute-start(bf16[256,1024]{1,0:T(8,128)(2,1)} %bitcast.6), channel_id=1, source_target_pairs={{0,256},{16,272},{32,288},{48,304},{64,320},{80,336},{96,352},{112... | collective-permute-start | bytes 1572872 | tf_op jit(solution)/shard_map/ppermute | solution.py:12
  60.4 0.7 convert_bitcast_fusion
  61.1 1.3 reshape.69
  62.4 6.1 %collective-permute-done.1 = bf16[1024,256]{1,0:T(8,128)(2,1)} collective-permute-done((bf16[1024,256]{1,0:T(8,128)(2,1)}, bf16[1024,256]{1,0:T(8,128)(2,1)}, u32[]{:S(2)}, u32[]{:S(2)}) %collective-permute-start.1) | collective-permute-done | bytes 524320 | tf_op jit(solution)/shard_map/ppermute | solution.py:12
  68.6 11.2 %collective-permute-done.2 = bf16[1024,256]{1,0:T(8,128)(2,1)} collective-permute-done((bf16[1024,256]{1,0:T(8,128)(2,1)}, bf16[1024,256]{1,0:T(8,128)(2,1)}, u32[]{:S(2)}, u32[]{:S(2)}) %collective-permute-start.2) | collective-permute-done | bytes 524320 | tf_op jit(solution)/shard_map/ppermute | solution.py:12
  79.8 2.1 %fusion.63 = f32[192,1024]{1,0:T(8,128)S(1)} fusion(bf16[192,2048]{1,0:T(8,128)(2,1)S(1)} %reshape.69, bf16[1024,256]{1,0:T(8,128)(2,1)} %collective-permute-done.2, bf16[1024,256]{1,0:T(8,128)(2,1)} %bitcast.8, bf16[1024,256]{1,0:T(8,128)(2,1)} %collective-permute-done.1, bf16[1024,256]{1,0:T(8,128)(2,1)} %bitcast.7), kind=kOutput, calls=%fused_computation.81 | convolution fusion | flops 411041792 | bytes 3276800 | tf_op jit(solution)/shard_map/dot_general | solution.py:71
  81.9 9.1 %collective-permute-done = bf16[256,1024]{1,0:T(8,128)(2,1)} collective-permute-done((bf16[256,1024]{1,0:T(8,128)(2,1)}, bf16[256,1024]{1,0:T(8,128)(2,1)}, u32[]{:S(2)}, u32[]{:S(2)}) %collective-permute-start) | collective-permute-done | bytes 524320 | tf_op jit(solution)/shard_map/ppermute | solution.py:12
  91.0 2.5 %multiply_convert_fusion.8 = (bf16[192,512]{1,0:T(8,128)(2,1)S(1)}, bf16[192,512]{1,0:T(8,128)(2,1)S(1)}, bf16[192,512]{1,0:T(8,128)(2,1)}) fusion(f32[192,1024]{1,0:T(8,128)S(1)} %fusion.63, bf16[256,1024]{1,0:T(8,128)(2,1)} %collective-permute-done, bf16[256,1024]{1,0:T(8,128)(2,1)} %bitcast.6, bf16[192,2048]{1,0:T(8,128)(2,1)S(1)} %reshape.69), kind=kOutput, calls=%fused_computation.58 | convolution fusion | flops 204898304 | bytes 2818048 | tf_op jit(solution)/shard_map/dot_general | solution.py:77
  93.5 0.7 copy-done.5
  94.3 3.1 %convolution_convert_fusion.2 = bf16[192,1024]{1,0:T(8,128)(2,1)} fusion(bf16[192,512]{1,0:T(8,128)(2,1)S(1)} %get-tuple-element.8, bf16[192,512]{1,0:T(8,128)(2,1)S(1)} %get-tuple-element.7, bf16[1024,256]{1,0:T(8,128)(2,1)} %collective-permute-done.2, bf16[1024,256]{1,0:T(8,128)(2,1)} %bitcast.8, bf16[1024,256]{1,0:T(8,128)(2,1)} %collective-permute-done.1, ...), kind=kOutput, calls=%fused_computation.17 | convolution fusion | flops 412024832 | bytes 2883584 | tf_op jit(solution)/shard_map/dot_general | solution.py:85
  97.4 1.9 %reshape.70 = bf16[16,12,1024]{2,1,0:T(8,128)(2,1)} reshape(bf16[192,1024]{1,0:T(8,128)(2,1)} %convolution_convert_fusion.2) | data formatting | bytes 786432 | tf_op jit(solution)/shard_map/reshape | solution.py:93
  99.2 2.2 %fusion.46 = f32[256,1024]{1,0:T(8,128)} fusion(bf16[192,2048]{1,0:T(8,128)(2,1)S(1)} %reshape.69, bf16[192,512]{1,0:T(8,128)(2,1)} %get-tuple-element.9), kind=kOutput, calls=%fused_computation.63 | convolution fusion | flops 100663296 | bytes 1540096 | tf_op jit(solution)/shard_map/dot_general | solution.py:103
  101.4 9.2 %all-to-all-done.1 = bf16[16,36,2048]{2,1,0:T(8,128)(2,1)S(1)} async-done(((bf16[16,36,2048]{2,1,0:T(8,128)(2,1)}), bf16[16,36,2048]{2,1,0:T(8,128)(2,1)S(1)}, u32[]{:S(2)}, u32[]{:S(2)}) %all-to-all-start.1) | async-done | bytes 2359328 | tf_op jit(solution)/shard_map/all_to_all | solution.py:56
  110.7 2.1 %reshape.71 = bf16[576,2048]{1,0:T(8,128)(2,1)} reshape(bf16[16,36,2048]{2,1,0:T(8,128)(2,1)S(1)} %all-to-all-done.1) | data formatting | bytes 4718592 | tf_op jit(solution)/shard_map/reshape | solution.py:68
  112.7 3.4 %fusion.28 = f32[576,1024]{1,0:T(8,128)S(1)} fusion(bf16[576,2048]{1,0:T(8,128)(2,1)} %reshape.71, bf16[1024,256]{1,0:T(8,128)(2,1)} %collective-permute-done.2, bf16[1024,256]{1,0:T(8,128)(2,1)} %bitcast.8, bf16[1024,256]{1,0:T(8,128)(2,1)} %collective-permute-done.1, bf16[1024,256]{1,0:T(8,128)(2,1)} %bitcast.7), kind=kOutput, calls=%fused_computation.49 | convolution fusion | flops 1216348160 | bytes 5636096 | tf_op jit(solution)/shard_map/dot_general | solution.py:71
  116.2 2.5 %multiply_convert_fusion.2 = (bf16[576,512]{1,0:T(8,128)(2,1)S(1)}, bf16[576,512]{1,0:T(8,128)(2,1)S(1)}, bf16[576,512]{1,0:T(8,128)(2,1)S(1)}) fusion(f32[576,1024]{1,0:T(8,128)S(1)} %fusion.28, bf16[256,1024]{1,0:T(8,128)(2,1)} %collective-permute-done, bf16[256,1024]{1,0:T(8,128)(2,1)} %bitcast.6, bf16[576,2048]{1,0:T(8,128)(2,1)S(1)} %copy-done), kind=kOutput, calls=%fused_computation.24 | convolution fusion | flops 610500608 | bytes 6356992 | tf_op jit(solution)/shard_map/dot_general | solution.py:77
  118.7 0.8 copy-done.10
  119.5 0.2 copy-done.12
  119.7 4.0 %convolution_convert_fusion = bf16[576,1024]{1,0:T(8,128)(2,1)} fusion(bf16[576,512]{1,0:T(8,128)(2,1)S(1)} %get-tuple-element.5, bf16[576,512]{1,0:T(8,128)(2,1)S(1)} %get-tuple-element.4, bf16[1024,256]{1,0:T(8,128)(2,1)} %collective-permute-done.2, bf16[1024,256]{1,0:T(8,128)(2,1)} %bitcast.8, bf16[1024,256]{1,0:T(8,128)(2,1)} %collective-permute-done.1, ...), kind=kOutput, calls=%fused_computation.6 | convolution fusion | flops 1219297280 | bytes 4456448 | tf_op jit(solution)/shard_map/dot_general | solution.py:85
  123.6 1.4 reshape.72
  125.1 1.6 pad_maximum_fusion.2
  126.7 5.7 %all-to-all-start.2 = ((bf16[16,48,1024]{2,1,0:T(8,128)(2,1)}), bf16[16,48,1024]{2,1,0:T(8,128)(2,1)S(1)}, u32[]{:S(2)}, u32[]{:S(2)}) async-start(bf16[16,48,1024]{2,1,0:T(8,128)(2,1)} %pad_maximum_fusion.2), calls=%async_computation.2 | async-start | bytes 3145728 | tf_op jit(solution)/shard_map/all_to_all | solution.py:95
  132.4 0.3 fusion.44
  132.7 0.4 fusion.57
  133.1 0.3 fusion.55
  133.5 0.3 fusion.61
  133.8 0.4 fusion.59
  134.2 0.6 copy-done.1
  134.8 0.6 fusion.3
  135.4 2.4 %collective-permute-start.5 = (bf16[256,1024]{1,0:T(8,128)(2,1)S(1)}, bf16[256,1024]{1,0:T(8,128)(2,1)S(1)}, u32[]{:S(2)}, u32[]{:S(2)}) collective-permute-start(bf16[256,1024]{1,0:T(8,128)(2,1)S(1)} %fusion.3), channel_id=1, source_target_pairs={{0,256},{16,272},{32,288},{48,304},{64,320},{80,336},{96,352},{112... | collective-permute-start | bytes 1572872 | tf_op jit(solution)/shard_map/ppermute | solution.py:12
  137.8 0.6 fusion.2
  138.5 4.6 %collective-permute-start.4 = (bf16[1024,256]{1,0:T(8,128)(2,1)S(1)}, bf16[1024,256]{1,0:T(8,128)(2,1)S(1)}, u32[]{:S(2)}, u32[]{:S(2)}) collective-permute-start(bf16[1024,256]{1,0:T(8,128)(2,1)S(1)} %fusion.2), channel_id=1, source_target_pairs={{0,256},{16,272},{32,288},{48,304},{64,320},{80,336},{96,352},{112... | collective-permute-start | bytes 1572872 | tf_op jit(solution)/shard_map/ppermute | solution.py:12
  143.1 0.6 fusion.1
  143.8 2.3 %collective-permute-start.3 = (bf16[1024,256]{1,0:T(8,128)(2,1)S(1)}, bf16[1024,256]{1,0:T(8,128)(2,1)S(1)}, u32[]{:S(2)}, u32[]{:S(2)}) collective-permute-start(bf16[1024,256]{1,0:T(8,128)(2,1)S(1)} %fusion.1), channel_id=1, source_target_pairs={{0,256},{16,272},{32,288},{48,304},{64,320},{80,336},{96,352},{112... | collective-permute-start | bytes 1572872 | tf_op jit(solution)/shard_map/ppermute | solution.py:12
  146.1 6.2 %collective-permute-done.5 = bf16[256,1024]{1,0:T(8,128)(2,1)S(1)} collective-permute-done((bf16[256,1024]{1,0:T(8,128)(2,1)S(1)}, bf16[256,1024]{1,0:T(8,128)(2,1)S(1)}, u32[]{:S(2)}, u32[]{:S(2)}) %collective-permute-start.5) | collective-permute-done | bytes 524320 | tf_op jit(solution)/shard_map/ppermute | solution.py:12
  152.3 1.4 fusion.16
  153.7 9.8 %collective-permute-done.4 = bf16[1024,256]{1,0:T(8,128)(2,1)S(1)} collective-permute-done((bf16[1024,256]{1,0:T(8,128)(2,1)S(1)}, bf16[1024,256]{1,0:T(8,128)(2,1)S(1)}, u32[]{:S(2)}, u32[]{:S(2)}) %collective-permute-start.4) | collective-permute-done | bytes 524320 | tf_op jit(solution)/shard_map/ppermute | solution.py:12
  163.5 1.4 fusion.37
  165.0 9.8 %collective-permute-done.3 = bf16[1024,256]{1,0:T(8,128)(2,1)S(1)} collective-permute-done((bf16[1024,256]{1,0:T(8,128)(2,1)S(1)}, bf16[1024,256]{1,0:T(8,128)(2,1)S(1)}, u32[]{:S(2)}, u32[]{:S(2)}) %collective-permute-start.3) | collective-permute-done | bytes 524320 | tf_op jit(solution)/shard_map/ppermute | solution.py:12
  174.8 1.4 fusion.34
  176.2 1.2 fusion.4
  (29 shorter events, 0.2 us)
Async XLA Ops:
  8.6 39.1 %all-to-all-start = ((bf16[16,12,2048]{2,1,0:T(8,128)(2,1)}), bf16[16,12,2048]{2,1,0:T(8,128)(2,1)}, u32[]{:S(2)}, u32[]{:S(2)}) async-start(bf16[16,12,2048]{2,1,0:T(8,128)(2,1)} %slice.108), calls=%async_computation | async-start | bytes 2097152 | tf_op jit(solution)/shard_map/all_to_all | solution.py:55
  47.6 63.0 %all-to-all-start.1 = ((bf16[16,36,2048]{2,1,0:T(8,128)(2,1)}), bf16[16,36,2048]{2,1,0:T(8,128)(2,1)S(1)}, u32[]{:S(2)}, u32[]{:S(2)}) async-start(bf16[16,36,2048]{2,1,0:T(8,128)(2,1)} %slice.113), calls=%async_computation.1 | async-start | bytes 5242880 | tf_op jit(solution)/shard_map/all_to_all | solution.py:56
  51.3 17.3 %collective-permute-start.1 = (bf16[1024,256]{1,0:T(8,128)(2,1)}, bf16[1024,256]{1,0:T(8,128)(2,1)}, u32[]{:S(2)}, u32[]{:S(2)}) collective-permute-start(bf16[1024,256]{1,0:T(8,128)(2,1)} %bitcast.7), channel_id=1, source_target_pairs={{0,256},{16,272},{32,288},{48,304},{64,320},{80,336},{96,352},{112... | collective-permute-start | bytes 1572872 | tf_op jit(solution)/shard_map/ppermute | solution.py:12
  53.6 26.2 %collective-permute-start.2 = (bf16[1024,256]{1,0:T(8,128)(2,1)}, bf16[1024,256]{1,0:T(8,128)(2,1)}, u32[]{:S(2)}, u32[]{:S(2)}) collective-permute-start(bf16[1024,256]{1,0:T(8,128)(2,1)} %bitcast.8), channel_id=1, source_target_pairs={{0,256},{16,272},{32,288},{48,304},{64,320},{80,336},{96,352},{112... | collective-permute-start | bytes 1572872 | tf_op jit(solution)/shard_map/ppermute | solution.py:12
  58.1 33.0 %collective-permute-start = (bf16[256,1024]{1,0:T(8,128)(2,1)}, bf16[256,1024]{1,0:T(8,128)(2,1)}, u32[]{:S(2)}, u32[]{:S(2)}) collective-permute-start(bf16[256,1024]{1,0:T(8,128)(2,1)} %bitcast.6), channel_id=1, source_target_pairs={{0,256},{16,272},{32,288},{48,304},{64,320},{80,336},{96,352},{112... | collective-permute-start | bytes 1572872 | tf_op jit(solution)/shard_map/ppermute | solution.py:12
  93.5 0.7 copy-start.5
  93.5 0.7 copy-start.7
  112.7 3.4 %copy-start = (bf16[576,2048]{1,0:T(8,128)(2,1)S(1)}, bf16[576,2048]{1,0:T(8,128)(2,1)}, u32[]{:S(2)}) copy-start(bf16[576,2048]{1,0:T(8,128)(2,1)} %reshape.71) | copy-start | bytes 7077892
  118.6 0.8 copy-start.10
  118.6 1.0 copy-start.12
  123.6 1.4 copy-start.2
  126.7 5.7 %copy-start.9 = (bf16[192,512]{1,0:T(8,128)(2,1)S(1)}, bf16[192,512]{1,0:T(8,128)(2,1)}, u32[]{:S(2)}) copy-start(bf16[192,512]{1,0:T(8,128)(2,1)} %get-tuple-element.9) | copy-start | bytes 589828
  126.7 6.0 %copy-start.8 = (bf16[192,512]{1,0:T(8,128)(2,1)S(1)}, bf16[192,512]{1,0:T(8,128)(2,1)}, u32[]{:S(2)}) copy-start(bf16[192,512]{1,0:T(8,128)(2,1)} %copy-done.7) | copy-start | bytes 589828
  126.7 49.5 %all-to-all-start.2 = ((bf16[16,48,1024]{2,1,0:T(8,128)(2,1)}), bf16[16,48,1024]{2,1,0:T(8,128)(2,1)S(1)}, u32[]{:S(2)}, u32[]{:S(2)}) async-start(bf16[16,48,1024]{2,1,0:T(8,128)(2,1)} %pad_maximum_fusion.2), calls=%async_computation.2 | async-start | bytes 3145728 | tf_op jit(solution)/shard_map/all_to_all | solution.py:95
  132.4 1.1 copy-start.6
  133.1 1.7 copy-start.1
  133.8 4.0 %copy-start.13 = (bf16[576,512]{1,0:T(8,128)(2,1)S(1)}, bf16[576,512]{1,0:T(8,128)(2,1)}, u32[]{:S(2)}) copy-start(bf16[576,512]{1,0:T(8,128)(2,1)} %copy-done.12) | copy-start | bytes 1769476
  135.4 7.7 %copy-start.11 = (bf16[576,512]{1,0:T(8,128)(2,1)S(1)}, bf16[576,512]{1,0:T(8,128)(2,1)}, u32[]{:S(2)}) copy-start(bf16[576,512]{1,0:T(8,128)(2,1)} %copy-done.10) | copy-start | bytes 1769476
  135.4 16.9 %collective-permute-start.5 = (bf16[256,1024]{1,0:T(8,128)(2,1)S(1)}, bf16[256,1024]{1,0:T(8,128)(2,1)S(1)}, u32[]{:S(2)}, u32[]{:S(2)}) collective-permute-start(bf16[256,1024]{1,0:T(8,128)(2,1)S(1)} %fusion.3), channel_id=1, source_target_pairs={{0,256},{16,272},{32,288},{48,304},{64,320},{80,336},{96,352},{112... | collective-permute-start | bytes 1572872 | tf_op jit(solution)/shard_map/ppermute | solution.py:12
  138.5 13.8 %copy-start.4 = (f32[256,1024]{1,0:T(8,128)S(1)}, f32[256,1024]{1,0:T(8,128)}, u32[]{:S(2)}) copy-start(f32[256,1024]{1,0:T(8,128)} %fusion.46) | copy-start | bytes 3145732
  138.5 25.1 %collective-permute-start.4 = (bf16[1024,256]{1,0:T(8,128)(2,1)S(1)}, bf16[1024,256]{1,0:T(8,128)(2,1)S(1)}, u32[]{:S(2)}, u32[]{:S(2)}) collective-permute-start(bf16[1024,256]{1,0:T(8,128)(2,1)S(1)} %fusion.2), channel_id=1, source_target_pairs={{0,256},{16,272},{32,288},{48,304},{64,320},{80,336},{96,352},{112... | collective-permute-start | bytes 1572872 | tf_op jit(solution)/shard_map/ppermute | solution.py:12
  143.8 31.0 %collective-permute-start.3 = (bf16[1024,256]{1,0:T(8,128)(2,1)S(1)}, bf16[1024,256]{1,0:T(8,128)(2,1)S(1)}, u32[]{:S(2)}, u32[]{:S(2)}) collective-permute-start(bf16[1024,256]{1,0:T(8,128)(2,1)S(1)} %fusion.1), channel_id=1, source_target_pairs={{0,256},{16,272},{32,288},{48,304},{64,320},{80,336},{96,352},{112... | collective-permute-start | bytes 1572872 | tf_op jit(solution)/shard_map/ppermute | solution.py:12
  165.0 11.2 %copy-start.3 = (bf16[192,768]{1,0:T(8,128)(2,1)S(1)}, bf16[192,768]{1,0:T(8,128)(2,1)}, u32[]{:S(2)}) copy-start(bf16[192,768]{1,0:T(8,128)(2,1)} %convert_bitcast_fusion) | copy-start | bytes 884740

commit v10 on v7

--- a/solution.py
+++ b/solution.py
@@ -87,8 +87,9 @@
         )
 
     peer_terms = grad_cols(half, hidden)
-    peer_g, peer_u, peer_d = partner(
-        tuple(t.astype(jnp.bfloat16) for t in peer_terms), "section", pair_bit
+    peer_d = partner(peer_terms[2].astype(jnp.bfloat16), "section", pair_bit)
+    peer_g, peer_u = partner(
+        tuple(t.astype(jnp.bfloat16) for t in peer_terms[:2]), "section", pair_bit
     )
     own_g, own_u, own_d = grad_cols(0, half)
     token_acc = jnp.dot(sel_t, home.reshape(rows, width), preferred_element_type=jnp.float32)

time: 154 us -> 154 us (level)
  no operation moved by 1% of the time
where the time goes in v10:
time: 154 us; the launch traced here: 153 us
  waiting for transfers between devices  84.8 us (55%)
  starting transfers between devices  35.5 us (23%)
  matrix products  24.5 us (16%)
  other arithmetic  3.62 us (2%)
  local copies, waits for them, and re-layouts  3.53 us (2%)
    all_to_all x1, waiting for transfers between devices, per_device(): lax.all_to_all(send, 'expert', split_axis=0, concat_axis=0, tiled=True)  42.8 us
    ppermute x6, waiting for transfers between devices, partner(): return lax.ppermute(value, axis, pairs)  42 us
    ppermute x6, starting transfers between devices, partner(): return lax.ppermute(value, axis, pairs)  19.6 us
    all_to_all x1, starting transfers between devices, per_device(): lax.all_to_all(send, 'expert', split_axis=0, concat_axis=0, tiled=True)  10.4 us
    all_to_all x1, starting transfers between devices, per_device(): lax.all_to_all(back, 'expert', split_axis=0, concat_axis=0, tiled=True)  5.59 us
    dot_general x1, matrix products, per_device(): gu_pre = jnp.dot(rows_in, full_gu, preferred_element_type=jnp.float32)  4.52 us
    dot_general x1, matrix products, per_device(): lax.dot_general(gu_grad, full_gu, contract_last, preferred_element_type=j...  4.44 us
    dot_general x1, matrix products, per_device(): lax.dot_general(rows_grad, full_down, contract_last, preferred_element_ty...  3.57 us
  transfers between devices with their start and end apart: 8, of which 6 were waited for; matrix products, arithmetic and copies ran while one was open for 9% of the time, Pallas kernels for 0%

profile of v10, /device:TPU:1, one launch (start us, length us, event | category | flops | bytes accessed | tf_op | source)
XLA Modules:
  0.0 153.0 jit_solution(3462566283870084222)
XLA Ops:
  0.6 0.8 copy.21
  1.4 0.1 eq.49
  1.6 0.1 eq.45
  1.7 0.9 reduce-window.6
  2.6 0.2 slice_reduce_fusion
  2.9 0.1 fusion.50
  3.0 0.1 reduce_sum.21
  3.1 0.1 copy.25
  3.2 0.2 fusion.11
  3.4 0.8 copy.26
  4.2 0.1 broadcast_in_dim.30
  4.4 2.1 %fusion.33 = f32[768,2048]{1,0:T(8,128)S(1)} fusion(pred[768,192]{0,1:T(8,128)(4,1)S(1)} %fusion.11, bf16[192,1024]{1,0:T(8,128)(2,1)} %bitcast.53, bf16[192,1024]{1,0:T(8,128)(2,1)} %bitcast.54), kind=kOutput, calls=%fused_computation.44 | convolution fusion | flops 605552640 | bytes 7225344 | tf_op jit(solution)/shard_map/dot_general | solution.py:50
  6.5 0.2 slice.123
  6.8 0.2 select_reduce_fusion
  7.0 0.2 fusion
  7.2 2.0 %pad_maximum_fusion = bf16[768,2048]{1,0:T(8,128)(2,1)} fusion(bf16[768,1024]{1,0:T(8,128)(2,1)S(1)} %fusion, bf16[768,1024]{1,0:T(8,128)(2,1)S(1)} %slice.123), kind=kLoop, calls=%fused_computation.3 | loop fusion | flops 6291456 | bytes 6291456 | tf_op jit(solution)/shard_map/concatenate | solution.py:53
  9.1 10.4 %all-to-all-start = ((bf16[16,48,2048]{2,1,0:T(8,128)(2,1)}), bf16[16,48,2048]{2,1,0:T(8,128)(2,1)S(1)}, u32[]{:S(2)}, u32[]{:S(2)}) async-start(bf16[16,48,2048]{2,1,0:T(8,128)(2,1)} %bitcast.5), calls=%async_computation | async-start | bytes 6291456 | tf_op jit(solution)/shard_map/all_to_all | solution.py:54
  19.5 2.9 %collective-permute-start.1 = (bf16[1024,256]{1,0:T(8,128)(2,1)}, bf16[1024,256]{1,0:T(8,128)(2,1)S(1)}, u32[]{:S(2)}, u32[]{:S(2)}) collective-permute-start(bf16[1024,256]{1,0:T(8,128)(2,1)} %bitcast.61), channel_id=1, source_target_pairs={{0,256},{16,272},{32,288},{48,304},{64,320},{80,336},{96,352},{112... | collective-permute-start | bytes 1572872 | tf_op jit(solution)/shard_map/ppermute | solution.py:12
  22.4 3.9 %collective-permute-start.2 = (bf16[1024,256]{1,0:T(8,128)(2,1)}, bf16[1024,256]{1,0:T(8,128)(2,1)}, u32[]{:S(2)}, u32[]{:S(2)}) collective-permute-start(bf16[1024,256]{1,0:T(8,128)(2,1)} %bitcast.58), channel_id=1, source_target_pairs={{0,256},{16,272},{32,288},{48,304},{64,320},{80,336},{96,352},{112... | collective-permute-start | bytes 1572872 | tf_op jit(solution)/shard_map/ppermute | solution.py:12
  26.3 2.9 %collective-permute-start = (bf16[256,1024]{1,0:T(8,128)(2,1)}, bf16[256,1024]{1,0:T(8,128)(2,1)}, u32[]{:S(2)}, u32[]{:S(2)}) collective-permute-start(bf16[256,1024]{1,0:T(8,128)(2,1)} %bitcast.56), channel_id=1, source_target_pairs={{0,256},{16,272},{32,288},{48,304},{64,320},{80,336},{96,352},{112... | collective-permute-start | bytes 1572872 | tf_op jit(solution)/shard_map/ppermute | solution.py:12
  29.2 7.1 %collective-permute-done.1 = bf16[1024,256]{1,0:T(8,128)(2,1)S(1)} collective-permute-done((bf16[1024,256]{1,0:T(8,128)(2,1)}, bf16[1024,256]{1,0:T(8,128)(2,1)S(1)}, u32[]{:S(2)}, u32[]{:S(2)}) %collective-permute-start.1) | collective-permute-done | bytes 524320 | tf_op jit(solution)/shard_map/ppermute | solution.py:12
  36.4 0.0 copy-start.5
  36.4 0.8 copy-done.5
  37.2 10.5 %collective-permute-done.2 = bf16[1024,256]{1,0:T(8,128)(2,1)} collective-permute-done((bf16[1024,256]{1,0:T(8,128)(2,1)}, bf16[1024,256]{1,0:T(8,128)(2,1)}, u32[]{:S(2)}, u32[]{:S(2)}) %collective-permute-start.2) | collective-permute-done | bytes 524320 | tf_op jit(solution)/shard_map/ppermute | solution.py:12
  47.7 42.8 %all-to-all-done = bf16[16,48,2048]{2,1,0:T(8,128)(2,1)S(1)} async-done(((bf16[16,48,2048]{2,1,0:T(8,128)(2,1)}), bf16[16,48,2048]{2,1,0:T(8,128)(2,1)S(1)}, u32[]{:S(2)}, u32[]{:S(2)}) %all-to-all-start) | async-done | bytes 3145760 | tf_op jit(solution)/shard_map/all_to_all | solution.py:54
  90.5 0.0 copy-start
  90.5 4.5 %fusion.21 = f32[768,1024]{0,1:T(8,128)S(1)} fusion(bf16[768,2048]{1,0:T(8,128)(2,1)S(1)} %bitcast.45, bf16[1024,256]{1,0:T(8,128)(2,1)} %collective-permute-done.2, bf16[1024,256]{1,0:T(8,128)(2,1)} %bitcast.59, bf16[1024,256]{1,0:T(8,128)(2,1)} %copy-done.5, bf16[1024,256]{1,0:T(8,128)(2,1)} %bitcast.62), kind=kOutput, calls=%fused_computation.40 | convolution fusion | flops 1619001344 | bytes 6815744 | tf_op jit(solution)/shard_map/dot_general | solution.py:67
  95.0 0.0 copy-start.3
  95.0 0.0 copy-start.4
  95.1 0.0 copy-start.6
  95.1 0.0 collective-permute-done
  95.1 0.0 copy-done
  95.1 0.0 copy-done.2
  95.1 3.6 %multiply_convert_fusion.2 = (bf16[768,512]{0,1:T(8,128)(2,1)S(1)}, bf16[768,512]{0,1:T(8,128)(2,1)S(1)}, bf16[768,512]{0,1:T(8,128)(2,1)}) fusion(f32[768,1024]{0,1:T(8,128)S(1)} %fusion.21, bf16[256,1024]{1,0:T(8,128)(2,1)} %collective-permute-done, bf16[256,1024]{1,0:T(8,128)(2,1)S(1)} %bitcast.57, bf16[768,2048]{1,0:T(8,128)(2,1)S(1)} %bitcast.46), kind=kOutput, calls=%fused_computation.11 | convolution fusion | flops 813301760 | bytes 8126464 | tf_op jit(solution)/shard_map/dot_general | solution.py:73
  98.7 0.0 copy-start.8
  98.7 0.0 copy-start.10
  98.7 0.0 copy-done.3
  98.7 0.0 copy-done.4
  98.7 0.0 copy-done.6
  98.7 4.4 %convolution_convert_fusion = bf16[768,1024]{1,0:T(8,128)(2,1)} fusion(bf16[768,512]{0,1:T(8,128)(2,1)S(1)} %get-tuple-element.5, bf16[768,512]{0,1:T(8,128)(2,1)S(1)} %get-tuple-element.4, bf16[1024,256]{1,0:T(8,128)(2,1)} %collective-permute-done.2, bf16[1024,256]{1,0:T(8,128)(2,1)S(1)} %bitcast.60, bf16[1024,256]{1,0:T(8,128)(2,1)S(1)} %copy-done.6, ...), kind=kOutput, calls=%fused_computation.5 | convolution fusion | flops 1622933504 | bytes 5242880 | tf_op jit(solution)/shard_map/dot_general | solution.py:79
  103.1 0.0 copy-done.8
  103.1 0.0 copy-done.10
  103.1 0.0 copy-start.7
  103.1 5.6 %all-to-all-start.1 = ((bf16[16,48,1024]{2,1,0:T(8,128)(2,1)}), bf16[16,48,1024]{2,1,0:T(8,128)(2,1)S(1)}, u32[]{:S(2)}, u32[]{:S(2)}) async-start(bf16[16,48,1024]{2,1,0:T(8,128)(2,1)} %bitcast.10), calls=%async_computation.1 | async-start | bytes 3145728 | tf_op jit(solution)/shard_map/all_to_all | solution.py:81
  108.8 0.0 copy-done.7
  108.8 2.1 %convolution_convert_fusion.1 = bf16[256,1024]{1,0:T(8,128)(2,1)S(1)} fusion(bf16[768,2048]{1,0:T(8,128)(2,1)} %bitcast.47, bf16[768,512]{0,1:T(8,128)(2,1)S(1)} %copy-done.7), kind=kOutput, calls=%fused_computation.14 | convolution fusion | flops 402915328 | bytes 2490368 | tf_op jit(solution)/shard_map/dot_general | solution.py:86
  110.9 0.0 copy-start.9
  110.9 3.0 %collective-permute-start.5 = (bf16[256,1024]{1,0:T(8,128)(2,1)S(1)}, bf16[256,1024]{1,0:T(8,128)(2,1)S(1)}, u32[]{:S(2)}, u32[]{:S(2)}) collective-permute-start(bf16[256,1024]{1,0:T(8,128)(2,1)S(1)} %convolution_convert_fusion.1), channel_id=1, source_target_pairs={{0,256},{16,272},{32,288},{48,304},{64,320},{80,336},{96,352},{112... | collective-permute-start | bytes 1572872 | tf_op jit(solution)/shard_map/ppermute | solution.py:12
  113.9 0.0 copy-done.1
  113.9 1.6 %convolution_convert_fusion.2 = bf16[1024,256]{1,0:T(8,128)(2,1)S(1)} fusion(bf16[768,2048]{1,0:T(8,128)(2,1)S(1)} %bitcast.48, bf16[768,512]{0,1:T(8,128)(2,1)} %copy-done.10), kind=kOutput, calls=%fused_computation.15 | convolution fusion | flops 402915328 | bytes 2490368 | tf_op jit(solution)/shard_map/dot_general | solution.py:85
  115.6 3.9 %collective-permute-start.4 = (bf16[1024,256]{1,0:T(8,128)(2,1)S(1)}, bf16[1024,256]{1,0:T(8,128)(2,1)S(1)}, u32[]{:S(2)}, u32[]{:S(2)}) collective-permute-start(bf16[1024,256]{1,0:T(8,128)(2,1)S(1)} %convolution_convert_fusion.2), channel_id=1, source_target_pairs={{0,256},{16,272},{32,288},{48,304},{64,320},{80,336},{96,352},{112... | collective-permute-start | bytes 1572872 | tf_op jit(solution)/shard_map/ppermute | solution.py:12
  119.5 0.0 copy-done.9
  119.5 0.6 convolution_convert_fusion.3
  120.1 0.0 copy-start.11
  120.2 3.0 %collective-permute-start.3 = (bf16[1024,256]{1,0:T(8,128)(2,1)S(1)}, bf16[1024,256]{1,0:T(8,128)(2,1)S(1)}, u32[]{:S(2)}, u32[]{:S(2)}) collective-permute-start(bf16[1024,256]{1,0:T(8,128)(2,1)S(1)} %convolution_convert_fusion.3), channel_id=1, source_target_pairs={{0,256},{16,272},{32,288},{48,304},{64,320},{80,336},{96,352},{112... | collective-permute-start | bytes 1572872 | tf_op jit(solution)/shard_map/ppermute | solution.py:12
  123.1 4.7 %collective-permute-done.5 = bf16[256,1024]{1,0:T(8,128)(2,1)S(1)} collective-permute-done((bf16[256,1024]{1,0:T(8,128)(2,1)S(1)}, bf16[256,1024]{1,0:T(8,128)(2,1)S(1)}, u32[]{:S(2)}, u32[]{:S(2)}) %collective-permute-start.5) | collective-permute-done | bytes 524320 | tf_op jit(solution)/shard_map/ppermute | solution.py:12
  127.8 1.4 fusion.37
  129.2 9.8 %collective-permute-done.4 = bf16[1024,256]{1,0:T(8,128)(2,1)S(1)} collective-permute-done((bf16[1024,256]{1,0:T(8,128)(2,1)S(1)}, bf16[1024,256]{1,0:T(8,128)(2,1)S(1)}, u32[]{:S(2)}, u32[]{:S(2)}) %collective-permute-start.4) | collective-permute-done | bytes 524320 | tf_op jit(solution)/shard_map/ppermute | solution.py:12
  139.1 0.0 copy-done.11
  139.1 1.4 fusion.30
  140.5 9.8 %collective-permute-done.3 = bf16[1024,256]{1,0:T(8,128)(2,1)S(1)} collective-permute-done((bf16[1024,256]{1,0:T(8,128)(2,1)S(1)}, bf16[1024,256]{1,0:T(8,128)(2,1)S(1)}, u32[]{:S(2)}, u32[]{:S(2)}) %collective-permute-start.3) | collective-permute-done | bytes 524320 | tf_op jit(solution)/shard_map/ppermute | solution.py:12
  150.3 1.4 fusion.27
  151.7 0.0 all-to-all-done.1
  151.7 1.2 fusion.5
  (7 shorter events, 0.1 us)
Async XLA Ops:
  9.1 81.4 %all-to-all-start = ((bf16[16,48,2048]{2,1,0:T(8,128)(2,1)}), bf16[16,48,2048]{2,1,0:T(8,128)(2,1)S(1)}, u32[]{:S(2)}, u32[]{:S(2)}) async-start(bf16[16,48,2048]{2,1,0:T(8,128)(2,1)} %bitcast.5), calls=%async_computation | async-start | bytes 6291456 | tf_op jit(solution)/shard_map/all_to_all | solution.py:54
  19.5 16.8 %collective-permute-start.1 = (bf16[1024,256]{1,0:T(8,128)(2,1)}, bf16[1024,256]{1,0:T(8,128)(2,1)S(1)}, u32[]{:S(2)}, u32[]{:S(2)}) collective-permute-start(bf16[1024,256]{1,0:T(8,128)(2,1)} %bitcast.61), channel_id=1, source_target_pairs={{0,256},{16,272},{32,288},{48,304},{64,320},{80,336},{96,352},{112... | collective-permute-start | bytes 1572872 | tf_op jit(solution)/shard_map/ppermute | solution.py:12
  22.4 25.3 %collective-permute-start.2 = (bf16[1024,256]{1,0:T(8,128)(2,1)}, bf16[1024,256]{1,0:T(8,128)(2,1)}, u32[]{:S(2)}, u32[]{:S(2)}) collective-permute-start(bf16[1024,256]{1,0:T(8,128)(2,1)} %bitcast.58), channel_id=1, source_target_pairs={{0,256},{16,272},{32,288},{48,304},{64,320},{80,336},{96,352},{112... | collective-permute-start | bytes 1572872 | tf_op jit(solution)/shard_map/ppermute | solution.py:12
  26.3 68.8 %collective-permute-start = (bf16[256,1024]{1,0:T(8,128)(2,1)}, bf16[256,1024]{1,0:T(8,128)(2,1)}, u32[]{:S(2)}, u32[]{:S(2)}) collective-permute-start(bf16[256,1024]{1,0:T(8,128)(2,1)} %bitcast.56), channel_id=1, source_target_pairs={{0,256},{16,272},{32,288},{48,304},{64,320},{80,336},{96,352},{112... | collective-permute-start | bytes 1572872 | tf_op jit(solution)/shard_map/ppermute | solution.py:12
  36.4 0.8 copy-start.5
  90.5 4.6 %copy-start = (bf16[16,48,2048]{2,1,0:T(8,128)(2,1)}, bf16[16,48,2048]{2,1,0:T(8,128)(2,1)S(1)}, u32[]{:S(2)}) copy-start(bf16[16,48,2048]{2,1,0:T(8,128)(2,1)S(1)} %all-to-all-done) | copy-start | bytes 9437188
  90.5 4.6 %copy-start.2 = (bf16[1,1,256,1024]{3,2,1,0:T(8,128)(2,1)S(1)}, bf16[1,1,256,1024]{3,2,1,0:T(8,128)(2,1)}, u32[]{:S(2)}) copy-start(bf16[1,1,256,1024]{3,2,1,0:T(8,128)(2,1)} %param.13) | copy-start | bytes 1572868
  95.0 3.6 %copy-start.3 = (bf16[1,1,1024,256]{3,2,1,0:T(8,128)(2,1)S(1)}, bf16[1,1,1024,256]{3,2,1,0:T(8,128)(2,1)}, u32[]{:S(2)}) copy-start(bf16[1,1,1024,256]{3,2,1,0:T(8,128)(2,1)} %param.12) | copy-start | bytes 1572868
  95.0 3.6 %copy-start.4 = (bf16[1,1,1024,256]{3,2,1,0:T(8,128)(2,1)S(1)}, bf16[1,1,1024,256]{3,2,1,0:T(8,128)(2,1)}, u32[]{:S(2)}) copy-start(bf16[1,1,1024,256]{3,2,1,0:T(8,128)(2,1)} %param.11) | copy-start | bytes 1572868
  95.1 3.6 %copy-start.6 = (bf16[1024,256]{1,0:T(8,128)(2,1)S(1)}, bf16[1024,256]{1,0:T(8,128)(2,1)}, u32[]{:S(2)}) copy-start(bf16[1024,256]{1,0:T(8,128)(2,1)} %copy-done.5) | copy-start | bytes 1572868
  98.7 4.5 %copy-start.8 = (bf16[768,512]{0,1:T(8,128)(2,1)}, bf16[768,512]{0,1:T(8,128)(2,1)S(1)}, u32[]{:S(2)}) copy-start(bf16[768,512]{0,1:T(8,128)(2,1)S(1)} %get-tuple-element.4) | copy-start | bytes 2359300
  98.7 4.5 %copy-start.10 = (bf16[768,512]{0,1:T(8,128)(2,1)}, bf16[768,512]{0,1:T(8,128)(2,1)S(1)}, u32[]{:S(2)}) copy-start(bf16[768,512]{0,1:T(8,128)(2,1)S(1)} %get-tuple-element.5) | copy-start | bytes 2359300
  103.1 5.6 %copy-start.7 = (bf16[768,512]{0,1:T(8,128)(2,1)S(1)}, bf16[768,512]{0,1:T(8,128)(2,1)}, u32[]{:S(2)}) copy-start(bf16[768,512]{0,1:T(8,128)(2,1)} %get-tuple-element.6) | copy-start | bytes 2359300
  103.1 48.6 %all-to-all-start.1 = ((bf16[16,48,1024]{2,1,0:T(8,128)(2,1)}), bf16[16,48,1024]{2,1,0:T(8,128)(2,1)S(1)}, u32[]{:S(2)}, u32[]{:S(2)}) async-start(bf16[16,48,1024]{2,1,0:T(8,128)(2,1)} %bitcast.10), calls=%async_computation.1 | async-start | bytes 3145728 | tf_op jit(solution)/shard_map/all_to_all | solution.py:81
  108.7 5.2 %copy-start.1 = (bf16[16,48,2048]{2,1,0:T(8,128)(2,1)S(1)}, bf16[16,48,2048]{2,1,0:T(8,128)(2,1)}, u32[]{:S(2)}) copy-start(bf16[16,48,2048]{2,1,0:T(8,128)(2,1)} %copy-done) | copy-start | bytes 9437188
  110.9 8.6 %copy-start.9 = (bf16[768,512]{0,1:T(8,128)(2,1)S(1)}, bf16[768,512]{0,1:T(8,128)(2,1)}, u32[]{:S(2)}) copy-start(bf16[768,512]{0,1:T(8,128)(2,1)} %copy-done.8) | copy-start | bytes 2359300
  110.9 16.9 %collective-permute-start.5 = (bf16[256,1024]{1,0:T(8,128)(2,1)S(1)}, bf16[256,1024]{1,0:T(8,128)(2,1)S(1)}, u32[]{:S(2)}, u32[]{:S(2)}) collective-permute-start(bf16[256,1024]{1,0:T(8,128)(2,1)S(1)} %convolution_convert_fusion.1), channel_id=1, source_target_pairs={{0,256},{16,272},{32,288},{48,304},{64,320},{80,336},{96,352},{112... | collective-permute-start | bytes 1572872 | tf_op jit(solution)/shard_map/ppermute | solution.py:12
  115.6 23.5 %collective-permute-start.4 = (bf16[1024,256]{1,0:T(8,128)(2,1)S(1)}, bf16[1024,256]{1,0:T(8,128)(2,1)S(1)}, u32[]{:S(2)}, u32[]{:S(2)}) collective-permute-start(bf16[1024,256]{1,0:T(8,128)(2,1)S(1)} %convolution_convert_fusion.2), channel_id=1, source_target_pairs={{0,256},{16,272},{32,288},{48,304},{64,320},{80,336},{96,352},{112... | collective-permute-start | bytes 1572872 | tf_op jit(solution)/shard_map/ppermute | solution.py:12
  120.1 18.9 %copy-start.11 = (bf16[768,512]{0,1:T(8,128)(2,1)S(1)}, bf16[768,512]{0,1:T(8,128)(2,1)}, u32[]{:S(2)}) copy-start(bf16[768,512]{0,1:T(8,128)(2,1)} %copy-done.10) | copy-start | bytes 2359300
  120.2 30.1 %collective-permute-start.3 = (bf16[1024,256]{1,0:T(8,128)(2,1)S(1)}, bf16[1024,256]{1,0:T(8,128)(2,1)S(1)}, u32[]{:S(2)}, u32[]{:S(2)}) collective-permute-start(bf16[1024,256]{1,0:T(8,128)(2,1)S(1)} %convolution_convert_fusion.3), channel_id=1, source_target_pairs={{0,256},{16,272},{32,288},{48,304},{64,320},{80,336},{96,352},{112... | collective-permute-start | bytes 1572872 | tf_op jit(solution)/shard_map/ppermute | solution.py:12

commit v11 on v10

--- a/solution.py
+++ b/solution.py
@@ -86,8 +86,11 @@
             lax.dot_general(act[:, lo:hi], rows_grad, contract_rows, preferred_element_type=jnp.float32),
         )
 
+    peer_d_send = lax.dot_general(
+        act[:, half:hidden], rows_grad, contract_rows, preferred_element_type=jnp.float32
+    ).astype(jnp.bfloat16)
     peer_terms = grad_cols(half, hidden)
-    peer_d = partner(peer_terms[2].astype(jnp.bfloat16), "section", pair_bit)
+    peer_d = partner(peer_d_send, "section", pair_bit)
     peer_g, peer_u = partner(
         tuple(t.astype(jnp.bfloat16) for t in peer_terms[:2]), "section", pair_bit
     )

time: 154 us -> 154 us (level)
    dot_general x0 -> x1, matrix products: none -> 2.13 us  [per_device(): lax.dot_general(act[:, half:hidden], rows_grad, contract_rows, preferred_...]
    dot_general x2 -> x1, matrix products: 3.52 us -> 1.39 us  [grad_cols(): lax.dot_general(act[:, lo:hi], rows_grad, contract_rows, preferred_elemen...]
where the time goes in v11:
time: 154 us; the launch traced here: 153 us
  waiting for transfers between devices  84.8 us (55%)
  starting transfers between devices  35.5 us (23%)
  matrix products  24.5 us (16%)
  other arithmetic  3.62 us (2%)
  local copies, waits for them, and re-layouts  3.53 us (2%)
    all_to_all x1, waiting for transfers between devices, per_device(): lax.all_to_all(send, 'expert', split_axis=0, concat_axis=0, tiled=True)  42.8 us
    ppermute x6, waiting for transfers between devices, partner(): return lax.ppermute(value, axis, pairs)  42 us
    ppermute x6, starting transfers between devices, partner(): return lax.ppermute(value, axis, pairs)  19.6 us
    all_to_all x1, starting transfers between devices, per_device(): lax.all_to_all(send, 'expert', split_axis=0, concat_axis=0, tiled=True)  10.4 us
    all_to_all x1, starting transfers between devices, per_device(): lax.all_to_all(back, 'expert', split_axis=0, concat_axis=0, tiled=True)  5.59 us
    dot_general x1, matrix products, per_device(): gu_pre = jnp.dot(rows_in, full_gu, preferred_element_type=jnp.float32)  4.52 us
    dot_general x1, matrix products, per_device(): lax.dot_general(gu_grad, full_gu, contract_last, preferred_element_type=j...  4.44 us
    dot_general x1, matrix products, per_device(): lax.dot_general(rows_grad, full_down, contract_last, preferred_element_ty...  3.57 us
  transfers between devices with their start and end apart: 8, of which 6 were waited for; matrix products, arithmetic and copies ran while one was open for 9% of the time, Pallas kernels for 0%

profile of v11, /device:TPU:1, one launch (start us, length us, event | category | flops | bytes accessed | tf_op | source)
XLA Modules:
  0.0 153.0 jit_solution(3462566283870084222)
XLA Ops:
  0.6 0.8 copy.21
  1.4 0.1 eq.49
  1.6 0.1 eq.45
  1.7 0.9 reduce-window.6
  2.6 0.2 slice_reduce_fusion
  2.9 0.1 fusion.50
  3.0 0.1 reduce_sum.21
  3.1 0.1 copy.25
  3.2 0.2 fusion.11
  3.4 0.8 copy.26
  4.2 0.1 broadcast_in_dim.30
  4.4 2.1 %fusion.33 = f32[768,2048]{1,0:T(8,128)S(1)} fusion(pred[768,192]{0,1:T(8,128)(4,1)S(1)} %fusion.11, bf16[192,1024]{1,0:T(8,128)(2,1)} %bitcast.53, bf16[192,1024]{1,0:T(8,128)(2,1)} %bitcast.54), kind=kOutput, calls=%fused_computation.44 | convolution fusion | flops 605552640 | bytes 7225344 | tf_op jit(solution)/shard_map/dot_general | solution.py:50
  6.5 0.2 slice.123
  6.8 0.2 select_reduce_fusion
  7.0 0.2 fusion
  7.2 2.0 %pad_maximum_fusion = bf16[768,2048]{1,0:T(8,128)(2,1)} fusion(bf16[768,1024]{1,0:T(8,128)(2,1)S(1)} %fusion, bf16[768,1024]{1,0:T(8,128)(2,1)S(1)} %slice.123), kind=kLoop, calls=%fused_computation.3 | loop fusion | flops 6291456 | bytes 6291456 | tf_op jit(solution)/shard_map/concatenate | solution.py:53
  9.1 10.4 %all-to-all-start = ((bf16[16,48,2048]{2,1,0:T(8,128)(2,1)}), bf16[16,48,2048]{2,1,0:T(8,128)(2,1)S(1)}, u32[]{:S(2)}, u32[]{:S(2)}) async-start(bf16[16,48,2048]{2,1,0:T(8,128)(2,1)} %bitcast.5), calls=%async_computation | async-start | bytes 6291456 | tf_op jit(solution)/shard_map/all_to_all | solution.py:54
  19.5 2.9 %collective-permute-start.1 = (bf16[1024,256]{1,0:T(8,128)(2,1)}, bf16[1024,256]{1,0:T(8,128)(2,1)S(1)}, u32[]{:S(2)}, u32[]{:S(2)}) collective-permute-start(bf16[1024,256]{1,0:T(8,128)(2,1)} %bitcast.61), channel_id=1, source_target_pairs={{0,256},{16,272},{32,288},{48,304},{64,320},{80,336},{96,352},{112... | collective-permute-start | bytes 1572872 | tf_op jit(solution)/shard_map/ppermute | solution.py:12
  22.4 3.9 %collective-permute-start.2 = (bf16[1024,256]{1,0:T(8,128)(2,1)}, bf16[1024,256]{1,0:T(8,128)(2,1)}, u32[]{:S(2)}, u32[]{:S(2)}) collective-permute-start(bf16[1024,256]{1,0:T(8,128)(2,1)} %bitcast.58), channel_id=1, source_target_pairs={{0,256},{16,272},{32,288},{48,304},{64,320},{80,336},{96,352},{112... | collective-permute-start | bytes 1572872 | tf_op jit(solution)/shard_map/ppermute | solution.py:12
  26.3 2.9 %collective-permute-start = (bf16[256,1024]{1,0:T(8,128)(2,1)}, bf16[256,1024]{1,0:T(8,128)(2,1)}, u32[]{:S(2)}, u32[]{:S(2)}) collective-permute-start(bf16[256,1024]{1,0:T(8,128)(2,1)} %bitcast.56), channel_id=1, source_target_pairs={{0,256},{16,272},{32,288},{48,304},{64,320},{80,336},{96,352},{112... | collective-permute-start | bytes 1572872 | tf_op jit(solution)/shard_map/ppermute | solution.py:12
  29.2 7.1 %collective-permute-done.1 = bf16[1024,256]{1,0:T(8,128)(2,1)S(1)} collective-permute-done((bf16[1024,256]{1,0:T(8,128)(2,1)}, bf16[1024,256]{1,0:T(8,128)(2,1)S(1)}, u32[]{:S(2)}, u32[]{:S(2)}) %collective-permute-start.1) | collective-permute-done | bytes 524320 | tf_op jit(solution)/shard_map/ppermute | solution.py:12
  36.4 0.0 copy-start.5
  36.4 0.8 copy-done.5
  37.2 10.5 %collective-permute-done.2 = bf16[1024,256]{1,0:T(8,128)(2,1)} collective-permute-done((bf16[1024,256]{1,0:T(8,128)(2,1)}, bf16[1024,256]{1,0:T(8,128)(2,1)}, u32[]{:S(2)}, u32[]{:S(2)}) %collective-permute-start.2) | collective-permute-done | bytes 524320 | tf_op jit(solution)/shard_map/ppermute | solution.py:12
  47.7 42.8 %all-to-all-done = bf16[16,48,2048]{2,1,0:T(8,128)(2,1)S(1)} async-done(((bf16[16,48,2048]{2,1,0:T(8,128)(2,1)}), bf16[16,48,2048]{2,1,0:T(8,128)(2,1)S(1)}, u32[]{:S(2)}, u32[]{:S(2)}) %all-to-all-start) | async-done | bytes 3145760 | tf_op jit(solution)/shard_map/all_to_all | solution.py:54
  90.5 0.0 copy-start
  90.5 4.5 %fusion.21 = f32[768,1024]{0,1:T(8,128)S(1)} fusion(bf16[768,2048]{1,0:T(8,128)(2,1)S(1)} %bitcast.45, bf16[1024,256]{1,0:T(8,128)(2,1)} %collective-permute-done.2, bf16[1024,256]{1,0:T(8,128)(2,1)} %bitcast.59, bf16[1024,256]{1,0:T(8,128)(2,1)} %copy-done.5, bf16[1024,256]{1,0:T(8,128)(2,1)} %bitcast.62), kind=kOutput, calls=%fused_computation.40 | convolution fusion | flops 1619001344 | bytes 6815744 | tf_op jit(solution)/shard_map/dot_general | solution.py:67
  95.0 0.0 copy-start.3
  95.0 0.0 copy-start.4
  95.1 0.0 copy-start.6
  95.1 0.0 collective-permute-done
  95.1 0.0 copy-done
  95.1 0.0 copy-done.2
  95.1 3.6 %multiply_convert_fusion.2 = (bf16[768,512]{0,1:T(8,128)(2,1)S(1)}, bf16[768,512]{0,1:T(8,128)(2,1)S(1)}, bf16[768,512]{0,1:T(8,128)(2,1)}) fusion(f32[768,1024]{0,1:T(8,128)S(1)} %fusion.21, bf16[256,1024]{1,0:T(8,128)(2,1)} %collective-permute-done, bf16[256,1024]{1,0:T(8,128)(2,1)S(1)} %bitcast.57, bf16[768,2048]{1,0:T(8,128)(2,1)S(1)} %bitcast.46), kind=kOutput, calls=%fused_computation.11 | convolution fusion | flops 813301760 | bytes 8126464 | tf_op jit(solution)/shard_map/dot_general | solution.py:73
  98.7 0.0 copy-start.8
  98.7 0.0 copy-start.10
  98.7 0.0 copy-done.3
  98.7 0.0 copy-done.4
  98.7 0.0 copy-done.6
  98.7 4.4 %convolution_convert_fusion = bf16[768,1024]{1,0:T(8,128)(2,1)} fusion(bf16[768,512]{0,1:T(8,128)(2,1)S(1)} %get-tuple-element.5, bf16[768,512]{0,1:T(8,128)(2,1)S(1)} %get-tuple-element.4, bf16[1024,256]{1,0:T(8,128)(2,1)} %collective-permute-done.2, bf16[1024,256]{1,0:T(8,128)(2,1)S(1)} %bitcast.60, bf16[1024,256]{1,0:T(8,128)(2,1)S(1)} %copy-done.6, ...), kind=kOutput, calls=%fused_computation.5 | convolution fusion | flops 1622933504 | bytes 5242880 | tf_op jit(solution)/shard_map/dot_general | solution.py:79
  103.1 0.0 copy-done.8
  103.1 0.0 copy-done.10
  103.1 0.0 copy-start.7
  103.1 5.6 %all-to-all-start.1 = ((bf16[16,48,1024]{2,1,0:T(8,128)(2,1)}), bf16[16,48,1024]{2,1,0:T(8,128)(2,1)S(1)}, u32[]{:S(2)}, u32[]{:S(2)}) async-start(bf16[16,48,1024]{2,1,0:T(8,128)(2,1)} %bitcast.10), calls=%async_computation.1 | async-start | bytes 3145728 | tf_op jit(solution)/shard_map/all_to_all | solution.py:81
  108.8 0.0 copy-done.7
  108.8 2.1 %convolution_convert_fusion.1 = bf16[256,1024]{1,0:T(8,128)(2,1)S(1)} fusion(bf16[768,2048]{1,0:T(8,128)(2,1)} %bitcast.47, bf16[768,512]{0,1:T(8,128)(2,1)S(1)} %copy-done.7), kind=kOutput, calls=%fused_computation.14 | convolution fusion | flops 402915328 | bytes 2490368 | tf_op jit(solution)/shard_map/dot_general | solution.py:89
  110.9 0.0 copy-start.9
  110.9 3.0 %collective-permute-start.5 = (bf16[256,1024]{1,0:T(8,128)(2,1)S(1)}, bf16[256,1024]{1,0:T(8,128)(2,1)S(1)}, u32[]{:S(2)}, u32[]{:S(2)}) collective-permute-start(bf16[256,1024]{1,0:T(8,128)(2,1)S(1)} %convolution_convert_fusion.1), channel_id=1, source_target_pairs={{0,256},{16,272},{32,288},{48,304},{64,320},{80,336},{96,352},{112... | collective-permute-start | bytes 1572872 | tf_op jit(solution)/shard_map/ppermute | solution.py:12
  113.9 0.0 copy-done.1
  113.9 1.6 %convolution_convert_fusion.2 = bf16[1024,256]{1,0:T(8,128)(2,1)S(1)} fusion(bf16[768,2048]{1,0:T(8,128)(2,1)S(1)} %bitcast.48, bf16[768,512]{0,1:T(8,128)(2,1)} %copy-done.10), kind=kOutput, calls=%fused_computation.15 | convolution fusion | flops 402915328 | bytes 2490368 | tf_op jit(solution)/shard_map/dot_general | solution.py:85
  115.6 3.9 %collective-permute-start.4 = (bf16[1024,256]{1,0:T(8,128)(2,1)S(1)}, bf16[1024,256]{1,0:T(8,128)(2,1)S(1)}, u32[]{:S(2)}, u32[]{:S(2)}) collective-permute-start(bf16[1024,256]{1,0:T(8,128)(2,1)S(1)} %convolution_convert_fusion.2), channel_id=1, source_target_pairs={{0,256},{16,272},{32,288},{48,304},{64,320},{80,336},{96,352},{112... | collective-permute-start | bytes 1572872 | tf_op jit(solution)/shard_map/ppermute | solution.py:12
  119.5 0.0 copy-done.9
  119.5 0.6 convolution_convert_fusion.3
  120.1 0.0 copy-start.11
  120.2 3.0 %collective-permute-start.3 = (bf16[1024,256]{1,0:T(8,128)(2,1)S(1)}, bf16[1024,256]{1,0:T(8,128)(2,1)S(1)}, u32[]{:S(2)}, u32[]{:S(2)}) collective-permute-start(bf16[1024,256]{1,0:T(8,128)(2,1)S(1)} %convolution_convert_fusion.3), channel_id=1, source_target_pairs={{0,256},{16,272},{32,288},{48,304},{64,320},{80,336},{96,352},{112... | collective-permute-start | bytes 1572872 | tf_op jit(solution)/shard_map/ppermute | solution.py:12
  123.1 4.7 %collective-permute-done.5 = bf16[256,1024]{1,0:T(8,128)(2,1)S(1)} collective-permute-done((bf16[256,1024]{1,0:T(8,128)(2,1)S(1)}, bf16[256,1024]{1,0:T(8,128)(2,1)S(1)}, u32[]{:S(2)}, u32[]{:S(2)}) %collective-permute-start.5) | collective-permute-done | bytes 524320 | tf_op jit(solution)/shard_map/ppermute | solution.py:12
  127.8 1.4 fusion.37
  129.2 9.8 %collective-permute-done.4 = bf16[1024,256]{1,0:T(8,128)(2,1)S(1)} collective-permute-done((bf16[1024,256]{1,0:T(8,128)(2,1)S(1)}, bf16[1024,256]{1,0:T(8,128)(2,1)S(1)}, u32[]{:S(2)}, u32[]{:S(2)}) %collective-permute-start.4) | collective-permute-done | bytes 524320 | tf_op jit(solution)/shard_map/ppermute | solution.py:12
  139.1 0.0 copy-done.11
  139.1 1.4 fusion.30
  140.5 9.8 %collective-permute-done.3 = bf16[1024,256]{1,0:T(8,128)(2,1)S(1)} collective-permute-done((bf16[1024,256]{1,0:T(8,128)(2,1)S(1)}, bf16[1024,256]{1,0:T(8,128)(2,1)S(1)}, u32[]{:S(2)}, u32[]{:S(2)}) %collective-permute-start.3) | collective-permute-done | bytes 524320 | tf_op jit(solution)/shard_map/ppermute | solution.py:12
  150.3 1.4 fusion.27
  151.7 0.0 all-to-all-done.1
  151.7 1.2 fusion.5
  (7 shorter events, 0.1 us)
Async XLA Ops:
  9.1 81.4 %all-to-all-start = ((bf16[16,48,2048]{2,1,0:T(8,128)(2,1)}), bf16[16,48,2048]{2,1,0:T(8,128)(2,1)S(1)}, u32[]{:S(2)}, u32[]{:S(2)}) async-start(bf16[16,48,2048]{2,1,0:T(8,128)(2,1)} %bitcast.5), calls=%async_computation | async-start | bytes 6291456 | tf_op jit(solution)/shard_map/all_to_all | solution.py:54
  19.5 16.8 %collective-permute-start.1 = (bf16[1024,256]{1,0:T(8,128)(2,1)}, bf16[1024,256]{1,0:T(8,128)(2,1)S(1)}, u32[]{:S(2)}, u32[]{:S(2)}) collective-permute-start(bf16[1024,256]{1,0:T(8,128)(2,1)} %bitcast.61), channel_id=1, source_target_pairs={{0,256},{16,272},{32,288},{48,304},{64,320},{80,336},{96,352},{112... | collective-permute-start | bytes 1572872 | tf_op jit(solution)/shard_map/ppermute | solution.py:12
  22.4 25.3 %collective-permute-start.2 = (bf16[1024,256]{1,0:T(8,128)(2,1)}, bf16[1024,256]{1,0:T(8,128)(2,1)}, u32[]{:S(2)}, u32[]{:S(2)}) collective-permute-start(bf16[1024,256]{1,0:T(8,128)(2,1)} %bitcast.58), channel_id=1, source_target_pairs={{0,256},{16,272},{32,288},{48,304},{64,320},{80,336},{96,352},{112... | collective-permute-start | bytes 1572872 | tf_op jit(solution)/shard_map/ppermute | solution.py:12
  26.3 68.8 %collective-permute-start = (bf16[256,1024]{1,0:T(8,128)(2,1)}, bf16[256,1024]{1,0:T(8,128)(2,1)}, u32[]{:S(2)}, u32[]{:S(2)}) collective-permute-start(bf16[256,1024]{1,0:T(8,128)(2,1)} %bitcast.56), channel_id=1, source_target_pairs={{0,256},{16,272},{32,288},{48,304},{64,320},{80,336},{96,352},{112... | collective-permute-start | bytes 1572872 | tf_op jit(solution)/shard_map/ppermute | solution.py:12
  36.4 0.8 copy-start.5
  90.5 4.6 %copy-start = (bf16[16,48,2048]{2,1,0:T(8,128)(2,1)}, bf16[16,48,2048]{2,1,0:T(8,128)(2,1)S(1)}, u32[]{:S(2)}) copy-start(bf16[16,48,2048]{2,1,0:T(8,128)(2,1)S(1)} %all-to-all-done) | copy-start | bytes 9437188
  90.5 4.6 %copy-start.2 = (bf16[1,1,256,1024]{3,2,1,0:T(8,128)(2,1)S(1)}, bf16[1,1,256,1024]{3,2,1,0:T(8,128)(2,1)}, u32[]{:S(2)}) copy-start(bf16[1,1,256,1024]{3,2,1,0:T(8,128)(2,1)} %param.13) | copy-start | bytes 1572868
  95.0 3.6 %copy-start.3 = (bf16[1,1,1024,256]{3,2,1,0:T(8,128)(2,1)S(1)}, bf16[1,1,1024,256]{3,2,1,0:T(8,128)(2,1)}, u32[]{:S(2)}) copy-start(bf16[1,1,1024,256]{3,2,1,0:T(8,128)(2,1)} %param.12) | copy-start | bytes 1572868
  95.0 3.6 %copy-start.4 = (bf16[1,1,1024,256]{3,2,1,0:T(8,128)(2,1)S(1)}, bf16[1,1,1024,256]{3,2,1,0:T(8,128)(2,1)}, u32[]{:S(2)}) copy-start(bf16[1,1,1024,256]{3,2,1,0:T(8,128)(2,1)} %param.11) | copy-start | bytes 1572868
  95.1 3.6 %copy-start.6 = (bf16[1024,256]{1,0:T(8,128)(2,1)S(1)}, bf16[1024,256]{1,0:T(8,128)(2,1)}, u32[]{:S(2)}) copy-start(bf16[1024,256]{1,0:T(8,128)(2,1)} %copy-done.5) | copy-start | bytes 1572868
  98.7 4.5 %copy-start.8 = (bf16[768,512]{0,1:T(8,128)(2,1)}, bf16[768,512]{0,1:T(8,128)(2,1)S(1)}, u32[]{:S(2)}) copy-start(bf16[768,512]{0,1:T(8,128)(2,1)S(1)} %get-tuple-element.4) | copy-start | bytes 2359300
  98.7 4.5 %copy-start.10 = (bf16[768,512]{0,1:T(8,128)(2,1)}, bf16[768,512]{0,1:T(8,128)(2,1)S(1)}, u32[]{:S(2)}) copy-start(bf16[768,512]{0,1:T(8,128)(2,1)S(1)} %get-tuple-element.5) | copy-start | bytes 2359300
  103.1 5.6 %copy-start.7 = (bf16[768,512]{0,1:T(8,128)(2,1)S(1)}, bf16[768,512]{0,1:T(8,128)(2,1)}, u32[]{:S(2)}) copy-start(bf16[768,512]{0,1:T(8,128)(2,1)} %get-tuple-element.6) | copy-start | bytes 2359300
  103.1 48.6 %all-to-all-start.1 = ((bf16[16,48,1024]{2,1,0:T(8,128)(2,1)}), bf16[16,48,1024]{2,1,0:T(8,128)(2,1)S(1)}, u32[]{:S(2)}, u32[]{:S(2)}) async-start(bf16[16,48,1024]{2,1,0:T(8,128)(2,1)} %bitcast.10), calls=%async_computation.1 | async-start | bytes 3145728 | tf_op jit(solution)/shard_map/all_to_all | solution.py:81
  108.7 5.2 %copy-start.1 = (bf16[16,48,2048]{2,1,0:T(8,128)(2,1)S(1)}, bf16[16,48,2048]{2,1,0:T(8,128)(2,1)}, u32[]{:S(2)}) copy-start(bf16[16,48,2048]{2,1,0:T(8,128)(2,1)} %copy-done) | copy-start | bytes 9437188
  110.9 8.6 %copy-start.9 = (bf16[768,512]{0,1:T(8,128)(2,1)S(1)}, bf16[768,512]{0,1:T(8,128)(2,1)}, u32[]{:S(2)}) copy-start(bf16[768,512]{0,1:T(8,128)(2,1)} %copy-done.8) | copy-start | bytes 2359300
  110.9 16.9 %collective-permute-start.5 = (bf16[256,1024]{1,0:T(8,128)(2,1)S(1)}, bf16[256,1024]{1,0:T(8,128)(2,1)S(1)}, u32[]{:S(2)}, u32[]{:S(2)}) collective-permute-start(bf16[256,1024]{1,0:T(8,128)(2,1)S(1)} %convolution_convert_fusion.1), channel_id=1, source_target_pairs={{0,256},{16,272},{32,288},{48,304},{64,320},{80,336},{96,352},{112... | collective-permute-start | bytes 1572872 | tf_op jit(solution)/shard_map/ppermute | solution.py:12
  115.6 23.5 %collective-permute-start.4 = (bf16[1024,256]{1,0:T(8,128)(2,1)S(1)}, bf16[1024,256]{1,0:T(8,128)(2,1)S(1)}, u32[]{:S(2)}, u32[]{:S(2)}) collective-permute-start(bf16[1024,256]{1,0:T(8,128)(2,1)S(1)} %convolution_convert_fusion.2), channel_id=1, source_target_pairs={{0,256},{16,272},{32,288},{48,304},{64,320},{80,336},{96,352},{112... | collective-permute-start | bytes 1572872 | tf_op jit(solution)/shard_map/ppermute | solution.py:12
  120.1 18.9 %copy-start.11 = (bf16[768,512]{0,1:T(8,128)(2,1)S(1)}, bf16[768,512]{0,1:T(8,128)(2,1)}, u32[]{:S(2)}) copy-start(bf16[768,512]{0,1:T(8,128)(2,1)} %copy-done.10) | copy-start | bytes 2359300
  120.2 30.1 %collective-permute-start.3 = (bf16[1024,256]{1,0:T(8,128)(2,1)S(1)}, bf16[1024,256]{1,0:T(8,128)(2,1)S(1)}, u32[]{:S(2)}, u32[]{:S(2)}) collective-permute-start(bf16[1024,256]{1,0:T(8,128)(2,1)S(1)} %convolution_convert_fusion.3), channel_id=1, source_target_pairs={{0,256},{16,272},{32,288},{48,304},{64,320},{80,336},{96,352},{112... | collective-permute-start | bytes 1572872 | tf_op jit(solution)/shard_map/ppermute | solution.py:12

commit v12 on v10

--- a/solution.py
+++ b/solution.py
@@ -16,9 +16,11 @@
     tok, topk = ids.shape
     count = tok * topk
     flat = ids.reshape(count)
-    onehot = (flat[:, None] == jnp.arange(experts, dtype=jnp.int32)[None, :]).astype(jnp.int32)
-    before = jnp.cumsum(onehot, axis=0) - onehot
-    rank = jnp.sum(before * onehot, axis=1)
+    match = flat[:, None] == jnp.arange(experts, dtype=jnp.int32)[None, :]
+    order = jnp.arange(count, dtype=jnp.int32)
+    earlier = (order[None, :] < order[:, None]).astype(jnp.bfloat16)
+    before = jnp.dot(earlier, match.astype(jnp.bfloat16), preferred_element_type=jnp.float32)
+    rank = jnp.sum(jnp.where(match, before, 0.0), axis=1).astype(jnp.int32)
     slot = flat * cap + rank
     hit = slot[None, :] == jnp.arange(experts * cap, dtype=jnp.int32)[:, None]
     return hit
@@ -44,7 +46,9 @@
     other_gate, other_up, other_down = partner((own_gate, own_up, own_down), "section", pair_bit)
 
     hit = dispatch_matrix(ids, cap, experts)
-    pair_gate = jnp.sum(jnp.where(hit, gates.reshape(tok * topk)[None, :], 0.0), axis=1)
+    pair_gate = jnp.sum(
+        jnp.where(hit.reshape(rows, tok, topk), gates[None, :, :], 0.0), axis=(1, 2)
+    )
     sel = hit.reshape(rows, tok, topk).any(axis=2).astype(jnp.bfloat16)
     both = jnp.concatenate([inputs, grads], axis=1)
     picked = jnp.dot(sel, both, preferred_element_type=jnp.float32)

time: 154 us -> 152 us (0.987)
  no operation moved by 1% of the time
where the time goes in v12:
time: 152 us; the launch traced here: 151 us
  waiting for transfers between devices  84.8 us (56%)
  starting transfers between devices  35.5 us (23%)
  matrix products  24.7 us (16%)
  other arithmetic  3.26 us (2%)
  local copies, waits for them, and re-layouts  2.22 us (1%)
    all_to_all x1, waiting for transfers between devices, per_device(): lax.all_to_all(send, 'expert', split_axis=0, concat_axis=0, tiled=True)  42.8 us
    ppermute x6, waiting for transfers between devices, partner(): return lax.ppermute(value, axis, pairs)  42 us
    ppermute x6, starting transfers between devices, partner(): return lax.ppermute(value, axis, pairs)  19.6 us
    all_to_all x1, starting transfers between devices, per_device(): lax.all_to_all(send, 'expert', split_axis=0, concat_axis=0, tiled=True)  10.4 us
    all_to_all x1, starting transfers between devices, per_device(): lax.all_to_all(back, 'expert', split_axis=0, concat_axis=0, tiled=True)  5.59 us
    dot_general x1, matrix products, per_device(): gu_pre = jnp.dot(rows_in, full_gu, preferred_element_type=jnp.float32)  4.52 us
    dot_general x1, matrix products, per_device(): lax.dot_general(gu_grad, full_gu, contract_last, preferred_element_type=j...  4.44 us
    dot_general x1, matrix products, per_device(): lax.dot_general(rows_grad, full_down, contract_last, preferred_element_ty...  3.57 us
  transfers between devices with their start and end apart: 8, of which 6 were waited for; matrix products, arithmetic and copies ran while one was open for 9% of the time, Pallas kernels for 0%

profile of v12, /device:TPU:1, one launch (start us, length us, event | category | flops | bytes accessed | tf_op | source)
XLA Modules:
  0.0 151.5 jit_solution(9259666443788195220)
XLA Ops:
  0.6 0.8 copy.20
  1.4 0.1 eq.29
  1.6 0.2 fusion.12
  1.8 0.1 convert_element_type.66
  2.0 0.1 copy.22
  2.0 0.2 fusion.11
  2.2 0.9 select_reduce_fusion
  3.1 2.1 %fusion.34 = f32[768,2048]{1,0:T(8,128)S(1)} fusion(pred[768,192]{0,1:T(8,128)(4,1)S(1)} %fusion.11, bf16[192,1024]{1,0:T(8,128)(2,1)} %bitcast.34, bf16[192,1024]{1,0:T(8,128)(2,1)} %bitcast.35), kind=kOutput, calls=%fused_computation.45 | convolution fusion | flops 605552640 | bytes 7225344 | tf_op jit(solution)/shard_map/dot_general | solution.py:54
  5.3 0.2 slice.113
  5.5 0.2 fusion
  5.7 1.9 %pad_maximum_fusion = bf16[768,2048]{1,0:T(8,128)(2,1)} fusion(bf16[768,1024]{1,0:T(8,128)(2,1)S(1)} %fusion, bf16[768,1024]{1,0:T(8,128)(2,1)S(1)} %slice.113), kind=kLoop, calls=%fused_computation.3 | loop fusion | flops 6291456 | bytes 6291456 | tf_op jit(solution)/shard_map/concatenate | solution.py:57
  7.7 10.4 %all-to-all-start = ((bf16[16,48,2048]{2,1,0:T(8,128)(2,1)}), bf16[16,48,2048]{2,1,0:T(8,128)(2,1)S(1)}, u32[]{:S(2)}, u32[]{:S(2)}) async-start(bf16[16,48,2048]{2,1,0:T(8,128)(2,1)} %bitcast.5), calls=%async_computation | async-start | bytes 6291456 | tf_op jit(solution)/shard_map/all_to_all | solution.py:58
  18.0 2.9 %collective-permute-start.1 = (bf16[1024,256]{1,0:T(8,128)(2,1)}, bf16[1024,256]{1,0:T(8,128)(2,1)S(1)}, u32[]{:S(2)}, u32[]{:S(2)}) collective-permute-start(bf16[1024,256]{1,0:T(8,128)(2,1)} %bitcast.42), channel_id=1, source_target_pairs={{0,256},{16,272},{32,288},{48,304},{64,320},{80,336},{96,352},{112... | collective-permute-start | bytes 1572872 | tf_op jit(solution)/shard_map/ppermute | solution.py:12
  20.9 3.9 %collective-permute-start.2 = (bf16[1024,256]{1,0:T(8,128)(2,1)}, bf16[1024,256]{1,0:T(8,128)(2,1)}, u32[]{:S(2)}, u32[]{:S(2)}) collective-permute-start(bf16[1024,256]{1,0:T(8,128)(2,1)} %bitcast.39), channel_id=1, source_target_pairs={{0,256},{16,272},{32,288},{48,304},{64,320},{80,336},{96,352},{112... | collective-permute-start | bytes 1572872 | tf_op jit(solution)/shard_map/ppermute | solution.py:12
  24.8 2.9 %collective-permute-start = (bf16[256,1024]{1,0:T(8,128)(2,1)}, bf16[256,1024]{1,0:T(8,128)(2,1)}, u32[]{:S(2)}, u32[]{:S(2)}) collective-permute-start(bf16[256,1024]{1,0:T(8,128)(2,1)} %bitcast.37), channel_id=1, source_target_pairs={{0,256},{16,272},{32,288},{48,304},{64,320},{80,336},{96,352},{112... | collective-permute-start | bytes 1572872 | tf_op jit(solution)/shard_map/ppermute | solution.py:12
  27.7 7.1 %collective-permute-done.1 = bf16[1024,256]{1,0:T(8,128)(2,1)S(1)} collective-permute-done((bf16[1024,256]{1,0:T(8,128)(2,1)}, bf16[1024,256]{1,0:T(8,128)(2,1)S(1)}, u32[]{:S(2)}, u32[]{:S(2)}) %collective-permute-start.1) | collective-permute-done | bytes 524320 | tf_op jit(solution)/shard_map/ppermute | solution.py:12
  34.9 0.0 copy-start.5
  34.9 0.8 copy-done.5
  35.7 10.5 %collective-permute-done.2 = bf16[1024,256]{1,0:T(8,128)(2,1)} collective-permute-done((bf16[1024,256]{1,0:T(8,128)(2,1)}, bf16[1024,256]{1,0:T(8,128)(2,1)}, u32[]{:S(2)}, u32[]{:S(2)}) %collective-permute-start.2) | collective-permute-done | bytes 524320 | tf_op jit(solution)/shard_map/ppermute | solution.py:12
  46.2 42.8 %all-to-all-done = bf16[16,48,2048]{2,1,0:T(8,128)(2,1)S(1)} async-done(((bf16[16,48,2048]{2,1,0:T(8,128)(2,1)}), bf16[16,48,2048]{2,1,0:T(8,128)(2,1)S(1)}, u32[]{:S(2)}, u32[]{:S(2)}) %all-to-all-start) | async-done | bytes 3145760 | tf_op jit(solution)/shard_map/all_to_all | solution.py:58
  89.0 0.0 copy-start
  89.0 0.0 copy-start.2
  89.0 4.5 %fusion.22 = f32[768,1024]{0,1:T(8,128)S(1)} fusion(bf16[768,2048]{1,0:T(8,128)(2,1)S(1)} %bitcast.26, bf16[1024,256]{1,0:T(8,128)(2,1)} %collective-permute-done.2, bf16[1024,256]{1,0:T(8,128)(2,1)} %bitcast.40, bf16[1024,256]{1,0:T(8,128)(2,1)} %copy-done.5, bf16[1024,256]{1,0:T(8,128)(2,1)} %bitcast.43), kind=kOutput, calls=%fused_computation.41 | convolution fusion | flops 1619001344 | bytes 6815744 | tf_op jit(solution)/shard_map/dot_general | solution.py:71
  93.6 0.0 copy-start.3
  93.6 0.0 copy-start.4
  93.6 0.0 copy-start.6
  93.6 0.0 collective-permute-done
  93.6 0.0 copy-done
  93.6 0.0 copy-done.2
  93.6 3.6 %multiply_convert_fusion.2 = (bf16[768,512]{0,1:T(8,128)(2,1)S(1)}, bf16[768,512]{0,1:T(8,128)(2,1)S(1)}, bf16[768,512]{0,1:T(8,128)(2,1)}) fusion(f32[768,1024]{0,1:T(8,128)S(1)} %fusion.22, bf16[256,1024]{1,0:T(8,128)(2,1)} %collective-permute-done, bf16[256,1024]{1,0:T(8,128)(2,1)S(1)} %bitcast.38, bf16[768,2048]{1,0:T(8,128)(2,1)S(1)} %bitcast.27), kind=kOutput, calls=%fused_computation.11 | convolution fusion | flops 813301760 | bytes 8126464 | tf_op jit(solution)/shard_map/dot_general | solution.py:77
  97.2 0.0 copy-start.8
  97.2 0.0 copy-start.10
  97.2 0.0 copy-done.3
  97.2 0.0 copy-done.4
  97.2 0.0 copy-done.6
  97.2 4.4 %convolution_convert_fusion = bf16[768,1024]{1,0:T(8,128)(2,1)} fusion(bf16[768,512]{0,1:T(8,128)(2,1)S(1)} %get-tuple-element.5, bf16[768,512]{0,1:T(8,128)(2,1)S(1)} %get-tuple-element.4, bf16[1024,256]{1,0:T(8,128)(2,1)} %collective-permute-done.2, bf16[1024,256]{1,0:T(8,128)(2,1)S(1)} %bitcast.41, bf16[1024,256]{1,0:T(8,128)(2,1)S(1)} %copy-done.6, ...), kind=kOutput, calls=%fused_computation.5 | convolution fusion | flops 1622933504 | bytes 5242880 | tf_op jit(solution)/shard_map/dot_general | solution.py:83
  101.7 0.0 copy-done.8
  101.7 0.0 copy-done.10
  101.7 0.0 copy-start.7
  101.7 5.6 %all-to-all-start.1 = ((bf16[16,48,1024]{2,1,0:T(8,128)(2,1)}), bf16[16,48,1024]{2,1,0:T(8,128)(2,1)S(1)}, u32[]{:S(2)}, u32[]{:S(2)}) async-start(bf16[16,48,1024]{2,1,0:T(8,128)(2,1)} %bitcast.10), calls=%async_computation.1 | async-start | bytes 3145728 | tf_op jit(solution)/shard_map/all_to_all | solution.py:85
  107.2 0.0 copy-start.1
  107.3 0.0 copy-done.7
  107.3 2.1 %convolution_convert_fusion.1 = bf16[256,1024]{1,0:T(8,128)(2,1)S(1)} fusion(bf16[768,2048]{1,0:T(8,128)(2,1)} %bitcast.28, bf16[768,512]{0,1:T(8,128)(2,1)S(1)} %copy-done.7), kind=kOutput, calls=%fused_computation.14 | convolution fusion | flops 402915328 | bytes 2490368 | tf_op jit(solution)/shard_map/dot_general | solution.py:90
  109.4 0.0 copy-start.9
  109.4 3.0 %collective-permute-start.5 = (bf16[256,1024]{1,0:T(8,128)(2,1)S(1)}, bf16[256,1024]{1,0:T(8,128)(2,1)S(1)}, u32[]{:S(2)}, u32[]{:S(2)}) collective-permute-start(bf16[256,1024]{1,0:T(8,128)(2,1)S(1)} %convolution_convert_fusion.1), channel_id=1, source_target_pairs={{0,256},{16,272},{32,288},{48,304},{64,320},{80,336},{96,352},{112... | collective-permute-start | bytes 1572872 | tf_op jit(solution)/shard_map/ppermute | solution.py:12
  112.4 0.0 copy-done.1
  112.4 1.6 %convolution_convert_fusion.2 = bf16[1024,256]{1,0:T(8,128)(2,1)S(1)} fusion(bf16[768,2048]{1,0:T(8,128)(2,1)S(1)} %bitcast.29, bf16[768,512]{0,1:T(8,128)(2,1)} %copy-done.10), kind=kOutput, calls=%fused_computation.15 | convolution fusion | flops 402915328 | bytes 2490368 | tf_op jit(solution)/shard_map/dot_general | solution.py:89
  114.1 3.9 %collective-permute-start.4 = (bf16[1024,256]{1,0:T(8,128)(2,1)S(1)}, bf16[1024,256]{1,0:T(8,128)(2,1)S(1)}, u32[]{:S(2)}, u32[]{:S(2)}) collective-permute-start(bf16[1024,256]{1,0:T(8,128)(2,1)S(1)} %convolution_convert_fusion.2), channel_id=1, source_target_pairs={{0,256},{16,272},{32,288},{48,304},{64,320},{80,336},{96,352},{112... | collective-permute-start | bytes 1572872 | tf_op jit(solution)/shard_map/ppermute | solution.py:12
  118.0 0.0 copy-done.9
  118.0 0.6 convolution_convert_fusion.3
  118.7 0.0 copy-start.11
  118.7 3.0 %collective-permute-start.3 = (bf16[1024,256]{1,0:T(8,128)(2,1)S(1)}, bf16[1024,256]{1,0:T(8,128)(2,1)S(1)}, u32[]{:S(2)}, u32[]{:S(2)}) collective-permute-start(bf16[1024,256]{1,0:T(8,128)(2,1)S(1)} %convolution_convert_fusion.3), channel_id=1, source_target_pairs={{0,256},{16,272},{32,288},{48,304},{64,320},{80,336},{96,352},{112... | collective-permute-start | bytes 1572872 | tf_op jit(solution)/shard_map/ppermute | solution.py:12
  121.7 4.7 %collective-permute-done.5 = bf16[256,1024]{1,0:T(8,128)(2,1)S(1)} collective-permute-done((bf16[256,1024]{1,0:T(8,128)(2,1)S(1)}, bf16[256,1024]{1,0:T(8,128)(2,1)S(1)}, u32[]{:S(2)}, u32[]{:S(2)}) %collective-permute-start.5) | collective-permute-done | bytes 524320 | tf_op jit(solution)/shard_map/ppermute | solution.py:12
  126.4 1.4 fusion.38
  127.7 9.8 %collective-permute-done.4 = bf16[1024,256]{1,0:T(8,128)(2,1)S(1)} collective-permute-done((bf16[1024,256]{1,0:T(8,128)(2,1)S(1)}, bf16[1024,256]{1,0:T(8,128)(2,1)S(1)}, u32[]{:S(2)}, u32[]{:S(2)}) %collective-permute-start.4) | collective-permute-done | bytes 524320 | tf_op jit(solution)/shard_map/ppermute | solution.py:12
  137.6 0.0 copy-done.11
  137.6 1.4 fusion.31
  139.0 9.8 %collective-permute-done.3 = bf16[1024,256]{1,0:T(8,128)(2,1)S(1)} collective-permute-done((bf16[1024,256]{1,0:T(8,128)(2,1)S(1)}, bf16[1024,256]{1,0:T(8,128)(2,1)S(1)}, u32[]{:S(2)}, u32[]{:S(2)}) %collective-permute-start.3) | collective-permute-done | bytes 524320 | tf_op jit(solution)/shard_map/ppermute | solution.py:12
  148.8 1.4 fusion.28
  150.3 0.0 all-to-all-done.1
  150.3 1.2 fusion.5
  (3 shorter events, 0.0 us)
Async XLA Ops:
  7.7 81.4 %all-to-all-start = ((bf16[16,48,2048]{2,1,0:T(8,128)(2,1)}), bf16[16,48,2048]{2,1,0:T(8,128)(2,1)S(1)}, u32[]{:S(2)}, u32[]{:S(2)}) async-start(bf16[16,48,2048]{2,1,0:T(8,128)(2,1)} %bitcast.5), calls=%async_computation | async-start | bytes 6291456 | tf_op jit(solution)/shard_map/all_to_all | solution.py:58
  18.0 16.8 %collective-permute-start.1 = (bf16[1024,256]{1,0:T(8,128)(2,1)}, bf16[1024,256]{1,0:T(8,128)(2,1)S(1)}, u32[]{:S(2)}, u32[]{:S(2)}) collective-permute-start(bf16[1024,256]{1,0:T(8,128)(2,1)} %bitcast.42), channel_id=1, source_target_pairs={{0,256},{16,272},{32,288},{48,304},{64,320},{80,336},{96,352},{112... | collective-permute-start | bytes 1572872 | tf_op jit(solution)/shard_map/ppermute | solution.py:12
  20.9 25.3 %collective-permute-start.2 = (bf16[1024,256]{1,0:T(8,128)(2,1)}, bf16[1024,256]{1,0:T(8,128)(2,1)}, u32[]{:S(2)}, u32[]{:S(2)}) collective-permute-start(bf16[1024,256]{1,0:T(8,128)(2,1)} %bitcast.39), channel_id=1, source_target_pairs={{0,256},{16,272},{32,288},{48,304},{64,320},{80,336},{96,352},{112... | collective-permute-start | bytes 1572872 | tf_op jit(solution)/shard_map/ppermute | solution.py:12
  24.8 68.8 %collective-permute-start = (bf16[256,1024]{1,0:T(8,128)(2,1)}, bf16[256,1024]{1,0:T(8,128)(2,1)}, u32[]{:S(2)}, u32[]{:S(2)}) collective-permute-start(bf16[256,1024]{1,0:T(8,128)(2,1)} %bitcast.37), channel_id=1, source_target_pairs={{0,256},{16,272},{32,288},{48,304},{64,320},{80,336},{96,352},{112... | collective-permute-start | bytes 1572872 | tf_op jit(solution)/shard_map/ppermute | solution.py:12
  34.9 0.8 copy-start.5
  89.0 4.6 %copy-start = (bf16[16,48,2048]{2,1,0:T(8,128)(2,1)}, bf16[16,48,2048]{2,1,0:T(8,128)(2,1)S(1)}, u32[]{:S(2)}) copy-start(bf16[16,48,2048]{2,1,0:T(8,128)(2,1)S(1)} %all-to-all-done) | copy-start | bytes 9437188
  89.0 4.6 %copy-start.2 = (bf16[1,1,256,1024]{3,2,1,0:T(8,128)(2,1)S(1)}, bf16[1,1,256,1024]{3,2,1,0:T(8,128)(2,1)}, u32[]{:S(2)}) copy-start(bf16[1,1,256,1024]{3,2,1,0:T(8,128)(2,1)} %param.13) | copy-start | bytes 1572868
  93.6 3.6 %copy-start.3 = (bf16[1,1,1024,256]{3,2,1,0:T(8,128)(2,1)S(1)}, bf16[1,1,1024,256]{3,2,1,0:T(8,128)(2,1)}, u32[]{:S(2)}) copy-start(bf16[1,1,1024,256]{3,2,1,0:T(8,128)(2,1)} %param.12) | copy-start | bytes 1572868
  93.6 3.6 %copy-start.4 = (bf16[1,1,1024,256]{3,2,1,0:T(8,128)(2,1)S(1)}, bf16[1,1,1024,256]{3,2,1,0:T(8,128)(2,1)}, u32[]{:S(2)}) copy-start(bf16[1,1,1024,256]{3,2,1,0:T(8,128)(2,1)} %param.11) | copy-start | bytes 1572868
  93.6 3.6 %copy-start.6 = (bf16[1024,256]{1,0:T(8,128)(2,1)S(1)}, bf16[1024,256]{1,0:T(8,128)(2,1)}, u32[]{:S(2)}) copy-start(bf16[1024,256]{1,0:T(8,128)(2,1)} %copy-done.5) | copy-start | bytes 1572868
  97.2 4.5 %copy-start.8 = (bf16[768,512]{0,1:T(8,128)(2,1)}, bf16[768,512]{0,1:T(8,128)(2,1)S(1)}, u32[]{:S(2)}) copy-start(bf16[768,512]{0,1:T(8,128)(2,1)S(1)} %get-tuple-element.4) | copy-start | bytes 2359300
  97.2 4.5 %copy-start.10 = (bf16[768,512]{0,1:T(8,128)(2,1)}, bf16[768,512]{0,1:T(8,128)(2,1)S(1)}, u32[]{:S(2)}) copy-start(bf16[768,512]{0,1:T(8,128)(2,1)S(1)} %get-tuple-element.5) | copy-start | bytes 2359300
  101.7 5.6 %copy-start.7 = (bf16[768,512]{0,1:T(8,128)(2,1)S(1)}, bf16[768,512]{0,1:T(8,128)(2,1)}, u32[]{:S(2)}) copy-start(bf16[768,512]{0,1:T(8,128)(2,1)} %get-tuple-element.6) | copy-start | bytes 2359300
  101.7 48.6 %all-to-all-start.1 = ((bf16[16,48,1024]{2,1,0:T(8,128)(2,1)}), bf16[16,48,1024]{2,1,0:T(8,128)(2,1)S(1)}, u32[]{:S(2)}, u32[]{:S(2)}) async-start(bf16[16,48,1024]{2,1,0:T(8,128)(2,1)} %bitcast.10), calls=%async_computation.1 | async-start | bytes 3145728 | tf_op jit(solution)/shard_map/all_to_all | solution.py:85
  107.2 5.2 %copy-start.1 = (bf16[16,48,2048]{2,1,0:T(8,128)(2,1)S(1)}, bf16[16,48,2048]{2,1,0:T(8,128)(2,1)}, u32[]{:S(2)}) copy-start(bf16[16,48,2048]{2,1,0:T(8,128)(2,1)} %copy-done) | copy-start | bytes 9437188
  109.4 8.6 %copy-start.9 = (bf16[768,512]{0,1:T(8,128)(2,1)S(1)}, bf16[768,512]{0,1:T(8,128)(2,1)}, u32[]{:S(2)}) copy-start(bf16[768,512]{0,1:T(8,128)(2,1)} %copy-done.8) | copy-start | bytes 2359300
  109.4 16.9 %collective-permute-start.5 = (bf16[256,1024]{1,0:T(8,128)(2,1)S(1)}, bf16[256,1024]{1,0:T(8,128)(2,1)S(1)}, u32[]{:S(2)}, u32[]{:S(2)}) collective-permute-start(bf16[256,1024]{1,0:T(8,128)(2,1)S(1)} %convolution_convert_fusion.1), channel_id=1, source_target_pairs={{0,256},{16,272},{32,288},{48,304},{64,320},{80,336},{96,352},{112... | collective-permute-start | bytes 1572872 | tf_op jit(solution)/shard_map/ppermute | solution.py:12
  114.1 23.5 %collective-permute-start.4 = (bf16[1024,256]{1,0:T(8,128)(2,1)S(1)}, bf16[1024,256]{1,0:T(8,128)(2,1)S(1)}, u32[]{:S(2)}, u32[]{:S(2)}) collective-permute-start(bf16[1024,256]{1,0:T(8,128)(2,1)S(1)} %convolution_convert_fusion.2), channel_id=1, source_target_pairs={{0,256},{16,272},{32,288},{48,304},{64,320},{80,336},{96,352},{112... | collective-permute-start | bytes 1572872 | tf_op jit(solution)/shard_map/ppermute | solution.py:12
  118.7 18.9 %copy-start.11 = (bf16[768,512]{0,1:T(8,128)(2,1)S(1)}, bf16[768,512]{0,1:T(8,128)(2,1)}, u32[]{:S(2)}) copy-start(bf16[768,512]{0,1:T(8,128)(2,1)} %copy-done.10) | copy-start | bytes 2359300
  118.7 30.1 %collective-permute-start.3 = (bf16[1024,256]{1,0:T(8,128)(2,1)S(1)}, bf16[1024,256]{1,0:T(8,128)(2,1)S(1)}, u32[]{:S(2)}, u32[]{:S(2)}) collective-permute-start(bf16[1024,256]{1,0:T(8,128)(2,1)S(1)} %convolution_convert_fusion.3), channel_id=1, source_target_pairs={{0,256},{16,272},{32,288},{48,304},{64,320},{80,336},{96,352},{112... | collective-permute-start | bytes 1572872 | tf_op jit(solution)/shard_map/ppermute | solution.py:12
